TPU v7x, 256 devices: a whole 4x4x8 slice. The times are simulated.
256 devices in a mesh: uly: 8 (over x_hi, y), blk: 32 (over x_lo, z, core).
Axes of the slice: x: 4 (x_hi: 2, x_lo: 2; x = x_hi * 2 + x_lo), y: 4, z: 8, core: 2. Of those that a mesh axis runs over, the one named last changes fastest.
Arguments:
- queries: bfloat16 [16384, 2048], P(('uly', 'blk')), may hold values from -6 to 6
- key_vector_rows: bfloat16 [16384, 256], P(('uly', 'blk')), may hold values from -6 to 6
- value_vector_rows: bfloat16 [16384, 256], P(('uly', 'blk')), may hold values from -6 to 6
- out_grad: bfloat16 [16384, 2048], P(('uly', 'blk')), may hold values from -6 to 6
- block_list: int32 [16, 128, 8], P('uly'), may hold values from 0 to 127, as said below
Outputs:
- attended: bfloat16 [16384, 2048], P(('uly', 'blk'))
- query_grad: bfloat16 [16384, 2048], P(('uly', 'blk'))
- gradient_keys: bfloat16 [16384, 256], P(('uly', 'blk'))
- gradient_values: bfloat16 [16384, 256], P(('uly', 'blk'))
Inputs may be any that keep to these rules, and one draw needn't show every extreme that they name: block_list[h, i] names key blocks for query block i of head h: its first entry is always i itself, every entry is at most i, and a block may be named several times.
All inputs are finite; a program needn't handle non-finite values.
Results may differ from a plain program's by a relative error of at most 0.039.
Values may be sent and summed in bfloat16 or wider, within the bound.
No kernel may reach another device: no remote copies, remote signals or barrier semaphores. Data moves between devices by JAX's collectives and lax.ppermute only.
A program may use at most 128 MiB of HBM per device.

v0:
```python
import math

import jax
import jax.numpy as jnp
from jax import lax
from jax.sharding import PartitionSpec as P

KEY_VALUE_HEADS = 2
HEAD_SIZE = 128
BLOCK = 128


def body(queries, key_vector_rows, value_vector_rows, out_grad, block_list):
    ulysses_width = lax.axis_size("uly")
    cycle_size = lax.axis_size("blk")
    segment_length = queries.shape[0]
    heads_dev = block_list.shape[0]
    list_len = block_list.shape[2]
    head_width = heads_dev * HEAD_SIZE
    copy_count = ulysses_width // KEY_VALUE_HEADS
    cycle_index = lax.axis_index("blk")
    score_scale = 1.0 / math.sqrt(HEAD_SIZE)
    sub_length = min(segment_length, BLOCK)
    sub_count = segment_length // sub_length
    unit_len = min(segment_length, BLOCK)
    units_per_block = BLOCK // unit_len
    units_per_segment = segment_length // unit_len
    total_tokens = segment_length * ulysses_width * cycle_size
    units_total = total_tokens // unit_len
    query_slots = queries.reshape(segment_length, ulysses_width, head_width)
    grad_slots = out_grad.reshape(segment_length, ulysses_width, head_width)
    kv_local = jnp.concatenate(
        [
            key_vector_rows.reshape(segment_length, KEY_VALUE_HEADS, HEAD_SIZE),
            value_vector_rows.reshape(segment_length, KEY_VALUE_HEADS, HEAD_SIZE),
        ],
        axis=2,
    )
    kv_slots = jnp.repeat(kv_local, copy_count, axis=1)
    query_all, kv_mine, grad_all = (
        lax.all_to_all(query_slots, "uly", split_axis=1, concat_axis=0, tiled=True),
        lax.all_to_all(kv_slots, "uly", split_axis=1, concat_axis=0, tiled=True),
        lax.all_to_all(grad_slots, "uly", split_axis=1, concat_axis=0, tiled=True),
    )
    keys_all = lax.all_gather(kv_mine[:, 0, :], "blk", axis=0, tiled=True)
    item_count = heads_dev * ulysses_width * sub_count
    query_items = (
        query_all.reshape(ulysses_width, sub_count, sub_length, heads_dev, HEAD_SIZE)
        .transpose(3, 0, 1, 2, 4)
        .reshape(item_count, sub_length, HEAD_SIZE)
    )
    grad_items = (
        grad_all.reshape(ulysses_width, sub_count, sub_length, heads_dev, HEAD_SIZE)
        .transpose(3, 0, 1, 2, 4)
        .reshape(item_count, sub_length, HEAD_SIZE)
    )
    item_ids = jnp.arange(item_count, dtype=jnp.int32)
    head_ids = item_ids // (ulysses_width * sub_count)
    slot_ids = item_ids // sub_count % ulysses_width
    sub_ids = item_ids % sub_count
    segments = slot_ids * cycle_size + cycle_index
    first_pos = segments * segment_length + sub_ids * sub_length
    query_block = first_pos // BLOCK
    entries = block_list[head_ids, query_block]
    earlier = jnp.arange(list_len)[:, None] > jnp.arange(list_len)[None, :]
    repeated = jnp.any((entries[:, :, None] == entries[:, None, :]) & earlier[None, :, :], axis=2)
    offsets = jnp.arange(BLOCK, dtype=jnp.int32)
    key_pos = (entries[:, :, None] * BLOCK + offsets[None, None, :]).reshape(
        item_count, list_len * BLOCK
    )
    live_keys = jnp.repeat(jnp.logical_not(repeated), BLOCK, axis=1)
    query_pos = first_pos[:, None] + jnp.arange(sub_length, dtype=jnp.int32)[None, :]
    allowed = (key_pos[:, None, :] <= query_pos[:, :, None]) & live_keys[:, None, :]
    unit_count = list_len * units_per_block
    natural_units = (
        entries[:, :, None] * units_per_block
        + jnp.arange(units_per_block, dtype=jnp.int32)[None, None, :]
    ).reshape(item_count, unit_count)
    unit_seg = natural_units // units_per_segment
    canon_units = (
        unit_seg % cycle_size * ulysses_width + unit_seg // cycle_size
    ) * units_per_segment + natural_units % units_per_segment
    keys_units = keys_all.reshape(units_total, unit_len * 2 * HEAD_SIZE)
    unit_iota = jnp.arange(units_total, dtype=jnp.int32)
    per_step = min(item_count, max(1, 512 // sub_length))
    step_count = item_count // per_step
    key_len = list_len * BLOCK

    def group_step(grad_acc, group_data):
        query_group, grad_group, fetch_group, canon_group, mask_group = group_data
        fetch_table = (fetch_group.reshape(-1)[:, None] == unit_iota[None, :]).astype(jnp.bfloat16)
        gathered = (
            jnp.dot(fetch_table, keys_units, preferred_element_type=jnp.float32)
            .astype(jnp.bfloat16)
            .reshape(per_step, key_len, 2 * HEAD_SIZE)
        )
        key_group = gathered[:, :, :HEAD_SIZE]
        value_group = gathered[:, :, HEAD_SIZE:]
        scores = (
            jnp.einsum("nqd,nkd->nqk", query_group, key_group, preferred_element_type=jnp.float32)
            * score_scale
        )
        masked = jnp.where(mask_group, scores, -1e30)
        row_max = jnp.max(masked, axis=2, keepdims=True)
        row_sum = jnp.sum(
            jnp.where(mask_group, jnp.exp(masked - row_max), 0.0), axis=2, keepdims=True
        )
        log_sum = row_max + jnp.log(row_sum)
        weights = jnp.where(mask_group, jnp.exp(masked - log_sum), 0.0)
        weights_low = weights.astype(jnp.bfloat16)
        out_group = jnp.einsum(
            "nqk,nkd->nqd", weights_low, value_group, preferred_element_type=jnp.float32
        ).astype(jnp.bfloat16)
        row_dot = jnp.sum(
            grad_group.astype(jnp.float32) * out_group.astype(jnp.float32), axis=2, keepdims=True
        )
        grad_weights = jnp.einsum(
            "nqd,nkd->nqk", grad_group, value_group, preferred_element_type=jnp.float32
        )
        score_grad = (weights * (grad_weights - row_dot) * score_scale).astype(jnp.bfloat16)
        query_group_grad = jnp.einsum(
            "nqk,nkd->nqd", score_grad, key_group, preferred_element_type=jnp.float32
        ).astype(jnp.bfloat16)
        key_portion = jnp.einsum(
            "nqk,nqd->nkd", score_grad, query_group, preferred_element_type=jnp.float32
        )
        value_portion = jnp.einsum(
            "nqk,nqd->nkd", weights_low, grad_group, preferred_element_type=jnp.float32
        )
        both_parts = jnp.concatenate([key_portion, value_portion], axis=2).reshape(
            per_step * unit_count, unit_len * 2 * HEAD_SIZE
        )
        place_table = (canon_group.reshape(-1)[:, None] == unit_iota[None, :]).astype(jnp.float32)
        grad_acc = grad_acc + jnp.dot(
            place_table.T,
            both_parts,
            preferred_element_type=jnp.float32,
            precision=lax.Precision.HIGHEST,
        )
        return (grad_acc, (out_group, query_group_grad))

    empty_grad = jnp.zeros((units_total, unit_len * 2 * HEAD_SIZE), jnp.float32)
    scan_inputs = (
        query_items.reshape(step_count, per_step, sub_length, HEAD_SIZE),
        grad_items.reshape(step_count, per_step, sub_length, HEAD_SIZE),
        canon_units.reshape(step_count, per_step, unit_count),
        canon_units.reshape(step_count, per_step, unit_count),
        allowed.reshape(step_count, per_step, sub_length, key_len),
    )
    unit_grads, item_outputs = lax.scan(group_step, empty_grad, scan_inputs)
    kv_grad_all = unit_grads.reshape(total_tokens, 2 * HEAD_SIZE)
    out_items = (
        item_outputs[0]
        .reshape(heads_dev, ulysses_width, sub_count, sub_length, HEAD_SIZE)
        .transpose(1, 2, 3, 0, 4)
        .reshape(ulysses_width * segment_length, 1, head_width)
    )
    qgrad_items = (
        item_outputs[1]
        .reshape(heads_dev, ulysses_width, sub_count, sub_length, HEAD_SIZE)
        .transpose(1, 2, 3, 0, 4)
        .reshape(ulysses_width * segment_length, 1, head_width)
    )
    attended_back, qgrad_back = (
        lax.all_to_all(out_items, "uly", split_axis=0, concat_axis=1, tiled=True),
        lax.all_to_all(qgrad_items, "uly", split_axis=0, concat_axis=1, tiled=True),
    )
    attended = attended_back.reshape(segment_length, ulysses_width * head_width)
    query_grad = qgrad_back.reshape(segment_length, ulysses_width * head_width)
    owned = lax.psum_scatter(kv_grad_all, "blk", scatter_dimension=0, tiled=True)
    result_tuple = lax.all_to_all(
        owned.reshape(ulysses_width * segment_length, 1, 2 * HEAD_SIZE),
        "uly",
        split_axis=0,
        concat_axis=1,
        tiled=True,
    )
    summed_total = result_tuple.reshape(
        segment_length, KEY_VALUE_HEADS, copy_count, 2 * HEAD_SIZE
    ).sum(axis=2)
    gradient_keys = (
        summed_total[:, :, :HEAD_SIZE]
        .reshape(segment_length, KEY_VALUE_HEADS * HEAD_SIZE)
        .astype(jnp.bfloat16)
    )
    gradient_values = (
        summed_total[:, :, HEAD_SIZE:]
        .reshape(segment_length, KEY_VALUE_HEADS * HEAD_SIZE)
        .astype(jnp.bfloat16)
    )
    return (attended, query_grad, gradient_keys, gradient_values)


def solution(mesh):
    in_specs = (
        P(("uly", "blk"), None),
        P(("uly", "blk"), None),
        P(("uly", "blk"), None),
        P(("uly", "blk"), None),
        P("uly", None, None),
    )
    out_specs = (
        P(("uly", "blk"), None),
        P(("uly", "blk"), None),
        P(("uly", "blk"), None),
        P(("uly", "blk"), None),
    )
    return jax.shard_map(body, mesh=mesh, in_specs=in_specs, out_specs=out_specs, check_vma=False)
```

profile of v0, /device:TPU:0, one launch (start us, length us, event | category | flops | bytes accessed | tf_op | source)
XLA Modules:
  0.0 419.6 jit_solution(4855047830497179188)
XLA Ops:
  7.2 0.8 reshape.298
  8.0 0.8 reshape.299
  8.9 13.9 %all_to_all.90 = bf16[64,8,256]{2,0,1:T(8,128)(2,1)} all-to-all(bf16[64,8,256]{2,0,1:T(8,128)(2,1)S(1)} %bitcast.151), channel_id=1, replica_groups=mesh['uly'=8,'blk'=32] {'uly'}, dimensions={1} | all-to-all | bytes 524288 | tf_op jit(solution)/shard_map/all_to_all | solution.py:42
  22.8 1.7 copy.123
  24.4 3.4 all-to-all-start
  27.9 0.8 copy.88
  30.4 1.7 copy.122
  32.1 4.5 %all-to-all-done = bf16[64,8,256]{2,0,1:T(8,128)(2,1)S(1)} async-done(((bf16[64,8,256]{2,0,1:T(8,128)(2,1)}), bf16[64,8,256]{2,0,1:T(8,128)(2,1)S(1)}, u32[]{:S(2)}, u32[]{:S(2)}) %all-to-all-start) | async-done | bytes 262176 | tf_op jit(solution)/shard_map/all_to_all | solution.py:41
  36.5 3.4 all-to-all-start.2
  40.0 1.0 compare_and_fusion
  41.1 9.5 %all-to-all-done.2 = bf16[64,8,256]{2,0,1:T(8,128)(2,1)S(1)} async-done(((bf16[64,8,256]{2,0,1:T(8,128)(2,1)}), bf16[64,8,256]{2,0,1:T(8,128)(2,1)S(1)}, u32[]{:S(2)}, u32[]{:S(2)}) %all-to-all-start.2) | async-done | bytes 262176 | tf_op jit(solution)/shard_map/all_to_all | solution.py:43
  50.7 42.7 %all-gather.2.cloned.1.call-done = bf16[16384,256]{1,0:T(8,128)(2,1)} async-done(((bf16[512,256]{1,0:T(8,128)(2,1)}), bf16[16384,256]{1,0:T(8,128)(2,1)}) %all-gather.2.cloned.1.call-update) | async-done | bytes 8388624 | tf_op jit(solution)/shard_map/all_gather | solution.py:45
  93.3 13.5 %reshape.301 = bf16[256,16384]{1,0:T(8,128)(2,1)} reshape(bf16[16384,256]{1,0:T(8,128)(2,1)} %all-gather.2.cloned.1.call-done) | data formatting | bytes 16777216 | tf_op jit(solution)/shard_map/reshape | solution.py:83
  106.8 124.2 %while.16 = (s32[]{:T(128)}, f32[256,16384]{1,0:T(8,128)}, bf16[2,8,64,128]{3,2,1,0:T(8,128)(2,1)S(1)}, bf16[2,8,64,128]{3,2,1,0:T(8,128)(2,1)S(1)}, s32[2,8,16]...) while((s32[]{:T(128)}, f32[256,16384]{1,0:T(8,128)}, ...), condition=%wide.region_5.6_spmd.clone, body=%wide.region_1.5_spmd.clone.sunk | while | flops 8343976960 | bytes 164273328 | solution.py:150
  106.9 6.7 %convolution_convert_fusion.2 = bf16[128,16384]{1,0:T(8,128)(2,1)} fusion(bf16[256,16384]{1,0:T(8,128)(2,1)} %get-tuple-element.291, s32[128]{0:T(128)S(1)} %eq.82), kind=kOutput, calls=%fused_computation.3.clone.1 | convolution fusion | flops 1075871744 | bytes 12583424 | tf_op jit(solution)/shard_map/while/body/eval_jaxpr/dot_general | solution.py:93
  113.5 7.4 %reshape.329 = bf16[8,1024,256]{2,1,0:T(8,128)(2,1)} reshape(bf16[128,16384]{1,0:T(8,128)(2,1)} %convolution_convert_fusion.2) | data formatting | bytes 8388608 | tf_op jit(solution)/shard_map/while/body/eval_jaxpr/reshape | solution.py:95
  120.9 2.7 fusion.88
  124.3 0.7 multiply_reduce_fusion.2
  125.0 1.0 multiply_convert_fusion.2
  126.5 0.8 fusion.89
  127.4 0.8 fusion.90
  128.1 4.1 pad_maximum_fusion.3
  132.2 9.1 %copy.125 = f32[8,1024,256]{2,1,0:T(8,128)} copy(f32[8,1024,256]{1,2,0:T(8,128)} %pad_maximum_fusion.3) | data formatting | bytes 16777216 | tf_op jit(solution)/shard_map/while/body/eval_jaxpr/concatenate | solution.py:130
  141.3 9.4 %reshape.330 = f32[128,16384]{1,0:T(8,128)} reshape(f32[8,1024,256]{2,1,0:T(8,128)} %copy.125) | data formatting | bytes 16777216 | tf_op jit(solution)/shard_map/while/body/eval_jaxpr/reshape | solution.py:130
  150.7 17.0 %convolution_add_fusion.2 = f32[256,16384]{1,0:T(8,128)} fusion(f32[128,16384]{1,0:T(8,128)} %reshape.330, f32[256,16384]{1,0:T(8,128)} %get-tuple-element.274, pred[]{:T(512)S(6)} %compare.31, s32[128]{0:T(128)S(1)} %eq.82), kind=kOutput, calls=%fused_computation.2.clone.1 | convolution fusion | flops 6450872320 | bytes 41943552 | tf_op jit(solution)/shard_map/while/body/eval_jaxpr/dot_general | solution.py:134
  167.8 6.7 %convolution_convert_fusion.2 = bf16[128,16384]{1,0:T(8,128)(2,1)} fusion(bf16[256,16384]{1,0:T(8,128)(2,1)} %get-tuple-element.291, s32[128]{0:T(128)S(1)} %eq.82), kind=kOutput, calls=%fused_computation.3.clone.1 | convolution fusion | flops 1075871744 | bytes 12583424 | tf_op jit(solution)/shard_map/while/body/eval_jaxpr/dot_general | solution.py:93
  174.4 7.4 %reshape.329 = bf16[8,1024,256]{2,1,0:T(8,128)(2,1)} reshape(bf16[128,16384]{1,0:T(8,128)(2,1)} %convolution_convert_fusion.2) | data formatting | bytes 8388608 | tf_op jit(solution)/shard_map/while/body/eval_jaxpr/reshape | solution.py:95
  181.8 2.7 fusion.88
  185.1 0.7 multiply_reduce_fusion.2
  185.9 1.0 multiply_convert_fusion.2
  187.4 0.8 fusion.89
  188.3 0.8 fusion.90
  189.0 4.1 pad_maximum_fusion.3
  193.1 9.1 %copy.125 = f32[8,1024,256]{2,1,0:T(8,128)} copy(f32[8,1024,256]{1,2,0:T(8,128)} %pad_maximum_fusion.3) | data formatting | bytes 16777216 | tf_op jit(solution)/shard_map/while/body/eval_jaxpr/concatenate | solution.py:130
  202.2 9.4 %reshape.330 = f32[128,16384]{1,0:T(8,128)} reshape(f32[8,1024,256]{2,1,0:T(8,128)} %copy.125) | data formatting | bytes 16777216 | tf_op jit(solution)/shard_map/while/body/eval_jaxpr/reshape | solution.py:130
  211.6 19.4 %convolution_add_fusion.2 = f32[256,16384]{1,0:T(8,128)} fusion(f32[128,16384]{1,0:T(8,128)} %reshape.330, f32[256,16384]{1,0:T(8,128)} %get-tuple-element.274, pred[]{:T(512)S(6)} %compare.31, s32[128]{0:T(128)S(1)} %eq.82), kind=kOutput, calls=%fused_computation.2.clone.1 | convolution fusion | flops 6450872320 | bytes 41943552 | tf_op jit(solution)/shard_map/while/body/eval_jaxpr/dot_general | solution.py:134
  231.0 18.0 %reshape.310 = f32[16384,256]{1,0:T(8,128)} reshape(f32[256,16384]{1,0:T(8,128)} %get-tuple-element.86) | data formatting | bytes 33554432 | tf_op jit(solution)/shard_map/reshape | solution.py:151
  249.9 2.2 reduce.1
  252.2 0.8 reshape.325
  252.9 6.9 %all-to-all-start.4 = ((bf16[8,2,8192]{2,1,0:T(2,128)(2,1)}), bf16[8,2,8192]{2,1,0:T(2,128)(2,1)S(1)}, u32[]{:S(2)}, u32[]{:S(2)}) async-start(bf16[8,2,8192]{2,1,0:T(2,128)(2,1)} %reshape.325), calls=%async_computation.4 | async-start | bytes 524288 | tf_op jit(solution)/shard_map/all_to_all | solution.py:166
  260.2 2.2 reduce
  262.4 0.8 reshape.323
  263.2 11.2 %all-to-all-done.4 = bf16[8,2,8192]{2,1,0:T(2,128)(2,1)S(1)} async-done(((bf16[8,2,8192]{2,1,0:T(2,128)(2,1)}), bf16[8,2,8192]{2,1,0:T(2,128)(2,1)S(1)}, u32[]{:S(2)}, u32[]{:S(2)}) %all-to-all-start.4) | async-done | bytes 262176 | tf_op jit(solution)/shard_map/all_to_all | solution.py:166
  274.4 3.4 all-to-all-start.3
  277.8 115.9 %reduce-scatter.2.cloned.1.call-done = f32[512,256]{1,0:T(8,128)} async-done(((f32[16384,256]{1,0:T(8,128)}), f32[512,256]{1,0:T(8,128)}) %reduce-scatter.2.cloned.1.call-update) | async-done | bytes 524304 | tf_op jit(solution)/shard_map/reduce_scatter | solution.py:170
  393.7 2.2 reshape.311
  396.0 6.3 %all-to-all-start.5 = ((f32[512,1,256]{2,1,0:T(1,128)}), f32[512,1,256]{2,1,0:T(1,128)S(1)}, u32[]{:S(2)}, u32[]{:S(2)}) async-start(f32[512,1,256]{2,1,0:T(1,128)} %reshape.311), calls=%async_computation.6 | async-start | bytes 1048576 | tf_op jit(solution)/shard_map/all_to_all | solution.py:171
  404.3 7.7 %all-to-all-done.5 = f32[512,1,256]{2,1,0:T(1,128)S(1)} async-done(((f32[512,1,256]{2,1,0:T(1,128)}), f32[512,1,256]{2,1,0:T(1,128)S(1)}, u32[]{:S(2)}, u32[]{:S(2)}) %all-to-all-start.5) | async-done | bytes 524320 | tf_op jit(solution)/shard_map/all_to_all | solution.py:171
  (69 shorter events, 8.7 us)
Async XLA Ops:
  7.2 86.2 %all-gather.2.cloned.1.call-start = ((), (), s32[]{:S(2)}) async-start(), calls=%async_computation.7 | async-start | bytes 8650752 | tf_op jit(solution)/shard_map/all_gather | solution.py:45
  24.4 12.1 %all-to-all-start = ((bf16[64,8,256]{2,0,1:T(8,128)(2,1)}), bf16[64,8,256]{2,0,1:T(8,128)(2,1)S(1)}, u32[]{:S(2)}, u32[]{:S(2)}) async-start(bf16[64,8,256]{2,0,1:T(8,128)(2,1)} %bitcast.115), calls=%async_computation | async-start | bytes 524288 | tf_op jit(solution)/shard_map/all_to_all | solution.py:41
  36.5 14.0 %all-to-all-start.2 = ((bf16[64,8,256]{2,0,1:T(8,128)(2,1)}), bf16[64,8,256]{2,0,1:T(8,128)(2,1)S(1)}, u32[]{:S(2)}, u32[]{:S(2)}) async-start(bf16[64,8,256]{2,0,1:T(8,128)(2,1)} %bitcast.114), calls=%async_computation.2 | async-start | bytes 524288 | tf_op jit(solution)/shard_map/all_to_all | solution.py:43
  39.9 353.8 %reduce-scatter.2.cloned.1.call-start = ((), (), s32[]{:S(2)}) async-start(), calls=%async_computation.8 | async-start | bytes 17301504 | tf_op jit(solution)/shard_map/reduce_scatter | solution.py:170
  120.9 3.3 copy-start
  181.8 3.3 copy-start
  252.9 21.5 %all-to-all-start.4 = ((bf16[8,2,8192]{2,1,0:T(2,128)(2,1)}), bf16[8,2,8192]{2,1,0:T(2,128)(2,1)S(1)}, u32[]{:S(2)}, u32[]{:S(2)}) async-start(bf16[8,2,8192]{2,1,0:T(2,128)(2,1)} %reshape.325), calls=%async_computation.4 | async-start | bytes 524288 | tf_op jit(solution)/shard_map/all_to_all | solution.py:166
  274.4 121.5 %all-to-all-start.3 = ((bf16[8,2,8192]{2,1,0:T(2,128)(2,1)}), bf16[8,2,8192]{2,1,0:T(2,128)(2,1)S(1)}, u32[]{:S(2)}, u32[]{:S(2)}) async-start(bf16[8,2,8192]{2,1,0:T(2,128)(2,1)} %reshape.323), calls=%async_computation.3 | async-start | bytes 524288 | tf_op jit(solution)/shard_map/all_to_all | solution.py:165
  396.0 16.0 %all-to-all-start.5 = ((f32[512,1,256]{2,1,0:T(1,128)}), f32[512,1,256]{2,1,0:T(1,128)S(1)}, u32[]{:S(2)}, u32[]{:S(2)}) async-start(f32[512,1,256]{2,1,0:T(1,128)} %reshape.311), calls=%async_computation.6 | async-start | bytes 1048576 | tf_op jit(solution)/shard_map/all_to_all | solution.py:171
Sparse Core Ops, SparseCore 0:
  22.9 70.4 all-gather.1
  249.1 144.5 reduce-scatter.1
where the time goes:
time: 422 us; the launch traced here: 420 us
  waiting for transfers between devices  191 us (45%)
  local copies, waits for them, and re-layouts  98.5 us (23%)
  matrix products  62.6 us (15%)
  starting transfers between devices  23.5 us (6%)
  other arithmetic  15.2 us (4%)
  between operations  14.3 us (3%)
  blocking collectives  13.9 us (3%)
    reduce_scatter x1, waiting for transfers between devices, body(): lax.psum_scatter(kv_grad_all, 'blk', scatter_dimension=0, tiled=True)  116 us
    all_gather x1, waiting for transfers between devices, body(): keys_all = lax.all_gather(kv_mine[:, 0, :], 'blk', axis=0, tiled=True)  42.7 us
    dot_general x2, matrix products, group_step(): jnp.dot(place_table.T, both_parts, preferred_element_type=jnp.float32, pr...  36.4 us
    reshape x2, local copies, waits for them, and re-layouts, group_step(): jnp.concatenate([key_portion, value_portion], axis=2)  18.8 us
    concatenate x2, local copies, waits for them, and re-layouts, group_step(): jnp.concatenate([key_portion, value_portion], axis=2)  18.2 us
    reshape x1, local copies, waits for them, and re-layouts, body(): kv_grad_all = unit_grads.reshape(total_tokens, 2 * HEAD_SIZE)  18 us
    reshape x2, local copies, waits for them, and re-layouts, group_step(): gathered = jnp.dot(fetch_table, keys_units, preferred_element_type=jnp.fl...  14.8 us
    all_to_all x1, blocking collectives, body(): lax.all_to_all(kv_slots, 'uly', split_axis=1, concat_axis=0, tiled=True)  13.9 us
  transfers between devices with their start and end apart: 7, of which 6 were waited for; matrix products, arithmetic and copies ran while one was open for 4% of the time, Pallas kernels for 0%

commit v1 on v0

--- a/solution.py
+++ b/solution.py
@@ -3,7 +3,7 @@
 import jax
 import jax.numpy as jnp
 from jax import lax
-from jax.sharding import PartitionSpec as P
+from jax.sharding import Mesh, PartitionSpec as P
 
 KEY_VALUE_HEADS = 2
 HEAD_SIZE = 128
@@ -12,13 +12,14 @@
 
 def body(queries, key_vector_rows, value_vector_rows, out_grad, block_list):
     ulysses_width = lax.axis_size("uly")
-    cycle_size = lax.axis_size("blk")
+    cycle_size = lax.axis_size("chip") * lax.axis_size("core")
     segment_length = queries.shape[0]
     heads_dev = block_list.shape[0]
     list_len = block_list.shape[2]
     head_width = heads_dev * HEAD_SIZE
     copy_count = ulysses_width // KEY_VALUE_HEADS
-    cycle_index = lax.axis_index("blk")
+    core_count = lax.axis_size("core")
+    cycle_index = lax.axis_index("chip") * core_count + lax.axis_index("core")
     score_scale = 1.0 / math.sqrt(HEAD_SIZE)
     sub_length = min(segment_length, BLOCK)
     sub_count = segment_length // sub_length
@@ -42,7 +43,10 @@
         lax.all_to_all(kv_slots, "uly", split_axis=1, concat_axis=0, tiled=True),
         lax.all_to_all(grad_slots, "uly", split_axis=1, concat_axis=0, tiled=True),
     )
-    keys_all = lax.all_gather(kv_mine[:, 0, :], "blk", axis=0, tiled=True)
+    keys_chip = lax.all_gather(kv_mine[:, 0, :], "chip", axis=0, tiled=False)
+    keys_all = lax.all_gather(keys_chip, "core", axis=1, tiled=False).reshape(
+        cycle_size * segment_length * ulysses_width, 2 * HEAD_SIZE
+    )
     item_count = heads_dev * ulysses_width * sub_count
     query_items = (
         query_all.reshape(ulysses_width, sub_count, sub_length, heads_dev, HEAD_SIZE)
@@ -80,6 +84,11 @@
     canon_units = (
         unit_seg % cycle_size * ulysses_width + unit_seg // cycle_size
     ) * units_per_segment + natural_units % units_per_segment
+    owner_of = unit_seg % cycle_size
+    grad_units = (
+        (owner_of % core_count * (cycle_size // core_count) + owner_of // core_count) * ulysses_width
+        + unit_seg // cycle_size
+    ) * units_per_segment + natural_units % units_per_segment
     keys_units = keys_all.reshape(units_total, unit_len * 2 * HEAD_SIZE)
     unit_iota = jnp.arange(units_total, dtype=jnp.int32)
     per_step = min(item_count, max(1, 512 // sub_length))
@@ -144,11 +153,10 @@
         query_items.reshape(step_count, per_step, sub_length, HEAD_SIZE),
         grad_items.reshape(step_count, per_step, sub_length, HEAD_SIZE),
         canon_units.reshape(step_count, per_step, unit_count),
-        canon_units.reshape(step_count, per_step, unit_count),
+        grad_units.reshape(step_count, per_step, unit_count),
         allowed.reshape(step_count, per_step, sub_length, key_len),
     )
     unit_grads, item_outputs = lax.scan(group_step, empty_grad, scan_inputs)
-    kv_grad_all = unit_grads.reshape(total_tokens, 2 * HEAD_SIZE)
     out_items = (
         item_outputs[0]
         .reshape(heads_dev, ulysses_width, sub_count, sub_length, HEAD_SIZE)
@@ -167,7 +175,14 @@
     )
     attended = attended_back.reshape(segment_length, ulysses_width * head_width)
     query_grad = qgrad_back.reshape(segment_length, ulysses_width * head_width)
-    owned = lax.psum_scatter(kv_grad_all, "blk", scatter_dimension=0, tiled=True)
+    grad_split = unit_grads.reshape(
+        core_count, cycle_size // core_count, ulysses_width * segment_length, 2 * HEAD_SIZE
+    )
+    core_index = lax.axis_index("core")
+    kept = lax.dynamic_index_in_dim(grad_split, core_index, axis=0, keepdims=False)
+    sent = lax.dynamic_index_in_dim(grad_split, 1 - core_index, axis=0, keepdims=False)
+    received = lax.ppermute(sent, "core", [(0, 1), (1, 0)])
+    owned = lax.psum_scatter(kept + received, "chip", scatter_dimension=0, tiled=True)
     result_tuple = lax.all_to_all(
         owned.reshape(ulysses_width * segment_length, 1, 2 * HEAD_SIZE),
         "uly",
@@ -192,17 +207,12 @@
 
 
 def solution(mesh):
-    in_specs = (
-        P(("uly", "blk"), None),
-        P(("uly", "blk"), None),
-        P(("uly", "blk"), None),
-        P(("uly", "blk"), None),
-        P("uly", None, None),
-    )
-    out_specs = (
-        P(("uly", "blk"), None),
-        P(("uly", "blk"), None),
-        P(("uly", "blk"), None),
-        P(("uly", "blk"), None),
-    )
-    return jax.shard_map(body, mesh=mesh, in_specs=in_specs, out_specs=out_specs, check_vma=False)
+    devices = mesh.devices
+    cores = 2
+    fine_mesh = Mesh(
+        devices.reshape(devices.shape[0], devices.shape[1] // cores, cores), ("uly", "chip", "core")
+    )
+    rows = P(("uly", "chip", "core"), None)
+    in_specs = (rows, rows, rows, rows, P("uly", None, None))
+    out_specs = (rows, rows, rows, rows)
+    return jax.shard_map(body, mesh=fine_mesh, in_specs=in_specs, out_specs=out_specs, check_vma=False)

time: 422 us -> 449 us (1.064)
  waiting for transfers between devices: 191 us -> 206 us
  other arithmetic: 15.2 us -> 25.6 us
  local copies, waits for them, and re-layouts: 98.5 us -> 104 us
    reduce_scatter x1, waiting for transfers between devices: 116 us -> 0.01 us  [body(): lax.psum_scatter(kept + received, 'chip', scatter_dimension=0, tiled=True)]
    all_to_all x1, waiting for transfers between devices: 11.2 us -> 88.3 us  [body(): lax.all_to_all(qgrad_items, 'uly', split_axis=0, concat_axis=1, tiled=True)]
    all_gather x1 -> x2, waiting for transfers between devices: 42.7 us -> 75.2 us  [the longest x1 75.1 us: body(): keys_chip = lax.all_gather(kv_mine[:, 0, :], 'chip', axis=0, tiled=False)]
    reshape x2 -> x1, local copies, waits for them, and re-layouts: 31.5 us -> 18 us  [body(): unit_grads.reshape(core_count, cycle_size // core_count, ulysses_width *...]
    ppermute x0 -> x1, waiting for transfers between devices: none -> 13.5 us  [body(): received = lax.ppermute(sent, 'core', [(0, 1), (1, 0)])]
    another operation x0 -> x1, local copies, waits for them, and re-layouts: none -> 13.5 us  [body(): keys_units = keys_all.reshape(units_total, unit_len * 2 * HEAD_SIZE)]
    add x0 -> x2, other arithmetic: none -> 10.3 us  [the longest x1 10.2 us: body(): kept + received]
    squeeze x0 -> x1, local copies, waits for them, and re-layouts: none -> 7.34 us  [body(): lax.dynamic_index_in_dim(grad_split, 1 - core_index, axis=0, keepdims=False)]
  transfers between devices with their start and end apart: 7 -> 9, of which waited for: 6 -> 7; matrix products, arithmetic and copies ran while one was open for 4% -> 4% of each run, Pallas kernels for 0% -> 0%
where the time goes in v1:
time: 449 us; the launch traced here: 447 us
  waiting for transfers between devices  206 us (46%)
  local copies, waits for them, and re-layouts  104 us (23%)
  matrix products  62.6 us (14%)
  other arithmetic  25.6 us (6%)
  starting transfers between devices  21 us (5%)
  between operations  14.1 us (3%)
  blocking collectives  13.9 us (3%)
    all_to_all x1, waiting for transfers between devices, body(): lax.all_to_all(qgrad_items, 'uly', split_axis=0, concat_axis=1, tiled=True)  88.3 us
    all_gather x1, waiting for transfers between devices, body(): keys_chip = lax.all_gather(kv_mine[:, 0, :], 'chip', axis=0, tiled=False)  75.1 us
    dot_general x2, matrix products, group_step(): jnp.dot(place_table.T, both_parts, preferred_element_type=jnp.float32, pr...  36.4 us
    reshape x2, local copies, waits for them, and re-layouts, group_step(): jnp.concatenate([key_portion, value_portion], axis=2)  18.7 us
    concatenate x2, local copies, waits for them, and re-layouts, group_step(): jnp.concatenate([key_portion, value_portion], axis=2)  18.2 us
    reshape x1, local copies, waits for them, and re-layouts, body(): unit_grads.reshape(core_count, cycle_size // core_count, ulysses_width *...  18 us
    reshape x2, local copies, waits for them, and re-layouts, group_step(): gathered = jnp.dot(fetch_table, keys_units, preferred_element_type=jnp.fl...  14.8 us
    all_to_all x1, blocking collectives, body(): lax.all_to_all(kv_slots, 'uly', split_axis=1, concat_axis=0, tiled=True)  13.9 us
  transfers between devices with their start and end apart: 9, of which 7 were waited for; matrix products, arithmetic and copies ran while one was open for 4% of the time, Pallas kernels for 0%

profile of v1, /device:TPU:0, one launch (start us, length us, event | category | flops | bytes accessed | tf_op | source)
XLA Modules:
  0.0 446.5 jit_solution(4975136799833612247)
XLA Ops:
  7.2 0.8 reshape.299
  8.1 0.8 reshape.300
  9.0 13.9 %all_to_all.90 = bf16[64,8,256]{2,0,1:T(8,128)(2,1)} all-to-all(bf16[64,8,256]{2,0,1:T(8,128)(2,1)S(1)} %bitcast.156), channel_id=1, replica_groups=mesh['uly'=8,'chip'=16,'core'=2] {'uly'}, dimensions={1} | all-to-all | bytes 524288 | tf_op jit(solution)/shard_map/all_to_all | solution.py:43
  22.9 75.1 %all-gather.4.cloned.1.call-done = bf16[16,512,256]{2,1,0:T(8,128)(2,1)} async-done(((bf16[1,512,256]{2,1,0:T(8,128)(2,1)}), bf16[16,512,256]{2,1,0:T(8,128)(2,1)}) %all-gather.4.cloned.1.call-update) | async-done | bytes 4194320 | tf_op jit(solution)/shard_map/all_gather | solution.py:46
  98.8 6.3 %all-to-all-start = ((bf16[64,8,256]{2,0,1:T(8,128)(2,1)}), bf16[64,8,256]{2,0,1:T(8,128)(2,1)S(1)}, u32[]{:S(2)}, u32[]{:S(2)}) async-start(bf16[64,8,256]{2,0,1:T(8,128)(2,1)} %bitcast.120), calls=%async_computation | async-start | bytes 524288 | tf_op jit(solution)/shard_map/all_to_all | solution.py:42
  107.8 7.0 %all-to-all-done = bf16[64,8,256]{2,0,1:T(8,128)(2,1)S(1)} async-done(((bf16[64,8,256]{2,0,1:T(8,128)(2,1)}), bf16[64,8,256]{2,0,1:T(8,128)(2,1)S(1)}, u32[]{:S(2)}, u32[]{:S(2)}) %all-to-all-start) | async-done | bytes 262176 | tf_op jit(solution)/shard_map/all_to_all | solution.py:42
  114.8 3.4 all-to-all-start.2
  118.2 1.0 compare_and_fusion
  119.3 7.5 %all-to-all-done.2 = bf16[64,8,256]{2,0,1:T(8,128)(2,1)S(1)} async-done(((bf16[64,8,256]{2,0,1:T(8,128)(2,1)}), bf16[64,8,256]{2,0,1:T(8,128)(2,1)S(1)}, u32[]{:S(2)}, u32[]{:S(2)}) %all-to-all-start.2) | async-done | bytes 262176 | tf_op jit(solution)/shard_map/all_to_all | solution.py:44
  127.0 13.5 %reshape_reshape.10 = bf16[256,16384]{1,0:T(8,128)(2,1)} reshape(bf16[16,1024,256]{2,1,0:T(8,128)(2,1)} %all-gather.6.cloned.1.call-done) | data formatting | bytes 16777216 | tf_op jit(solution)/shard_map/reshape;reshape | solution.py:92
  140.5 124.3 %while.16 = (s32[]{:T(128)}, f32[256,16384]{1,0:T(8,128)}, bf16[2,8,64,128]{3,2,1,0:T(8,128)(2,1)S(1)}, bf16[2,8,64,128]{3,2,1,0:T(8,128)(2,1)S(1)}, s32[2,8,16]...) while((s32[]{:T(128)}, f32[256,16384]{1,0:T(8,128)}, ...), condition=%wide.region_5.6_spmd.clone.clone, body=%wide.region_1.5_spmd.clone.clone.sunk | while | flops 8343976960 | bytes 164275376 | solution.py:159
  140.7 6.6 %convolution_convert_fusion.2 = bf16[128,16384]{1,0:T(8,128)(2,1)} fusion(bf16[256,16384]{1,0:T(8,128)(2,1)} %get-tuple-element.338, s32[128]{0:T(128)S(1)} %eq.95), kind=kOutput, calls=%fused_computation.3.clone.1 | convolution fusion | flops 1075871744 | bytes 12583424 | tf_op jit(solution)/shard_map/while/body/eval_jaxpr/dot_general | solution.py:102
  147.3 7.4 %reshape.333 = bf16[8,1024,256]{2,1,0:T(8,128)(2,1)} reshape(bf16[128,16384]{1,0:T(8,128)(2,1)} %convolution_convert_fusion.2) | data formatting | bytes 8388608 | tf_op jit(solution)/shard_map/while/body/eval_jaxpr/reshape | solution.py:104
  154.7 2.7 fusion.88
  158.0 0.7 multiply_reduce_fusion.2
  158.8 1.0 multiply_convert_fusion.2
  160.3 0.8 fusion.89
  161.1 0.8 fusion.90
  161.9 4.1 pad_maximum_fusion.3
  166.0 9.1 %copy.156 = f32[8,1024,256]{2,1,0:T(8,128)} copy(f32[8,1024,256]{1,2,0:T(8,128)} %pad_maximum_fusion.3) | data formatting | bytes 16777216 | tf_op jit(solution)/shard_map/while/body/eval_jaxpr/concatenate | solution.py:139
  175.1 9.4 %reshape.334 = f32[128,16384]{1,0:T(8,128)} reshape(f32[8,1024,256]{2,1,0:T(8,128)} %copy.156) | data formatting | bytes 16777216 | tf_op jit(solution)/shard_map/while/body/eval_jaxpr/reshape | solution.py:139
  184.5 17.0 %convolution_add_fusion.2 = f32[256,16384]{1,0:T(8,128)} fusion(f32[128,16384]{1,0:T(8,128)} %reshape.334, f32[256,16384]{1,0:T(8,128)} %get-tuple-element.319, pred[]{:T(512)S(6)} %compare.40, s32[128]{0:T(128)S(1)} %eq.96), kind=kOutput, calls=%fused_computation.2.clone.1 | convolution fusion | flops 6450872320 | bytes 41943552 | tf_op jit(solution)/shard_map/while/body/eval_jaxpr/dot_general | solution.py:143
  201.6 6.7 %convolution_convert_fusion.2 = bf16[128,16384]{1,0:T(8,128)(2,1)} fusion(bf16[256,16384]{1,0:T(8,128)(2,1)} %get-tuple-element.338, s32[128]{0:T(128)S(1)} %eq.95), kind=kOutput, calls=%fused_computation.3.clone.1 | convolution fusion | flops 1075871744 | bytes 12583424 | tf_op jit(solution)/shard_map/while/body/eval_jaxpr/dot_general | solution.py:102
  208.3 7.4 %reshape.333 = bf16[8,1024,256]{2,1,0:T(8,128)(2,1)} reshape(bf16[128,16384]{1,0:T(8,128)(2,1)} %convolution_convert_fusion.2) | data formatting | bytes 8388608 | tf_op jit(solution)/shard_map/while/body/eval_jaxpr/reshape | solution.py:104
  215.7 2.7 fusion.88
  219.0 0.7 multiply_reduce_fusion.2
  219.7 1.0 multiply_convert_fusion.2
  221.3 0.8 fusion.89
  222.1 0.8 fusion.90
  222.8 4.1 pad_maximum_fusion.3
  226.9 9.1 %copy.156 = f32[8,1024,256]{2,1,0:T(8,128)} copy(f32[8,1024,256]{1,2,0:T(8,128)} %pad_maximum_fusion.3) | data formatting | bytes 16777216 | tf_op jit(solution)/shard_map/while/body/eval_jaxpr/concatenate | solution.py:139
  236.0 9.4 %reshape.334 = f32[128,16384]{1,0:T(8,128)} reshape(f32[8,1024,256]{2,1,0:T(8,128)} %copy.156) | data formatting | bytes 16777216 | tf_op jit(solution)/shard_map/while/body/eval_jaxpr/reshape | solution.py:139
  245.4 19.4 %convolution_add_fusion.2 = f32[256,16384]{1,0:T(8,128)} fusion(f32[128,16384]{1,0:T(8,128)} %reshape.334, f32[256,16384]{1,0:T(8,128)} %get-tuple-element.319, pred[]{:T(512)S(6)} %compare.40, s32[128]{0:T(128)S(1)} %eq.96), kind=kOutput, calls=%fused_computation.2.clone.1 | convolution fusion | flops 6450872320 | bytes 41943552 | tf_op jit(solution)/shard_map/while/body/eval_jaxpr/dot_general | solution.py:143
  264.8 18.0 %reshape.310 = f32[2,16,512,256]{3,2,1,0:T(8,128)} reshape(f32[256,16384]{1,0:T(8,128)} %get-tuple-element.68) | data formatting | bytes 33554432 | tf_op jit(solution)/shard_map/reshape | solution.py:178
  282.8 7.3 %dynamic-slice_bitcast_fusion = f32[16,512,256]{2,1,0:T(8,128)} fusion(f32[2,16,512,256]{3,2,1,0:T(8,128)} %reshape.310, s32[]{:T(128)S(6)} %select_n.139), kind=kLoop, calls=%fused_computation.46 | loop fusion | bytes 16777220 | tf_op jit(solution)/shard_map/jit(dynamic_index_in_dim)/squeeze | solution.py:183
  290.1 13.5 %collective-permute-done = f32[16,512,256]{2,1,0:T(8,128)} collective-permute-done((f32[16,512,256]{2,1,0:T(8,128)}, f32[16,512,256]{2,1,0:T(8,128)}, u32[]{:S(2)}, u32[]{:S(2)}) %collective-permute-start) | collective-permute-done | bytes 8388640 | tf_op jit(solution)/shard_map/ppermute | solution.py:184
  303.6 10.2 %bitcast_add_fusion = f32[16,512,256]{2,1,0:T(8,128)} fusion(f32[16,512,256]{2,1,0:T(8,128)} %collective-permute-done, f32[2,16,512,256]{3,2,1,0:T(8,128)} %reshape.310, s32[]{:T(128)S(6)} %select_n.138), kind=kLoop, calls=%fused_computation.45 | loop fusion | flops 2097152 | bytes 25165828 | tf_op jit(solution)/shard_map/add | solution.py:185
  314.8 2.2 reduce.1
  317.0 0.8 reshape.329
  317.8 3.4 all-to-all-start.4
  321.7 2.2 reduce
  323.9 0.8 reshape.327
  324.6 88.3 %all-to-all-done.4 = bf16[8,2,8192]{2,1,0:T(2,128)(2,1)S(1)} async-done(((bf16[8,2,8192]{2,1,0:T(2,128)(2,1)}), bf16[8,2,8192]{2,1,0:T(2,128)(2,1)S(1)}, u32[]{:S(2)}, u32[]{:S(2)}) %all-to-all-start.4) | async-done | bytes 262176 | tf_op jit(solution)/shard_map/all_to_all | solution.py:174
  412.9 4.2 all-to-all-start.3
  417.2 2.4 copy.135
  419.6 6.5 %all-to-all-done.3 = bf16[8,2,8192]{2,1,0:T(2,128)(2,1)S(1)} async-done(((bf16[8,2,8192]{2,1,0:T(2,128)(2,1)}), bf16[8,2,8192]{2,1,0:T(2,128)(2,1)S(1)}, u32[]{:S(2)}, u32[]{:S(2)}) %all-to-all-start.3) | async-done | bytes 262176 | tf_op jit(solution)/shard_map/all_to_all | solution.py:173
  426.1 3.5 all-to-all-start.5
  431.7 7.6 %all-to-all-done.5 = f32[512,1,256]{2,1,0:T(1,128)S(1)} async-done(((f32[512,1,256]{2,1,0:T(1,128)}), f32[512,1,256]{2,1,0:T(1,128)S(1)}, u32[]{:S(2)}, u32[]{:S(2)}) %all-to-all-start.5) | async-done | bytes 524320 | tf_op jit(solution)/shard_map/all_to_all | solution.py:186
  (86 shorter events, 10.7 us)
Async XLA Ops:
  7.2 90.9 %copy-start.1 = (bf16[64,2048]{1,0:T(8,128)(2,1)S(1)}, bf16[64,2048]{1,0:T(8,128)(2,1)}, u32[]{:S(2)}) copy-start(bf16[64,2048]{1,0:T(8,128)(2,1)} %param.7) | copy-start | bytes 786436
  7.2 98.0 %copy-start.3 = (s32[2,128,8]{1,2,0:T(8,128)S(1)}, s32[2,128,8]{1,2,0:T(8,128)}, u32[]{:S(2)}) copy-start(s32[2,128,8]{1,2,0:T(8,128)} %param.11) | copy-start | bytes 24580
  7.2 99.9 %copy-start.2 = (bf16[64,2048]{1,0:T(8,128)(2,1)S(1)}, bf16[64,2048]{1,0:T(8,128)(2,1)}, u32[]{:S(2)}) copy-start(bf16[64,2048]{1,0:T(8,128)(2,1)} %param.10) | copy-start | bytes 786436
  7.2 90.8 %all-gather.4.cloned.1.call-start = ((), (), s32[]{:S(2)}) async-start(), calls=%async_computation.7 | async-start | bytes 4456448 | tf_op jit(solution)/shard_map/all_gather | solution.py:46
  22.8 104.2 %all-gather.6.cloned.1.call-start = ((), (), s32[]{:S(2)}) async-start(), calls=%async_computation.9 | async-start | bytes 12582912 | tf_op jit(solution)/shard_map/all_gather | solution.py:47
  98.8 16.0 %all-to-all-start = ((bf16[64,8,256]{2,0,1:T(8,128)(2,1)}), bf16[64,8,256]{2,0,1:T(8,128)(2,1)S(1)}, u32[]{:S(2)}, u32[]{:S(2)}) async-start(bf16[64,8,256]{2,0,1:T(8,128)(2,1)} %bitcast.120), calls=%async_computation | async-start | bytes 524288 | tf_op jit(solution)/shard_map/all_to_all | solution.py:42
  114.8 12.1 %all-to-all-start.2 = ((bf16[64,8,256]{2,0,1:T(8,128)(2,1)}), bf16[64,8,256]{2,0,1:T(8,128)(2,1)S(1)}, u32[]{:S(2)}, u32[]{:S(2)}) async-start(bf16[64,8,256]{2,0,1:T(8,128)(2,1)} %bitcast.119), calls=%async_computation.2 | async-start | bytes 524288 | tf_op jit(solution)/shard_map/all_to_all | solution.py:44
  118.2 299.0 %reduce-scatter.2.cloned.1.call-start = ((), (), s32[]{:S(2)}) async-start(), calls=%async_computation.8 | async-start | bytes 8912896 | tf_op jit(solution)/shard_map/reduce_scatter | solution.py:185
  154.7 3.3 copy-start
  215.6 3.3 copy-start
  290.1 13.5 %collective-permute-start = (f32[16,512,256]{2,1,0:T(8,128)}, f32[16,512,256]{2,1,0:T(8,128)}, u32[]{:S(2)}, u32[]{:S(2)}) collective-permute-start(f32[16,512,256]{2,1,0:T(8,128)} %dynamic-slice_bitcast_fusion), channel_id=1, source_target_pairs={{0,1},{1,0},{2,3},{3,2},{4,5},{5,4},{6,7},{7,6},{8,9},{9,8},{10,11... | collective-permute-start | bytes 25165832 | tf_op jit(solution)/shard_map/ppermute | solution.py:184
  317.8 95.1 %all-to-all-start.4 = ((bf16[8,2,8192]{2,1,0:T(2,128)(2,1)}), bf16[8,2,8192]{2,1,0:T(2,128)(2,1)S(1)}, u32[]{:S(2)}, u32[]{:S(2)}) async-start(bf16[8,2,8192]{2,1,0:T(2,128)(2,1)} %reshape.329), calls=%async_computation.4 | async-start | bytes 524288 | tf_op jit(solution)/shard_map/all_to_all | solution.py:174
  412.9 13.1 %all-to-all-start.3 = ((bf16[8,2,8192]{2,1,0:T(2,128)(2,1)}), bf16[8,2,8192]{2,1,0:T(2,128)(2,1)S(1)}, u32[]{:S(2)}, u32[]{:S(2)}) async-start(bf16[8,2,8192]{2,1,0:T(2,128)(2,1)} %reshape.327), calls=%async_computation.3 | async-start | bytes 524288 | tf_op jit(solution)/shard_map/all_to_all | solution.py:173
  426.1 13.2 %all-to-all-start.5 = ((f32[512,1,256]{2,1,0:T(1,128)}), f32[512,1,256]{2,1,0:T(1,128)S(1)}, u32[]{:S(2)}, u32[]{:S(2)}) async-start(f32[512,1,256]{2,1,0:T(1,128)} %copy.135), calls=%async_computation.6 | async-start | bytes 1048576 | tf_op jit(solution)/shard_map/all_to_all | solution.py:186
Sparse Core Ops, SparseCore 0:
  23.0 75.0 all-gather.3
  99.8 22.8 all-gather.5
  314.0 97.9 reduce-scatter.1

commit v2 on v0

v2 whole, which is shorter than its diff:
```python
import functools
import math

import jax
import jax.numpy as jnp
from jax import lax
from jax.experimental import pallas as pl
from jax.experimental.pallas import tpu as pltpu
from jax.sharding import PartitionSpec as P

KEY_VALUE_HEADS = 2
HEAD_SIZE = 128
BLOCK = 128


def attention_kernel(
    tab_ref, q_ref, g_ref, kv_ref, out_ref, dq_ref, dkv_ref, kvg_ref,
    *, heads_dev, slots, seg_len, list_len, units_per_block, score_scale,
):
    dkv_ref[...] = jnp.zeros(dkv_ref.shape, jnp.float32)
    n_items = heads_dev * slots
    key_len = list_len * BLOCK
    base_at = n_items
    rows_at = n_items + n_items * list_len
    lane = lax.broadcasted_iota(jnp.int32, (1, key_len), 1)
    lane_block = lane // BLOCK
    lane_offset = lane % BLOCK
    query_offset = lax.broadcasted_iota(jnp.int32, (seg_len, 1), 0)
    nt = (((1,), (1,)), ((), ()))
    tn = (((0,), (0,)), ((), ()))
    for head in range(heads_dev):
        cols = slice(head * HEAD_SIZE, (head + 1) * HEAD_SIZE)

        def item_step(slot, carry, head=head, cols=cols):
            item = head * slots + slot
            rows = pl.ds(pl.multiple_of(slot * seg_len, seg_len), seg_len)
            query_block = q_ref[rows, cols]
            grad_block = g_ref[rows, cols]
            key_pos = lane_offset
            base = jnp.zeros((1, key_len), jnp.int32)
            for j in range(list_len):
                base = jnp.where(lane_block == j, tab_ref[base_at + item * list_len + j], base)
                for u in range(units_per_block):
                    src = tab_ref[rows_at + (item * list_len + j) * units_per_block + u]
                    kvg_ref[pl.ds(j * BLOCK + u * seg_len, seg_len), :] = kv_ref[
                        pl.ds(pl.multiple_of(src, seg_len), seg_len), :
                    ]
            key_pos = base + lane_offset
            query_pos = tab_ref[item] + query_offset
            allowed = key_pos <= query_pos
            key_group = kvg_ref[:, :HEAD_SIZE]
            value_group = kvg_ref[:, HEAD_SIZE:]
            scores = (
                lax.dot_general(query_block, key_group, nt, preferred_element_type=jnp.float32)
                * score_scale
            )
            masked = jnp.where(allowed, scores, -1e30)
            row_max = jnp.max(masked, axis=1, keepdims=True)
            row_sum = jnp.sum(
                jnp.where(allowed, jnp.exp(masked - row_max), 0.0), axis=1, keepdims=True
            )
            log_sum = row_max + jnp.log(row_sum)
            weights = jnp.where(allowed, jnp.exp(masked - log_sum), 0.0)
            weights_low = weights.astype(jnp.bfloat16)
            out_block = jnp.dot(
                weights_low, value_group, preferred_element_type=jnp.float32
            ).astype(jnp.bfloat16)
            out_ref[rows, cols] = out_block
            row_dot = jnp.sum(
                grad_block.astype(jnp.float32) * out_block.astype(jnp.float32),
                axis=1,
                keepdims=True,
            )
            grad_weights = lax.dot_general(
                grad_block, value_group, nt, preferred_element_type=jnp.float32
            )
            score_grad = (weights * (grad_weights - row_dot) * score_scale).astype(jnp.bfloat16)
            dq_ref[rows, cols] = jnp.dot(
                score_grad, key_group, preferred_element_type=jnp.float32
            ).astype(jnp.bfloat16)
            key_part = lax.dot_general(score_grad, query_block, tn, preferred_element_type=jnp.float32)
            value_part = lax.dot_general(weights_low, grad_block, tn, preferred_element_type=jnp.float32)
            for j in range(list_len):
                for u in range(units_per_block):
                    dst = tab_ref[rows_at + (item * list_len + j) * units_per_block + u]
                    dst_rows = pl.ds(pl.multiple_of(dst, seg_len), seg_len)
                    lo = j * BLOCK + u * seg_len
                    dkv_ref[dst_rows, :HEAD_SIZE] += key_part[lo : lo + seg_len]
                    dkv_ref[dst_rows, HEAD_SIZE:] += value_part[lo : lo + seg_len]
            return carry

        lax.fori_loop(0, slots, item_step, 0)


def body(queries, key_vector_rows, value_vector_rows, out_grad, block_list):
    ulysses_width = lax.axis_size("uly")
    cycle_size = lax.axis_size("blk")
    segment_length = queries.shape[0]
    heads_dev = block_list.shape[0]
    list_len = block_list.shape[2]
    head_width = heads_dev * HEAD_SIZE
    copy_count = ulysses_width // KEY_VALUE_HEADS
    cycle_index = lax.axis_index("blk")
    score_scale = 1.0 / math.sqrt(HEAD_SIZE)
    sub_length = min(segment_length, BLOCK)
    sub_count = segment_length // sub_length
    unit_len = min(segment_length, BLOCK)
    units_per_block = BLOCK // unit_len
    units_per_segment = segment_length // unit_len
    total_tokens = segment_length * ulysses_width * cycle_size
    units_total = total_tokens // unit_len
    query_slots = queries.reshape(segment_length, ulysses_width, head_width)
    grad_slots = out_grad.reshape(segment_length, ulysses_width, head_width)
    kv_local = jnp.concatenate(
        [
            key_vector_rows.reshape(segment_length, KEY_VALUE_HEADS, HEAD_SIZE),
            value_vector_rows.reshape(segment_length, KEY_VALUE_HEADS, HEAD_SIZE),
        ],
        axis=2,
    )
    kv_slots = jnp.repeat(kv_local, copy_count, axis=1)
    query_all, kv_mine, grad_all = (
        lax.all_to_all(query_slots, "uly", split_axis=1, concat_axis=0, tiled=True),
        lax.all_to_all(kv_slots, "uly", split_axis=1, concat_axis=0, tiled=True),
        lax.all_to_all(grad_slots, "uly", split_axis=1, concat_axis=0, tiled=True),
    )
    keys_all = lax.all_gather(kv_mine[:, 0, :], "blk", axis=0, tiled=True)
    item_count = heads_dev * ulysses_width
    item_ids = jnp.arange(item_count, dtype=jnp.int32)
    head_ids = item_ids // ulysses_width
    slot_ids = item_ids % ulysses_width
    first_pos = (slot_ids * cycle_size + cycle_index) * segment_length
    entries = block_list[head_ids, first_pos // BLOCK]
    earlier = jnp.arange(list_len)[:, None] > jnp.arange(list_len)[None, :]
    repeated = jnp.any((entries[:, :, None] == entries[:, None, :]) & earlier[None, :, :], axis=2)
    key_base = jnp.where(repeated, 1 << 30, entries * BLOCK)
    units_per_block = BLOCK // segment_length
    natural_segs = (
        entries[:, :, None] * units_per_block
        + jnp.arange(units_per_block, dtype=jnp.int32)[None, None, :]
    )
    canon_rows = (
        natural_segs % cycle_size * ulysses_width + natural_segs // cycle_size
    ) * segment_length
    table = jnp.concatenate(
        [first_pos.reshape(-1), key_base.reshape(-1), canon_rows.reshape(-1)]
    ).astype(jnp.int32)
    q_rows = query_all.reshape(ulysses_width * segment_length, head_width)
    g_rows = grad_all.reshape(ulysses_width * segment_length, head_width)
    kernel = functools.partial(
        attention_kernel,
        heads_dev=heads_dev,
        slots=ulysses_width,
        seg_len=segment_length,
        list_len=list_len,
        units_per_block=units_per_block,
        score_scale=score_scale,
    )
    out_rows, qgrad_rows, kv_grad_all = pl.pallas_call(
        kernel,
        out_shape=(
            jax.ShapeDtypeStruct(q_rows.shape, jnp.bfloat16),
            jax.ShapeDtypeStruct(q_rows.shape, jnp.bfloat16),
            jax.ShapeDtypeStruct(keys_all.shape, jnp.float32),
        ),
        in_specs=[
            pl.BlockSpec(memory_space=pltpu.SMEM),
            pl.BlockSpec(memory_space=pltpu.VMEM),
            pl.BlockSpec(memory_space=pltpu.VMEM),
            pl.BlockSpec(memory_space=pltpu.VMEM),
        ],
        out_specs=(
            pl.BlockSpec(memory_space=pltpu.VMEM),
            pl.BlockSpec(memory_space=pltpu.VMEM),
            pl.BlockSpec(memory_space=pltpu.VMEM),
        ),
        scratch_shapes=[pltpu.VMEM((list_len * BLOCK, 2 * HEAD_SIZE), jnp.bfloat16)],
        compiler_params=pltpu.CompilerParams(vmem_limit_bytes=48 * 1024 * 1024),
    )(table, q_rows, g_rows, keys_all)
    out_items = out_rows.reshape(ulysses_width * segment_length, 1, head_width)
    qgrad_items = qgrad_rows.reshape(ulysses_width * segment_length, 1, head_width)
    attended_back, qgrad_back = (
        lax.all_to_all(out_items, "uly", split_axis=0, concat_axis=1, tiled=True),
        lax.all_to_all(qgrad_items, "uly", split_axis=0, concat_axis=1, tiled=True),
    )
    attended = attended_back.reshape(segment_length, ulysses_width * head_width)
    query_grad = qgrad_back.reshape(segment_length, ulysses_width * head_width)
    owned = lax.psum_scatter(kv_grad_all, "blk", scatter_dimension=0, tiled=True)
    result_tuple = lax.all_to_all(
        owned.reshape(ulysses_width * segment_length, 1, 2 * HEAD_SIZE),
        "uly",
        split_axis=0,
        concat_axis=1,
        tiled=True,
    )
    summed_total = result_tuple.reshape(
        segment_length, KEY_VALUE_HEADS, copy_count, 2 * HEAD_SIZE
    ).sum(axis=2)
    gradient_keys = (
        summed_total[:, :, :HEAD_SIZE]
        .reshape(segment_length, KEY_VALUE_HEADS * HEAD_SIZE)
        .astype(jnp.bfloat16)
    )
    gradient_values = (
        summed_total[:, :, HEAD_SIZE:]
        .reshape(segment_length, KEY_VALUE_HEADS * HEAD_SIZE)
        .astype(jnp.bfloat16)
    )
    return (attended, query_grad, gradient_keys, gradient_values)


def solution(mesh):
    in_specs = (
        P(("uly", "blk"), None),
        P(("uly", "blk"), None),
        P(("uly", "blk"), None),
        P(("uly", "blk"), None),
        P("uly", None, None),
    )
    out_specs = (
        P(("uly", "blk"), None),
        P(("uly", "blk"), None),
        P(("uly", "blk"), None),
        P(("uly", "blk"), None),
    )
    return jax.shard_map(body, mesh=mesh, in_specs=in_specs, out_specs=out_specs, check_vma=False)
```

time: 422 us -> 292 us (0.69)
  local copies, waits for them, and re-layouts: 98.5 us -> 13.9 us
  matrix products: 62.6 us -> 0 us
  Pallas kernels: 0 us -> 26.7 us
  other arithmetic: 15.2 us -> 2.03 us
  waiting for transfers between devices: 191 us -> 196 us
    reshape x11 -> x1, local copies, waits for them, and re-layouts: 66 us -> 0.51 us  [body(): out_items = out_rows.reshape(ulysses_width * segment_length, 1, head_width)]
    dot_general x16 -> x0, matrix products: 62.6 us -> none  [the longest x2 36.4 us: group_step(): jnp.dot(place_table.T, both_parts, preferred_element_type=jnp.float32, pr...]
    pallas_call x0 -> x1, Pallas kernels: none -> 26.7 us  [body(): pl.pallas_call(kernel, out_shape=(jax.ShapeDtypeStruct(q_rows.shape, jnp....]
    concatenate x2 -> x0, local copies, waits for them, and re-layouts: 18.2 us -> none  [group_step(): jnp.concatenate([key_portion, value_portion], axis=2)]
    all_to_all x1, waiting for transfers between devices: 11.2 us -> 0.01 us  [body(): lax.all_to_all(qgrad_items, 'uly', split_axis=0, concat_axis=1, tiled=True)]
    concatenate x3 -> x2, other arithmetic: 8.13 us -> 0.1 us  [the longest x1 0.08 us: body(): jnp.concatenate([first_pos.reshape(-1), key_base.reshape(-1), canon_rows....]
    all_to_all x1, waiting for transfers between devices: 0.01 us -> 7.53 us  [body(): lax.all_to_all(out_items, 'uly', split_axis=0, concat_axis=1, tiled=True)]
    reduce_scatter x1, waiting for transfers between devices: 116 us -> 123 us  [body(): lax.psum_scatter(kv_grad_all, 'blk', scatter_dimension=0, tiled=True)]
  transfers between devices with their start and end apart: 7 -> 7, of which waited for: 6 -> 6; matrix products, arithmetic and copies ran while one was open for 4% -> 5% of each run, Pallas kernels for 0% -> 0%
where the time goes in v2:
time: 292 us; the launch traced here: 291 us
  waiting for transfers between devices  196 us (67%)
  Pallas kernels  26.7 us (9%)
  starting transfers between devices  23.7 us (8%)
  between operations  14.2 us (5%)
  local copies, waits for them, and re-layouts  13.9 us (5%)
  blocking collectives  13.9 us (5%)
    reduce_scatter x1, waiting for transfers between devices, body(): lax.psum_scatter(kv_grad_all, 'blk', scatter_dimension=0, tiled=True)  123 us
    all_gather x1, waiting for transfers between devices, body(): keys_all = lax.all_gather(kv_mine[:, 0, :], 'blk', axis=0, tiled=True)  42.8 us
    pallas_call x1, Pallas kernels, body(): pl.pallas_call(kernel, out_shape=(jax.ShapeDtypeStruct(q_rows.shape, jnp....  26.7 us
    all_to_all x1, blocking collectives, body(): lax.all_to_all(kv_slots, 'uly', split_axis=1, concat_axis=0, tiled=True)  13.9 us
    all_to_all x1, waiting for transfers between devices, body(): lax.all_to_all(grad_slots, 'uly', split_axis=1, concat_axis=0, tiled=True)  10.4 us
    all_to_all x1, waiting for transfers between devices, body(): lax.all_to_all(owned.reshape(ulysses_width * segment_length, 1, 2 * HEAD_...  7.7 us
    all_to_all x1, waiting for transfers between devices, body(): lax.all_to_all(out_items, 'uly', split_axis=0, concat_axis=1, tiled=True)  7.53 us
    all_to_all x1, starting transfers between devices, body(): lax.all_to_all(out_items, 'uly', split_axis=0, concat_axis=1, tiled=True)  7.14 us
  transfers between devices with their start and end apart: 7, of which 6 were waited for; matrix products, arithmetic and copies ran while one was open for 5% of the time, Pallas kernels for 0%

profile of v2, /device:TPU:0, one launch (start us, length us, event | category | flops | bytes accessed | tf_op | source)
XLA Modules:
  0.0 290.7 jit_solution(5211992153100360752)
XLA Ops:
  7.2 0.0 all-gather.2.cloned.1.call-start
  7.2 0.8 reshape.212
  8.0 0.8 reshape.213
  8.8 0.1 pad_maximum_fusion
  8.9 13.9 %all_to_all.90 = bf16[64,8,256]{2,0,1:T(8,128)(2,1)} all-to-all(bf16[64,8,256]{2,0,1:T(8,128)(2,1)S(1)} %bitcast.69), channel_id=1, replica_groups=mesh['uly'=8,'blk'=32] {'uly'}, dimensions={1} | all-to-all | bytes 524288 | tf_op jit(solution)/shard_map/all_to_all | solution.py:124
  22.7 0.0 all-gather.2.cloned.1.call-update
  22.8 1.7 copy.80
  24.4 3.4 %all-to-all-start = ((bf16[64,8,256]{2,0,1:T(8,128)(2,1)}), bf16[64,8,256]{2,0,1:T(8,128)(2,1)S(1)}, u32[]{:S(2)}, u32[]{:S(2)}) async-start(bf16[64,8,256]{2,0,1:T(8,128)(2,1)} %bitcast.59), calls=%async_computation | async-start | bytes 524288 | tf_op jit(solution)/shard_map/all_to_all | solution.py:123
  27.9 0.8 copy.50
  28.7 0.6 gather_fusion
  29.3 0.1 copy.51
  29.4 0.1 and_reduce_fusion
  29.5 0.1 copy.53
  29.6 0.1 iota_add_fusion
  29.7 0.1 add.111
  29.8 1.7 copy.79
  31.5 5.0 %all-to-all-done = bf16[64,8,256]{2,0,1:T(8,128)(2,1)S(1)} async-done(((bf16[64,8,256]{2,0,1:T(8,128)(2,1)}), bf16[64,8,256]{2,0,1:T(8,128)(2,1)S(1)}, u32[]{:S(2)}, u32[]{:S(2)}) %all-to-all-start) | async-done | bytes 262176 | tf_op jit(solution)/shard_map/all_to_all | solution.py:123
  36.5 3.4 %all-to-all-start.1 = ((bf16[64,8,256]{2,0,1:T(8,128)(2,1)}), bf16[64,8,256]{2,0,1:T(8,128)(2,1)S(1)}, u32[]{:S(2)}, u32[]{:S(2)}) async-start(bf16[64,8,256]{2,0,1:T(8,128)(2,1)} %bitcast.58), calls=%async_computation.1 | async-start | bytes 524288 | tf_op jit(solution)/shard_map/all_to_all | solution.py:125
  39.9 0.0 reduce-scatter.2.cloned.1.call-start
  40.0 0.1 select_n.86
  40.1 0.1 pad_add_fusion.tab_ref
  40.2 10.4 %all-to-all-done.1 = bf16[64,8,256]{2,0,1:T(8,128)(2,1)S(1)} async-done(((bf16[64,8,256]{2,0,1:T(8,128)(2,1)}), bf16[64,8,256]{2,0,1:T(8,128)(2,1)S(1)}, u32[]{:S(2)}, u32[]{:S(2)}) %all-to-all-start.1) | async-done | bytes 262176 | tf_op jit(solution)/shard_map/all_to_all | solution.py:125
  50.5 42.8 %all-gather.2.cloned.1.call-done.kv_ref = bf16[16384,256]{1,0:T(8,128)(2,1)} async-done(((bf16[512,256]{1,0:T(8,128)(2,1)}), bf16[16384,256]{1,0:T(8,128)(2,1)}) %all-gather.2.cloned.1.call-update) | async-done | bytes 8388624 | tf_op jit(solution)/shard_map/all_gather | solution.py:127
  93.3 26.7 %shard_map.84 = (bf16[512,256]{1,0:T(8,128)(2,1)S(1)}, bf16[512,256]{1,0:T(8,128)(2,1)S(1)}, f32[16384,256]{1,0:T(8,128)}) custom-call(s32[400]{0:T(512)S(1)} %pad_add_fusion.tab_ref, bf16[512,256]{1,0:T(8,128)(2,1)S(1)} %bitcast.61, bf16[512,256]{1,0:T(8,128)(2,1)S(1)} %bitcast.62, bf16[16384,256]{1,0:T(8,128)(2,1)} %all-gather.2.cloned.1.call-done.kv_ref), custom_call_target="tpu_custom_call" | custom-call | tf_op jit(solution)/shard_map/pallas_call | solution.py:159
  120.1 0.0 reduce-scatter.2.cloned.1.call-update
  120.1 0.5 broadcast.264
  120.6 0.8 reduce
  121.4 0.8 reshape.227
  122.2 7.1 %all-to-all-start.3 = ((bf16[8,2,8192]{2,1,0:T(2,128)(2,1)}), bf16[8,2,8192]{2,1,0:T(2,128)(2,1)S(1)}, u32[]{:S(2)}, u32[]{:S(2)}) async-start(bf16[8,2,8192]{2,1,0:T(2,128)(2,1)} %reshape.227), calls=%async_computation.3 | async-start | bytes 524288 | tf_op jit(solution)/shard_map/all_to_all | solution.py:183
  129.3 0.8 reduce.1
  130.1 0.8 reshape.229
  130.9 7.5 %all-to-all-done.3 = bf16[8,2,8192]{2,1,0:T(2,128)(2,1)S(1)} async-done(((bf16[8,2,8192]{2,1,0:T(2,128)(2,1)}), bf16[8,2,8192]{2,1,0:T(2,128)(2,1)S(1)}, u32[]{:S(2)}, u32[]{:S(2)}) %all-to-all-start.3) | async-done | bytes 262176 | tf_op jit(solution)/shard_map/all_to_all | solution.py:183
  138.4 3.4 %all-to-all-start.4 = ((bf16[8,2,8192]{2,1,0:T(2,128)(2,1)}), bf16[8,2,8192]{2,1,0:T(2,128)(2,1)S(1)}, u32[]{:S(2)}, u32[]{:S(2)}) async-start(bf16[8,2,8192]{2,1,0:T(2,128)(2,1)} %reshape.229), calls=%async_computation.4 | async-start | bytes 524288 | tf_op jit(solution)/shard_map/all_to_all | solution.py:184
  141.8 122.9 %reduce-scatter.2.cloned.1.call-done = f32[512,256]{1,0:T(8,128)} async-done(((f32[16384,256]{1,0:T(8,128)}), f32[512,256]{1,0:T(8,128)}) %reduce-scatter.2.cloned.1.call-update) | async-done | bytes 524304 | tf_op jit(solution)/shard_map/reduce_scatter | solution.py:188
  264.7 2.4 copy.61
  267.1 0.0 all-to-all-done.4
  267.1 6.2 %all-to-all-start.5 = ((f32[512,1,256]{2,1,0:T(1,128)}), f32[512,1,256]{2,1,0:T(1,128)S(1)}, u32[]{:S(2)}, u32[]{:S(2)}) async-start(f32[512,1,256]{2,1,0:T(1,128)} %copy.61), calls=%async_computation.6 | async-start | bytes 1048576 | tf_op jit(solution)/shard_map/all_to_all | solution.py:189
  273.4 0.3 reshape.228
  273.7 0.7 copy.71
  274.4 0.3 reshape.230
  274.7 0.7 copy.72
  275.4 7.7 %all-to-all-done.5 = f32[512,1,256]{2,1,0:T(1,128)S(1)} async-done(((f32[512,1,256]{2,1,0:T(1,128)}), f32[512,1,256]{2,1,0:T(1,128)S(1)}, u32[]{:S(2)}, u32[]{:S(2)}) %all-to-all-start.5) | async-done | bytes 524320 | tf_op jit(solution)/shard_map/all_to_all | solution.py:189
  283.2 0.6 copy_bitcast_fusion.2
  (12 shorter events, 0.2 us)
Async XLA Ops:
  7.2 86.2 %all-gather.2.cloned.1.call-start = ((), (), s32[]{:S(2)}) async-start(), calls=%async_computation.7 | async-start | bytes 8650752 | tf_op jit(solution)/shard_map/all_gather | solution.py:127
  24.4 12.1 %all-to-all-start = ((bf16[64,8,256]{2,0,1:T(8,128)(2,1)}), bf16[64,8,256]{2,0,1:T(8,128)(2,1)S(1)}, u32[]{:S(2)}, u32[]{:S(2)}) async-start(bf16[64,8,256]{2,0,1:T(8,128)(2,1)} %bitcast.59), calls=%async_computation | async-start | bytes 524288 | tf_op jit(solution)/shard_map/all_to_all | solution.py:123
  36.5 14.0 %all-to-all-start.1 = ((bf16[64,8,256]{2,0,1:T(8,128)(2,1)}), bf16[64,8,256]{2,0,1:T(8,128)(2,1)S(1)}, u32[]{:S(2)}, u32[]{:S(2)}) async-start(bf16[64,8,256]{2,0,1:T(8,128)(2,1)} %bitcast.58), calls=%async_computation.1 | async-start | bytes 524288 | tf_op jit(solution)/shard_map/all_to_all | solution.py:125
  39.9 224.8 %reduce-scatter.2.cloned.1.call-start = ((), (), s32[]{:S(2)}) async-start(), calls=%async_computation.8 | async-start | bytes 17301504 | tf_op jit(solution)/shard_map/reduce_scatter | solution.py:188
  122.2 16.2 %all-to-all-start.3 = ((bf16[8,2,8192]{2,1,0:T(2,128)(2,1)}), bf16[8,2,8192]{2,1,0:T(2,128)(2,1)S(1)}, u32[]{:S(2)}, u32[]{:S(2)}) async-start(bf16[8,2,8192]{2,1,0:T(2,128)(2,1)} %reshape.227), calls=%async_computation.3 | async-start | bytes 524288 | tf_op jit(solution)/shard_map/all_to_all | solution.py:183
  138.4 128.7 %all-to-all-start.4 = ((bf16[8,2,8192]{2,1,0:T(2,128)(2,1)}), bf16[8,2,8192]{2,1,0:T(2,128)(2,1)S(1)}, u32[]{:S(2)}, u32[]{:S(2)}) async-start(bf16[8,2,8192]{2,1,0:T(2,128)(2,1)} %reshape.229), calls=%async_computation.4 | async-start | bytes 524288 | tf_op jit(solution)/shard_map/all_to_all | solution.py:184
  267.1 16.0 %all-to-all-start.5 = ((f32[512,1,256]{2,1,0:T(1,128)}), f32[512,1,256]{2,1,0:T(1,128)S(1)}, u32[]{:S(2)}, u32[]{:S(2)}) async-start(f32[512,1,256]{2,1,0:T(1,128)} %copy.61), calls=%async_computation.6 | async-start | bytes 1048576 | tf_op jit(solution)/shard_map/all_to_all | solution.py:189
Sparse Core Ops, SparseCore 0:
  22.9 70.4 all-gather.1
  120.2 144.4 reduce-scatter.1

commit v3 on v2

--- a/solution.py
+++ b/solution.py
@@ -6,7 +6,7 @@
 from jax import lax
 from jax.experimental import pallas as pl
 from jax.experimental.pallas import tpu as pltpu
-from jax.sharding import PartitionSpec as P
+from jax.sharding import Mesh, PartitionSpec as P
 
 KEY_VALUE_HEADS = 2
 HEAD_SIZE = 128
@@ -93,7 +93,9 @@
 
 
 def body(queries, key_vector_rows, value_vector_rows, out_grad, block_list):
-    ulysses_width = lax.axis_size("uly")
+    group_count = lax.axis_size("xh")
+    row_count = lax.axis_size("y")
+    ulysses_width = group_count * row_count
     cycle_size = lax.axis_size("blk")
     segment_length = queries.shape[0]
     heads_dev = block_list.shape[0]
@@ -118,13 +120,18 @@
         ],
         axis=2,
     )
-    kv_slots = jnp.repeat(kv_local, copy_count, axis=1)
-    query_all, kv_mine, grad_all = (
-        lax.all_to_all(query_slots, "uly", split_axis=1, concat_axis=0, tiled=True),
-        lax.all_to_all(kv_slots, "uly", split_axis=1, concat_axis=0, tiled=True),
-        lax.all_to_all(grad_slots, "uly", split_axis=1, concat_axis=0, tiled=True),
-    )
-    keys_all = lax.all_gather(kv_mine[:, 0, :], "blk", axis=0, tiled=True)
+    kv_by_group = kv_local.transpose(1, 0, 2)
+    kv_pair = lax.all_to_all(kv_by_group, "xh", split_axis=0, concat_axis=0, tiled=True)
+    keys_all = lax.all_gather(
+        kv_pair.reshape(group_count * segment_length, 2 * HEAD_SIZE),
+        ("y", "blk"),
+        axis=0,
+        tiled=True,
+    )
+    query_all, grad_all = (
+        lax.all_to_all(query_slots, ("xh", "y"), split_axis=1, concat_axis=0, tiled=True),
+        lax.all_to_all(grad_slots, ("xh", "y"), split_axis=1, concat_axis=0, tiled=True),
+    )
     item_count = heads_dev * ulysses_width
     item_ids = jnp.arange(item_count, dtype=jnp.int32)
     head_ids = item_ids // ulysses_width
@@ -139,8 +146,10 @@
         entries[:, :, None] * units_per_block
         + jnp.arange(units_per_block, dtype=jnp.int32)[None, None, :]
     )
+    seg_slot = natural_segs // cycle_size
     canon_rows = (
-        natural_segs % cycle_size * ulysses_width + natural_segs // cycle_size
+        (seg_slot % row_count * cycle_size + natural_segs % cycle_size) * group_count
+        + seg_slot // row_count
     ) * segment_length
     table = jnp.concatenate(
         [first_pos.reshape(-1), key_base.reshape(-1), canon_rows.reshape(-1)]
@@ -180,47 +189,39 @@
     out_items = out_rows.reshape(ulysses_width * segment_length, 1, head_width)
     qgrad_items = qgrad_rows.reshape(ulysses_width * segment_length, 1, head_width)
     attended_back, qgrad_back = (
-        lax.all_to_all(out_items, "uly", split_axis=0, concat_axis=1, tiled=True),
-        lax.all_to_all(qgrad_items, "uly", split_axis=0, concat_axis=1, tiled=True),
+        lax.all_to_all(out_items, ("xh", "y"), split_axis=0, concat_axis=1, tiled=True),
+        lax.all_to_all(qgrad_items, ("xh", "y"), split_axis=0, concat_axis=1, tiled=True),
     )
     attended = attended_back.reshape(segment_length, ulysses_width * head_width)
     query_grad = qgrad_back.reshape(segment_length, ulysses_width * head_width)
-    owned = lax.psum_scatter(kv_grad_all, "blk", scatter_dimension=0, tiled=True)
-    result_tuple = lax.all_to_all(
-        owned.reshape(ulysses_width * segment_length, 1, 2 * HEAD_SIZE),
-        "uly",
+    owned = lax.psum_scatter(kv_grad_all, ("y", "blk"), scatter_dimension=0, tiled=True)
+    by_group = lax.all_to_all(
+        owned.reshape(group_count, segment_length, 2 * HEAD_SIZE),
+        "xh",
         split_axis=0,
-        concat_axis=1,
+        concat_axis=0,
         tiled=True,
-    )
-    summed_total = result_tuple.reshape(
-        segment_length, KEY_VALUE_HEADS, copy_count, 2 * HEAD_SIZE
-    ).sum(axis=2)
+    ).transpose(1, 0, 2)
     gradient_keys = (
-        summed_total[:, :, :HEAD_SIZE]
-        .reshape(segment_length, KEY_VALUE_HEADS * HEAD_SIZE)
+        by_group[:, :, :HEAD_SIZE]
+        .reshape(segment_length, group_count * HEAD_SIZE)
         .astype(jnp.bfloat16)
     )
     gradient_values = (
-        summed_total[:, :, HEAD_SIZE:]
-        .reshape(segment_length, KEY_VALUE_HEADS * HEAD_SIZE)
+        by_group[:, :, HEAD_SIZE:]
+        .reshape(segment_length, group_count * HEAD_SIZE)
         .astype(jnp.bfloat16)
     )
     return (attended, query_grad, gradient_keys, gradient_values)
 
 
 def solution(mesh):
-    in_specs = (
-        P(("uly", "blk"), None),
-        P(("uly", "blk"), None),
-        P(("uly", "blk"), None),
-        P(("uly", "blk"), None),
-        P("uly", None, None),
-    )
-    out_specs = (
-        P(("uly", "blk"), None),
-        P(("uly", "blk"), None),
-        P(("uly", "blk"), None),
-        P(("uly", "blk"), None),
-    )
-    return jax.shard_map(body, mesh=mesh, in_specs=in_specs, out_specs=out_specs, check_vma=False)
+    devices = mesh.devices
+    fine_mesh = Mesh(
+        devices.reshape(KEY_VALUE_HEADS, devices.shape[0] // KEY_VALUE_HEADS, devices.shape[1]),
+        ("xh", "y", "blk"),
+    )
+    rows = P(("xh", "y", "blk"), None)
+    in_specs = (rows, rows, rows, rows, P(("xh", "y"), None, None))
+    out_specs = (rows, rows, rows, rows)
+    return jax.shard_map(body, mesh=fine_mesh, in_specs=in_specs, out_specs=out_specs, check_vma=False)

time: 292 us -> 879 us (3.01)
  waiting for transfers between devices: 196 us -> 788 us
    reduce_scatter x1, waiting for transfers between devices: 123 us -> 570 us  [body(): lax.psum_scatter(kv_grad_all, ('y', 'blk'), scatter_dimension=0, tiled=True)]
    all_gather x1, waiting for transfers between devices: 42.8 us -> 192 us  [body(): lax.all_gather(kv_pair.reshape(group_count * segment_length, 2 * HEAD_SIZ...]
    all_to_all x5 -> x4, starting transfers between devices: 23.6 us -> 15.8 us  [the longest x1 5.06 us: body(): lax.all_to_all(out_items, ('xh', 'y'), split_axis=0, concat_axis=1, tiled...]
    all_to_all x1 -> x2, blocking collectives: 13.9 us -> 20.5 us  [the longest x1 11.8 us: body(): lax.all_to_all(qgrad_items, ('xh', 'y'), split_axis=0, concat_axis=1, til...]
    all_to_all x5 -> x4, waiting for transfers between devices: 30.6 us -> 25.2 us  [the longest x1 8.41 us: body(): lax.all_to_all(grad_slots, ('xh', 'y'), split_axis=1, concat_axis=0, tile...]
  transfers between devices with their start and end apart: 7 -> 6, of which waited for: 6 -> 6; matrix products, arithmetic and copies ran while one was open for 5% -> 1% of each run, Pallas kernels for 0% -> 0%
where the time goes in v3:
time: 879 us; the launch traced here: 878 us
  waiting for transfers between devices  788 us (90%)
  Pallas kernels  26.7 us (3%)
  blocking collectives  20.5 us (2%)
  starting transfers between devices  15.9 us (2%)
  between operations  14.1 us (2%)
  local copies, waits for them, and re-layouts  11.3 us (1%)
    reduce_scatter x1, waiting for transfers between devices, body(): lax.psum_scatter(kv_grad_all, ('y', 'blk'), scatter_dimension=0, tiled=True)  570 us
    all_gather x1, waiting for transfers between devices, body(): lax.all_gather(kv_pair.reshape(group_count * segment_length, 2 * HEAD_SIZ...  192 us
    pallas_call x1, Pallas kernels, body(): pl.pallas_call(kernel, out_shape=(jax.ShapeDtypeStruct(q_rows.shape, jnp....  26.7 us
  transfers between devices with their start and end apart: 6, of which 6 were waited for; matrix products, arithmetic and copies ran while one was open for 1% of the time, Pallas kernels for 0%

profile of v3, /device:TPU:0, one launch (start us, length us, event | category | flops | bytes accessed | tf_op | source)
XLA Modules:
  0.0 878.4 jit_solution(4932211710005320610)
XLA Ops:
  7.2 0.0 copy-start
  7.2 0.0 all-gather.2.cloned.1.call-start
  7.2 0.7 copy-done
  7.9 0.8 copy_bitcast_fusion.4
  8.7 8.7 all_to_all.70
  17.4 0.0 all-gather.2.cloned.1.call-update
  17.4 1.7 copy.91
  19.1 3.9 all-to-all-start
  23.0 0.8 copy.58
  23.9 0.6 gather_fusion
  24.5 0.1 copy.59
  24.6 0.1 and_reduce_fusion
  24.7 0.1 copy.61
  24.8 0.1 iota_add_fusion
  24.8 0.1 add.122
  25.0 1.7 copy.90
  26.7 5.1 all-to-all-done
  31.7 3.4 all-to-all-start.1
  35.2 0.0 reduce-scatter.2.cloned.1.call-start
  35.2 0.1 select_n.95
  35.3 0.1 pad_add_fusion.tab_ref
  35.4 8.4 all-to-all-done.1
  43.8 192.4 %all-gather.2.cloned.1.call-done.kv_ref = bf16[16384,256]{1,0:T(8,128)(2,1)} async-done(((bf16[128,256]{1,0:T(8,128)(2,1)}), bf16[16384,256]{1,0:T(8,128)(2,1)}) %all-gather.2.cloned.1.call-update) | async-done | bytes 8388624 | tf_op jit(solution)/shard_map/all_gather | solution.py:125
  236.3 26.7 %shard_map.84 = (bf16[512,256]{1,0:T(8,128)(2,1)S(1)}, bf16[512,256]{1,0:T(8,128)(2,1)S(1)}, f32[16384,256]{1,0:T(8,128)}) custom-call(s32[400]{0:T(512)S(1)} %pad_add_fusion.tab_ref, bf16[512,256]{1,0:T(8,128)(2,1)S(1)} %bitcast.66, bf16[512,256]{1,0:T(8,128)(2,1)S(1)} %bitcast.67, bf16[16384,256]{1,0:T(8,128)(2,1)} %all-gather.2.cloned.1.call-done.kv_ref), custom_call_target="tpu_custom_call" | custom-call | tf_op jit(solution)/shard_map/pallas_call | solution.py:168
  263.0 0.0 reduce-scatter.2.cloned.1.call-update
  263.0 0.5 broadcast.284
  263.5 0.8 reduce
  264.3 0.8 reshape.221
  265.1 5.1 all-to-all-start.3
  270.2 0.8 reduce.1
  271.0 0.1 reshape.223
  271.1 7.8 all-to-all-done.3
  278.9 11.8 %all_to_all.71 = bf16[8,2,8192]{2,1,0:T(2,128)(2,1)S(1)} all-to-all(bf16[8,2,8192]{2,1,0:T(2,128)(2,1)S(1)} %reshape.223), channel_id=1, replica_groups=mesh['xh'=2,'y'=4,'blk'=32] {'xh','y'}, dimensions={0} | all-to-all | bytes 524288 | tf_op jit(solution)/shard_map/all_to_all | solution.py:193
  290.7 570.1 %reduce-scatter.2.cloned.1.call-done = f32[128,256]{1,0:T(8,128)} async-done(((f32[16384,256]{1,0:T(8,128)}), f32[128,256]{1,0:T(8,128)}) %reduce-scatter.2.cloned.1.call-update) | async-done | bytes 131088 | tf_op jit(solution)/shard_map/reduce_scatter | solution.py:197
  860.8 3.4 all-to-all-start.5
  864.3 0.3 reshape.222
  864.6 0.7 copy.80
  865.3 0.3 reshape.224
  865.6 0.7 copy.81
  866.4 3.9 all-to-all-done.5
  870.3 0.6 copy.92
  870.9 0.6 copy.93
  (10 shorter events, 0.2 us)
Async XLA Ops:
  7.2 0.8 copy-start
  7.2 229.1 %all-gather.2.cloned.1.call-start = ((), (), s32[]{:S(2)}) async-start(), calls=%async_computation.7 | async-start | bytes 8454144 | tf_op jit(solution)/shard_map/all_gather | solution.py:125
  19.1 12.7 %all-to-all-start = ((bf16[64,8,256]{2,0,1:T(8,128)(2,1)}), bf16[64,8,256]{2,0,1:T(8,128)(2,1)S(1)}, u32[]{:S(2)}, u32[]{:S(2)}) async-start(bf16[64,8,256]{2,0,1:T(8,128)(2,1)} %bitcast.63), calls=%async_computation | async-start | bytes 524288 | tf_op jit(solution)/shard_map/all_to_all | solution.py:132
  31.7 12.1 %all-to-all-start.1 = ((bf16[64,8,256]{2,0,1:T(8,128)(2,1)}), bf16[64,8,256]{2,0,1:T(8,128)(2,1)S(1)}, u32[]{:S(2)}, u32[]{:S(2)}) async-start(bf16[64,8,256]{2,0,1:T(8,128)(2,1)} %bitcast.62), calls=%async_computation.1 | async-start | bytes 524288 | tf_op jit(solution)/shard_map/all_to_all | solution.py:133
  35.2 825.7 %reduce-scatter.2.cloned.1.call-start = ((), (), s32[]{:S(2)}) async-start(), calls=%async_computation.8 | async-start | bytes 16908288 | tf_op jit(solution)/shard_map/reduce_scatter | solution.py:197
  265.1 13.8 %all-to-all-start.3 = ((bf16[8,2,8192]{2,1,0:T(2,128)(2,1)}), bf16[8,2,8192]{2,1,0:T(2,128)(2,1)S(1)}, u32[]{:S(2)}, u32[]{:S(2)}) async-start(bf16[8,2,8192]{2,1,0:T(2,128)(2,1)} %reshape.221), calls=%async_computation.3 | async-start | bytes 524288 | tf_op jit(solution)/shard_map/all_to_all | solution.py:192
  860.8 9.4 %all-to-all-start.5 = ((f32[2,64,256]{2,1,0:T(8,128)}), f32[2,64,256]{2,1,0:T(8,128)S(1)}, u32[]{:S(2)}, u32[]{:S(2)}) async-start(f32[2,64,256]{2,1,0:T(8,128)} %bitcast.77), calls=%async_computation.6 | async-start | bytes 262144 | tf_op jit(solution)/shard_map/all_to_all | solution.py:198
Sparse Core Ops, SparseCore 0:
  17.5 218.6 all-gather.1
  263.1 597.6 reduce-scatter.1

commit v4 on v2

--- a/solution.py
+++ b/solution.py
@@ -6,7 +6,7 @@
 from jax import lax
 from jax.experimental import pallas as pl
 from jax.experimental.pallas import tpu as pltpu
-from jax.sharding import PartitionSpec as P
+from jax.sharding import Mesh, PartitionSpec as P
 
 KEY_VALUE_HEADS = 2
 HEAD_SIZE = 128
@@ -22,6 +22,8 @@
     key_len = list_len * BLOCK
     base_at = n_items
     rows_at = n_items + n_items * list_len
+    grad_at = rows_at + n_items * list_len * units_per_block
+    plane_rows = dkv_ref.shape[1]
     lane = lax.broadcasted_iota(jnp.int32, (1, key_len), 1)
     lane_block = lane // BLOCK
     lane_offset = lane % BLOCK
@@ -82,11 +84,12 @@
             value_part = lax.dot_general(weights_low, grad_block, tn, preferred_element_type=jnp.float32)
             for j in range(list_len):
                 for u in range(units_per_block):
-                    dst = tab_ref[rows_at + (item * list_len + j) * units_per_block + u]
-                    dst_rows = pl.ds(pl.multiple_of(dst, seg_len), seg_len)
+                    dst = tab_ref[grad_at + (item * list_len + j) * units_per_block + u]
+                    plane = dst // plane_rows
+                    dst_rows = pl.ds(pl.multiple_of(dst % plane_rows, seg_len), seg_len)
                     lo = j * BLOCK + u * seg_len
-                    dkv_ref[dst_rows, :HEAD_SIZE] += key_part[lo : lo + seg_len]
-                    dkv_ref[dst_rows, HEAD_SIZE:] += value_part[lo : lo + seg_len]
+                    dkv_ref[plane, dst_rows, :HEAD_SIZE] += key_part[lo : lo + seg_len]
+                    dkv_ref[plane, dst_rows, HEAD_SIZE:] += value_part[lo : lo + seg_len]
             return carry
 
         lax.fori_loop(0, slots, item_step, 0)
@@ -94,13 +97,16 @@
 
 def body(queries, key_vector_rows, value_vector_rows, out_grad, block_list):
     ulysses_width = lax.axis_size("uly")
-    cycle_size = lax.axis_size("blk")
+    core_count = lax.axis_size("core")
+    chip_count = lax.axis_size("chip")
+    cycle_size = chip_count * core_count
     segment_length = queries.shape[0]
     heads_dev = block_list.shape[0]
     list_len = block_list.shape[2]
     head_width = heads_dev * HEAD_SIZE
     copy_count = ulysses_width // KEY_VALUE_HEADS
-    cycle_index = lax.axis_index("blk")
+    core_index = lax.axis_index("core")
+    cycle_index = lax.axis_index("chip") * core_count + core_index
     score_scale = 1.0 / math.sqrt(HEAD_SIZE)
     sub_length = min(segment_length, BLOCK)
     sub_count = segment_length // sub_length
@@ -124,7 +130,7 @@
         lax.all_to_all(kv_slots, "uly", split_axis=1, concat_axis=0, tiled=True),
         lax.all_to_all(grad_slots, "uly", split_axis=1, concat_axis=0, tiled=True),
     )
-    keys_all = lax.all_gather(kv_mine[:, 0, :], "blk", axis=0, tiled=True)
+    keys_all = lax.all_gather(kv_mine[:, 0, :], ("chip", "core"), axis=0, tiled=True)
     item_count = heads_dev * ulysses_width
     item_ids = jnp.arange(item_count, dtype=jnp.int32)
     head_ids = item_ids // ulysses_width
@@ -142,8 +148,22 @@
     canon_rows = (
         natural_segs % cycle_size * ulysses_width + natural_segs // cycle_size
     ) * segment_length
+    seg_owner = natural_segs % cycle_size
+    grad_rows = (
+        (
+            (seg_owner % core_count - core_index) % core_count * chip_count
+            + seg_owner // core_count
+        )
+        * ulysses_width
+        + natural_segs // cycle_size
+    ) * segment_length
     table = jnp.concatenate(
-        [first_pos.reshape(-1), key_base.reshape(-1), canon_rows.reshape(-1)]
+        [
+            first_pos.reshape(-1),
+            key_base.reshape(-1),
+            canon_rows.reshape(-1),
+            grad_rows.reshape(-1),
+        ]
     ).astype(jnp.int32)
     q_rows = query_all.reshape(ulysses_width * segment_length, head_width)
     g_rows = grad_all.reshape(ulysses_width * segment_length, head_width)
@@ -161,7 +181,9 @@
         out_shape=(
             jax.ShapeDtypeStruct(q_rows.shape, jnp.bfloat16),
             jax.ShapeDtypeStruct(q_rows.shape, jnp.bfloat16),
-            jax.ShapeDtypeStruct(keys_all.shape, jnp.float32),
+            jax.ShapeDtypeStruct(
+                (core_count, keys_all.shape[0] // core_count, keys_all.shape[1]), jnp.float32
+            ),
         ),
         in_specs=[
             pl.BlockSpec(memory_space=pltpu.SMEM),
@@ -185,7 +207,11 @@
     )
     attended = attended_back.reshape(segment_length, ulysses_width * head_width)
     query_grad = qgrad_back.reshape(segment_length, ulysses_width * head_width)
-    owned = lax.psum_scatter(kv_grad_all, "blk", scatter_dimension=0, tiled=True)
+    received = lax.ppermute(kv_grad_all[1], "core", [(0, 1), (1, 0)])
+    chip_part = (kv_grad_all[0] + received).reshape(
+        chip_count, ulysses_width * segment_length, 2 * HEAD_SIZE
+    )
+    owned = lax.psum_scatter(chip_part, "chip", scatter_dimension=0, tiled=True)
     result_tuple = lax.all_to_all(
         owned.reshape(ulysses_width * segment_length, 1, 2 * HEAD_SIZE),
         "uly",
@@ -210,17 +236,12 @@
 
 
 def solution(mesh):
-    in_specs = (
-        P(("uly", "blk"), None),
-        P(("uly", "blk"), None),
-        P(("uly", "blk"), None),
-        P(("uly", "blk"), None),
-        P("uly", None, None),
-    )
-    out_specs = (
-        P(("uly", "blk"), None),
-        P(("uly", "blk"), None),
-        P(("uly", "blk"), None),
-        P(("uly", "blk"), None),
-    )
-    return jax.shard_map(body, mesh=mesh, in_specs=in_specs, out_specs=out_specs, check_vma=False)
+    devices = mesh.devices
+    cores = 2
+    fine_mesh = Mesh(
+        devices.reshape(devices.shape[0], devices.shape[1] // cores, cores), ("uly", "chip", "core")
+    )
+    rows = P(("uly", "chip", "core"), None)
+    in_specs = (rows, rows, rows, rows, P("uly", None, None))
+    out_specs = (rows, rows, rows, rows)
+    return jax.shard_map(body, mesh=fine_mesh, in_specs=in_specs, out_specs=out_specs, check_vma=False)

time: 292 us -> 277 us (0.949)
  waiting for transfers between devices: 196 us -> 169 us
  other arithmetic: 2.03 us -> 12.1 us
  local copies, waits for them, and re-layouts: 13.9 us -> 17.8 us
    reduce_scatter x1, waiting for transfers between devices: 123 us -> 79.2 us  [body(): owned = lax.psum_scatter(chip_part, 'chip', scatter_dimension=0, tiled=True)]
    ppermute x0 -> x1, waiting for transfers between devices: none -> 13.1 us  [body(): received = lax.ppermute(kv_grad_all[1], 'core', [(0, 1), (1, 0)])]
    add x0 -> x1, other arithmetic: none -> 10.1 us  [body(): kv_grad_all[0] + received]
    all_to_all x1, waiting for transfers between devices: 0.01 us -> 7.53 us  [body(): lax.all_to_all(qgrad_items, 'uly', split_axis=0, concat_axis=1, tiled=True)]
    all_to_all x1, waiting for transfers between devices: 7.53 us -> 2.45 us  [body(): lax.all_to_all(out_items, 'uly', split_axis=0, concat_axis=1, tiled=True)]
    squeeze x0 -> x1, local copies, waits for them, and re-layouts: none -> 3.92 us  [body(): received = lax.ppermute(kv_grad_all[1], 'core', [(0, 1), (1, 0)])]
    all_to_all x1, starting transfers between devices: 7.14 us -> 3.41 us  [body(): lax.all_to_all(out_items, 'uly', split_axis=0, concat_axis=1, tiled=True)]
    all_to_all x1, starting transfers between devices: 3.41 us -> 7.12 us  [body(): lax.all_to_all(qgrad_items, 'uly', split_axis=0, concat_axis=1, tiled=True)]
  transfers between devices with their start and end apart: 7 -> 8, of which waited for: 6 -> 8; matrix products, arithmetic and copies ran while one was open for 5% -> 5% of each run, Pallas kernels for 0% -> 0%
where the time goes in v4:
time: 277 us; the launch traced here: 276 us
  waiting for transfers between devices  169 us (61%)
  Pallas kernels  26.9 us (10%)
  starting transfers between devices  21.7 us (8%)
  local copies, waits for them, and re-layouts  17.8 us (6%)
  between operations  14.2 us (5%)
  blocking collectives  13.9 us (5%)
  other arithmetic  12.1 us (4%)
    reduce_scatter x1, waiting for transfers between devices, body(): owned = lax.psum_scatter(chip_part, 'chip', scatter_dimension=0, tiled=True)  79.2 us
    all_gather x1, waiting for transfers between devices, body(): lax.all_gather(kv_mine[:, 0, :], ('chip', 'core'), axis=0, tiled=True)  42.8 us
    pallas_call x1, Pallas kernels, body(): pl.pallas_call(kernel, out_shape=(jax.ShapeDtypeStruct(q_rows.shape, jnp....  26.9 us
    all_to_all x1, blocking collectives, body(): lax.all_to_all(kv_slots, 'uly', split_axis=1, concat_axis=0, tiled=True)  13.9 us
    ppermute x1, waiting for transfers between devices, body(): received = lax.ppermute(kv_grad_all[1], 'core', [(0, 1), (1, 0)])  13.1 us
    all_to_all x1, waiting for transfers between devices, body(): lax.all_to_all(grad_slots, 'uly', split_axis=1, concat_axis=0, tiled=True)  10.4 us
    add x1, other arithmetic, body(): kv_grad_all[0] + received  10.1 us
    all_to_all x1, waiting for transfers between devices, body(): lax.all_to_all(owned.reshape(ulysses_width * segment_length, 1, 2 * HEAD_...  8.89 us
  transfers between devices with their start and end apart: 8, of which 8 were waited for; matrix products, arithmetic and copies ran while one was open for 5% of the time, Pallas kernels for 0%

profile of v4, /device:TPU:0, one launch (start us, length us, event | category | flops | bytes accessed | tf_op | source)
XLA Modules:
  0.0 276.0 jit_solution(12918839815903799351)
XLA Ops:
  7.2 0.0 all-gather.2.cloned.1.call-start
  7.2 0.8 reshape.218
  8.0 0.8 reshape.219
  8.8 0.1 pad_maximum_fusion
  8.9 13.9 %all_to_all.90 = bf16[64,8,256]{2,0,1:T(8,128)(2,1)} all-to-all(bf16[64,8,256]{2,0,1:T(8,128)(2,1)S(1)} %bitcast.75), channel_id=1, replica_groups=mesh['uly'=8,'chip'=16,'core'=2] {'uly'}, dimensions={1} | all-to-all | bytes 524288 | tf_op jit(solution)/shard_map/all_to_all | solution.py:130
  22.7 0.0 all-gather.2.cloned.1.call-update
  22.8 1.7 copy.91
  24.4 3.4 %all-to-all-start = ((bf16[64,8,256]{2,0,1:T(8,128)(2,1)}), bf16[64,8,256]{2,0,1:T(8,128)(2,1)S(1)}, u32[]{:S(2)}, u32[]{:S(2)}) async-start(bf16[64,8,256]{2,0,1:T(8,128)(2,1)} %bitcast.64), calls=%async_computation | async-start | bytes 524288 | tf_op jit(solution)/shard_map/all_to_all | solution.py:129
  27.9 0.8 copy.61
  28.7 0.6 gather_fusion
  29.3 0.1 copy.62
  29.4 0.1 and_reduce_fusion
  29.5 0.1 copy.64
  29.6 0.1 iota_add_fusion
  29.7 0.1 add.143
  29.8 1.7 copy.90
  31.5 5.0 %all-to-all-done = bf16[64,8,256]{2,0,1:T(8,128)(2,1)S(1)} async-done(((bf16[64,8,256]{2,0,1:T(8,128)(2,1)}), bf16[64,8,256]{2,0,1:T(8,128)(2,1)S(1)}, u32[]{:S(2)}, u32[]{:S(2)}) %all-to-all-start) | async-done | bytes 262176 | tf_op jit(solution)/shard_map/all_to_all | solution.py:129
  36.5 3.4 %all-to-all-start.1 = ((bf16[64,8,256]{2,0,1:T(8,128)(2,1)}), bf16[64,8,256]{2,0,1:T(8,128)(2,1)S(1)}, u32[]{:S(2)}, u32[]{:S(2)}) async-start(bf16[64,8,256]{2,0,1:T(8,128)(2,1)} %bitcast.63), calls=%async_computation.1 | async-start | bytes 524288 | tf_op jit(solution)/shard_map/all_to_all | solution.py:131
  39.9 0.0 reduce-scatter.2.cloned.1.call-start
  40.0 0.1 select_n.105
  40.1 0.1 pad_add_fusion.tab_ref
  40.2 10.4 %all-to-all-done.1 = bf16[64,8,256]{2,0,1:T(8,128)(2,1)S(1)} async-done(((bf16[64,8,256]{2,0,1:T(8,128)(2,1)}), bf16[64,8,256]{2,0,1:T(8,128)(2,1)S(1)}, u32[]{:S(2)}, u32[]{:S(2)}) %all-to-all-start.1) | async-done | bytes 262176 | tf_op jit(solution)/shard_map/all_to_all | solution.py:131
  50.5 42.8 %all-gather.2.cloned.1.call-done.kv_ref = bf16[16384,256]{1,0:T(8,128)(2,1)} async-done(((bf16[512,256]{1,0:T(8,128)(2,1)}), bf16[16384,256]{1,0:T(8,128)(2,1)}) %all-gather.2.cloned.1.call-update) | async-done | bytes 8388624 | tf_op jit(solution)/shard_map/all_gather | solution.py:133
  93.3 26.9 %shard_map.84 = (bf16[512,256]{1,0:T(8,128)(2,1)S(1)}, bf16[512,256]{1,0:T(8,128)(2,1)S(1)}, f32[2,8192,256]{2,1,0:T(8,128)}) custom-call(s32[656]{0:T(1024)S(1)} %pad_add_fusion.tab_ref, bf16[512,256]{1,0:T(8,128)(2,1)S(1)} %bitcast.66, bf16[512,256]{1,0:T(8,128)(2,1)S(1)} %bitcast.67, bf16[16384,256]{1,0:T(8,128)(2,1)} %all-gather.2.cloned.1.call-done.kv_ref), custom_call_target="tpu_custom_call" | custom-call | tf_op jit(solution)/shard_map/pallas_call | solution.py:179
  120.2 3.9 %slice_bitcast_fusion = f32[8192,256]{1,0:T(8,128)S(1)} fusion(f32[2,8192,256]{2,1,0:T(8,128)} %get-tuple-element.9), kind=kLoop, calls=%fused_computation.2 | loop fusion | bytes 16777216 | tf_op jit(solution)/shard_map/squeeze | solution.py:210
  124.2 0.3 collective-permute-start
  124.5 13.1 %collective-permute-done = f32[8192,256]{1,0:T(8,128)} collective-permute-done((f32[8192,256]{1,0:T(8,128)S(1)}, f32[8192,256]{1,0:T(8,128)}, u32[]{:S(2)}, u32[]{:S(2)}) %collective-permute-start) | collective-permute-done | bytes 8388640 | tf_op jit(solution)/shard_map/ppermute | solution.py:210
  137.5 10.1 %bitcast_add_fusion = f32[8192,256]{1,0:T(8,128)} fusion(f32[8192,256]{1,0:T(8,128)} %collective-permute-done, f32[2,8192,256]{2,1,0:T(8,128)} %get-tuple-element.9), kind=kLoop, calls=%fused_computation.1 | loop fusion | flops 2097152 | bytes 25165824 | tf_op jit(solution)/shard_map/add | solution.py:211
  147.6 0.0 reduce-scatter.2.cloned.1.call-update
  147.7 0.5 broadcast.346
  148.2 0.8 reduce.1
  149.0 0.8 reshape.236
  149.7 7.1 %all-to-all-start.4 = ((bf16[8,2,8192]{2,1,0:T(2,128)(2,1)}), bf16[8,2,8192]{2,1,0:T(2,128)(2,1)S(1)}, u32[]{:S(2)}, u32[]{:S(2)}) async-start(bf16[8,2,8192]{2,1,0:T(2,128)(2,1)} %reshape.236), calls=%async_computation.4 | async-start | bytes 524288 | tf_op jit(solution)/shard_map/all_to_all | solution.py:206
  156.9 0.8 reduce
  157.7 0.8 reshape.234
  158.5 7.5 %all-to-all-done.4 = bf16[8,2,8192]{2,1,0:T(2,128)(2,1)S(1)} async-done(((bf16[8,2,8192]{2,1,0:T(2,128)(2,1)}), bf16[8,2,8192]{2,1,0:T(2,128)(2,1)S(1)}, u32[]{:S(2)}, u32[]{:S(2)}) %all-to-all-start.4) | async-done | bytes 262176 | tf_op jit(solution)/shard_map/all_to_all | solution.py:206
  166.0 3.4 %all-to-all-start.3 = ((bf16[8,2,8192]{2,1,0:T(2,128)(2,1)}), bf16[8,2,8192]{2,1,0:T(2,128)(2,1)S(1)}, u32[]{:S(2)}, u32[]{:S(2)}) async-start(bf16[8,2,8192]{2,1,0:T(2,128)(2,1)} %reshape.234), calls=%async_computation.3 | async-start | bytes 524288 | tf_op jit(solution)/shard_map/all_to_all | solution.py:205
  169.4 79.2 %reduce-scatter.2.cloned.1.call-done = f32[1,512,256]{2,1,0:T(8,128)} async-done(((f32[16,512,256]{2,1,0:T(8,128)}), f32[1,512,256]{2,1,0:T(8,128)}) %reduce-scatter.2.cloned.1.call-update) | async-done | bytes 524304 | tf_op jit(solution)/shard_map/reduce_scatter | solution.py:214
  248.6 2.4 copy.72
  251.0 2.5 all-to-all-done.3
  253.4 4.0 %all-to-all-start.5 = ((f32[512,1,256]{2,1,0:T(1,128)}), f32[512,1,256]{2,1,0:T(1,128)S(1)}, u32[]{:S(2)}, u32[]{:S(2)}) async-start(f32[512,1,256]{2,1,0:T(1,128)} %copy.72), calls=%async_computation.6 | async-start | bytes 1048576 | tf_op jit(solution)/shard_map/all_to_all | solution.py:215
  257.4 0.3 reshape.235
  257.7 0.7 copy.82
  258.4 0.3 reshape.237
  258.8 0.7 copy.83
  259.5 8.9 %all-to-all-done.5 = f32[512,1,256]{2,1,0:T(1,128)S(1)} async-done(((f32[512,1,256]{2,1,0:T(1,128)}), f32[512,1,256]{2,1,0:T(1,128)S(1)}, u32[]{:S(2)}, u32[]{:S(2)}) %all-to-all-start.5) | async-done | bytes 524320 | tf_op jit(solution)/shard_map/all_to_all | solution.py:215
  268.5 0.6 copy_bitcast_fusion.2
  (13 shorter events, 0.3 us)
Async XLA Ops:
  7.2 86.2 %all-gather.2.cloned.1.call-start = ((), (), s32[]{:S(2)}) async-start(), calls=%async_computation.7 | async-start | bytes 8650752 | tf_op jit(solution)/shard_map/all_gather | solution.py:133
  24.4 12.1 %all-to-all-start = ((bf16[64,8,256]{2,0,1:T(8,128)(2,1)}), bf16[64,8,256]{2,0,1:T(8,128)(2,1)S(1)}, u32[]{:S(2)}, u32[]{:S(2)}) async-start(bf16[64,8,256]{2,0,1:T(8,128)(2,1)} %bitcast.64), calls=%async_computation | async-start | bytes 524288 | tf_op jit(solution)/shard_map/all_to_all | solution.py:129
  36.5 14.0 %all-to-all-start.1 = ((bf16[64,8,256]{2,0,1:T(8,128)(2,1)}), bf16[64,8,256]{2,0,1:T(8,128)(2,1)S(1)}, u32[]{:S(2)}, u32[]{:S(2)}) async-start(bf16[64,8,256]{2,0,1:T(8,128)(2,1)} %bitcast.63), calls=%async_computation.1 | async-start | bytes 524288 | tf_op jit(solution)/shard_map/all_to_all | solution.py:131
  39.9 208.7 %reduce-scatter.2.cloned.1.call-start = ((), (), s32[]{:S(2)}) async-start(), calls=%async_computation.8 | async-start | bytes 8912896 | tf_op jit(solution)/shard_map/reduce_scatter | solution.py:214
  124.2 13.4 %collective-permute-start = (f32[8192,256]{1,0:T(8,128)S(1)}, f32[8192,256]{1,0:T(8,128)}, u32[]{:S(2)}, u32[]{:S(2)}) collective-permute-start(f32[8192,256]{1,0:T(8,128)S(1)} %slice_bitcast_fusion), channel_id=1, source_target_pairs={{0,1},{1,0},{2,3},{3,2},{4,5},{5,4},{6,7},{7,6},{8,9},{9,8},{10,11... | collective-permute-start | bytes 25165832 | tf_op jit(solution)/shard_map/ppermute | solution.py:210
  149.7 16.2 %all-to-all-start.4 = ((bf16[8,2,8192]{2,1,0:T(2,128)(2,1)}), bf16[8,2,8192]{2,1,0:T(2,128)(2,1)S(1)}, u32[]{:S(2)}, u32[]{:S(2)}) async-start(bf16[8,2,8192]{2,1,0:T(2,128)(2,1)} %reshape.236), calls=%async_computation.4 | async-start | bytes 524288 | tf_op jit(solution)/shard_map/all_to_all | solution.py:206
  166.0 87.4 %all-to-all-start.3 = ((bf16[8,2,8192]{2,1,0:T(2,128)(2,1)}), bf16[8,2,8192]{2,1,0:T(2,128)(2,1)S(1)}, u32[]{:S(2)}, u32[]{:S(2)}) async-start(bf16[8,2,8192]{2,1,0:T(2,128)(2,1)} %reshape.234), calls=%async_computation.3 | async-start | bytes 524288 | tf_op jit(solution)/shard_map/all_to_all | solution.py:205
  253.4 14.9 %all-to-all-start.5 = ((f32[512,1,256]{2,1,0:T(1,128)}), f32[512,1,256]{2,1,0:T(1,128)S(1)}, u32[]{:S(2)}, u32[]{:S(2)}) async-start(f32[512,1,256]{2,1,0:T(1,128)} %copy.72), calls=%async_computation.6 | async-start | bytes 1048576 | tf_op jit(solution)/shard_map/all_to_all | solution.py:215
Sparse Core Ops, SparseCore 0:
  22.9 70.4 all-gather.1
  147.8 100.7 reduce-scatter.1

commit v5 on v4

--- a/solution.py
+++ b/solution.py
@@ -14,16 +14,24 @@
 
 
 def attention_kernel(
-    tab_ref, q_ref, g_ref, kv_ref, out_ref, dq_ref, dkv_ref, kvg_ref,
-    *, heads_dev, slots, seg_len, list_len, units_per_block, score_scale,
+    *refs, heads_dev, slots, first_slot, slot_count, carry_low, seg_len, list_len,
+    units_per_block, score_scale,
 ):
-    dkv_ref[...] = jnp.zeros(dkv_ref.shape, jnp.float32)
+    if carry_low:
+        tab_ref, q_ref, g_ref, kv_ref, low_in_ref, out_ref, dq_ref, low_ref, kvg_ref = refs
+        high_ref = None
+        low_ref[...] = low_in_ref[...]
+    else:
+        tab_ref, q_ref, g_ref, kv_ref, out_ref, dq_ref, low_ref, high_ref, kvg_ref = refs
+        low_ref[...] = jnp.zeros(low_ref.shape, jnp.float32)
+        high_ref[...] = jnp.zeros(high_ref.shape, jnp.float32)
     n_items = heads_dev * slots
     key_len = list_len * BLOCK
     base_at = n_items
     rows_at = n_items + n_items * list_len
     grad_at = rows_at + n_items * list_len * units_per_block
-    plane_rows = dkv_ref.shape[1]
+    plane_rows = low_ref.shape[1]
+    half_rows = low_ref.shape[0] * plane_rows
     lane = lax.broadcasted_iota(jnp.int32, (1, key_len), 1)
     lane_block = lane // BLOCK
     lane_offset = lane % BLOCK
@@ -33,9 +41,11 @@
     for head in range(heads_dev):
         cols = slice(head * HEAD_SIZE, (head + 1) * HEAD_SIZE)
 
-        def item_step(slot, carry, head=head, cols=cols):
+        def item_step(step, carry, head=head, cols=cols):
+            slot = first_slot + step
             item = head * slots + slot
             rows = pl.ds(pl.multiple_of(slot * seg_len, seg_len), seg_len)
+            out_rows = pl.ds(pl.multiple_of(step * seg_len, seg_len), seg_len)
             query_block = q_ref[rows, cols]
             grad_block = g_ref[rows, cols]
             key_pos = lane_offset
@@ -67,7 +77,7 @@
             out_block = jnp.dot(
                 weights_low, value_group, preferred_element_type=jnp.float32
             ).astype(jnp.bfloat16)
-            out_ref[rows, cols] = out_block
+            out_ref[out_rows, cols] = out_block
             row_dot = jnp.sum(
                 grad_block.astype(jnp.float32) * out_block.astype(jnp.float32),
                 axis=1,
@@ -77,7 +87,7 @@
                 grad_block, value_group, nt, preferred_element_type=jnp.float32
             )
             score_grad = (weights * (grad_weights - row_dot) * score_scale).astype(jnp.bfloat16)
-            dq_ref[rows, cols] = jnp.dot(
+            dq_ref[out_rows, cols] = jnp.dot(
                 score_grad, key_group, preferred_element_type=jnp.float32
             ).astype(jnp.bfloat16)
             key_part = lax.dot_general(score_grad, query_block, tn, preferred_element_type=jnp.float32)
@@ -85,14 +95,27 @@
             for j in range(list_len):
                 for u in range(units_per_block):
                     dst = tab_ref[grad_at + (item * list_len + j) * units_per_block + u]
-                    plane = dst // plane_rows
+                    half = dst // half_rows
+                    plane = dst // plane_rows % 2
                     dst_rows = pl.ds(pl.multiple_of(dst % plane_rows, seg_len), seg_len)
                     lo = j * BLOCK + u * seg_len
-                    dkv_ref[plane, dst_rows, :HEAD_SIZE] += key_part[lo : lo + seg_len]
-                    dkv_ref[plane, dst_rows, HEAD_SIZE:] += value_part[lo : lo + seg_len]
+                    key_rows = key_part[lo : lo + seg_len]
+                    value_rows = value_part[lo : lo + seg_len]
+
+                    @pl.when(half == 0)
+                    def _(plane=plane, dst_rows=dst_rows, key_rows=key_rows, value_rows=value_rows):
+                        low_ref[plane, dst_rows, :HEAD_SIZE] += key_rows
+                        low_ref[plane, dst_rows, HEAD_SIZE:] += value_rows
+
+                    if high_ref is not None:
+
+                        @pl.when(half != 0)
+                        def _(plane=plane, dst_rows=dst_rows, key_rows=key_rows, value_rows=value_rows):
+                            high_ref[plane, dst_rows, :HEAD_SIZE] += key_rows
+                            high_ref[plane, dst_rows, HEAD_SIZE:] += value_rows
             return carry
 
-        lax.fori_loop(0, slots, item_step, 0)
+        lax.fori_loop(0, slot_count, item_step, 0)
 
 
 def body(queries, key_vector_rows, value_vector_rows, out_grad, block_list):
@@ -148,14 +171,14 @@
     canon_rows = (
         natural_segs % cycle_size * ulysses_width + natural_segs // cycle_size
     ) * segment_length
+    half_slots = ulysses_width // 2
     seg_owner = natural_segs % cycle_size
+    seg_slot = natural_segs // cycle_size
+    plane_rows = chip_count * half_slots * segment_length
     grad_rows = (
-        (
-            (seg_owner % core_count - core_index) % core_count * chip_count
-            + seg_owner // core_count
-        )
-        * ulysses_width
-        + natural_segs // cycle_size
+        seg_slot // half_slots * core_count + (seg_owner % core_count - core_index) % core_count
+    ) * plane_rows + (
+        seg_owner // core_count * half_slots + seg_slot % half_slots
     ) * segment_length
     table = jnp.concatenate(
         [
@@ -167,8 +190,7 @@
     ).astype(jnp.int32)
     q_rows = query_all.reshape(ulysses_width * segment_length, head_width)
     g_rows = grad_all.reshape(ulysses_width * segment_length, head_width)
-    kernel = functools.partial(
-        attention_kernel,
+    common = dict(
         heads_dev=heads_dev,
         slots=ulysses_width,
         seg_len=segment_length,
@@ -176,29 +198,47 @@
         units_per_block=units_per_block,
         score_scale=score_scale,
     )
-    out_rows, qgrad_rows, kv_grad_all = pl.pallas_call(
-        kernel,
-        out_shape=(
-            jax.ShapeDtypeStruct(q_rows.shape, jnp.bfloat16),
-            jax.ShapeDtypeStruct(q_rows.shape, jnp.bfloat16),
-            jax.ShapeDtypeStruct(
-                (core_count, keys_all.shape[0] // core_count, keys_all.shape[1]), jnp.float32
-            ),
+    plane_shape = jax.ShapeDtypeStruct((core_count, plane_rows, 2 * HEAD_SIZE), jnp.float32)
+    high_count = ulysses_width - half_slots
+    part_rows = jax.ShapeDtypeStruct((high_count * segment_length, head_width), jnp.bfloat16)
+    low_rows = jax.ShapeDtypeStruct((half_slots * segment_length, head_width), jnp.bfloat16)
+    vmem = pl.BlockSpec(memory_space=pltpu.VMEM)
+    smem = pl.BlockSpec(memory_space=pltpu.SMEM)
+    scratch = [pltpu.VMEM((list_len * BLOCK, 2 * HEAD_SIZE), jnp.bfloat16)]
+    params = pltpu.CompilerParams(vmem_limit_bytes=48 * 1024 * 1024)
+    out_high, qgrad_high, low_part, high_part = pl.pallas_call(
+        functools.partial(
+            attention_kernel, first_slot=half_slots, slot_count=high_count, carry_low=False, **common
         ),
-        in_specs=[
-            pl.BlockSpec(memory_space=pltpu.SMEM),
-            pl.BlockSpec(memory_space=pltpu.VMEM),
-            pl.BlockSpec(memory_space=pltpu.VMEM),
-            pl.BlockSpec(memory_space=pltpu.VMEM),
-        ],
-        out_specs=(
-            pl.BlockSpec(memory_space=pltpu.VMEM),
-            pl.BlockSpec(memory_space=pltpu.VMEM),
-            pl.BlockSpec(memory_space=pltpu.VMEM),
+        out_shape=(part_rows, part_rows, plane_shape, plane_shape),
+        in_specs=[smem, vmem, vmem, vmem],
+        out_specs=(vmem, vmem, vmem, vmem),
+        scratch_shapes=scratch,
+        compiler_params=params,
+    )(table, q_rows, g_rows, keys_all)
+    pair = [(0, 1), (1, 0)]
+    high_sum = (high_part[0] + lax.ppermute(high_part[1], "core", pair)).reshape(
+        chip_count, half_slots * segment_length, 2 * HEAD_SIZE
+    )
+    high_sum, low_part = lax.optimization_barrier((high_sum, low_part))
+    owned_high = lax.psum_scatter(high_sum, "chip", scatter_dimension=0, tiled=True)
+    out_low, qgrad_low, low_total = pl.pallas_call(
+        functools.partial(
+            attention_kernel, first_slot=0, slot_count=half_slots, carry_low=True, **common
         ),
-        scratch_shapes=[pltpu.VMEM((list_len * BLOCK, 2 * HEAD_SIZE), jnp.bfloat16)],
-        compiler_params=pltpu.CompilerParams(vmem_limit_bytes=48 * 1024 * 1024),
-    )(table, q_rows, g_rows, keys_all)
+        out_shape=(low_rows, low_rows, plane_shape),
+        in_specs=[smem, vmem, vmem, vmem, vmem],
+        out_specs=(vmem, vmem, vmem),
+        scratch_shapes=scratch,
+        compiler_params=params,
+    )(table, q_rows, g_rows, keys_all, low_part)
+    low_sum = (low_total[0] + lax.ppermute(low_total[1], "core", pair)).reshape(
+        chip_count, half_slots * segment_length, 2 * HEAD_SIZE
+    )
+    owned_low = lax.psum_scatter(low_sum, "chip", scatter_dimension=0, tiled=True)
+    owned = jnp.concatenate([owned_low, owned_high], axis=1)
+    out_rows = jnp.concatenate([out_low, out_high], axis=0)
+    qgrad_rows = jnp.concatenate([qgrad_low, qgrad_high], axis=0)
     out_items = out_rows.reshape(ulysses_width * segment_length, 1, head_width)
     qgrad_items = qgrad_rows.reshape(ulysses_width * segment_length, 1, head_width)
     attended_back, qgrad_back = (
@@ -207,11 +247,6 @@
     )
     attended = attended_back.reshape(segment_length, ulysses_width * head_width)
     query_grad = qgrad_back.reshape(segment_length, ulysses_width * head_width)
-    received = lax.ppermute(kv_grad_all[1], "core", [(0, 1), (1, 0)])
-    chip_part = (kv_grad_all[0] + received).reshape(
-        chip_count, ulysses_width * segment_length, 2 * HEAD_SIZE
-    )
-    owned = lax.psum_scatter(chip_part, "chip", scatter_dimension=0, tiled=True)
     result_tuple = lax.all_to_all(
         owned.reshape(ulysses_width * segment_length, 1, 2 * HEAD_SIZE),
         "uly",

time: 277 us -> 316 us (1.14)
  waiting for transfers between devices: 169 us -> 192 us
  Pallas kernels: 26.9 us -> 42.3 us
  starting transfers between devices: 21.7 us -> 27.4 us
  other arithmetic: 12.1 us -> 8.15 us
    reduce_scatter x1 -> x2, waiting for transfers between devices: 79.2 us -> 100 us  [the longest x1 80.4 us: body(): lax.psum_scatter(low_sum, 'chip', scatter_dimension=0, tiled=True)]
    pallas_call x1 -> x2, Pallas kernels: 26.9 us -> 42.3 us  [the longest x1 21.6 us: body(): pl.pallas_call(functools.partial(attention_kernel, first_slot=half_slots,...]
    all_to_all x1, waiting for transfers between devices: 2.45 us -> 11.7 us  [body(): lax.all_to_all(out_items, 'uly', split_axis=0, concat_axis=1, tiled=True)]
    all_to_all x1, waiting for transfers between devices: 7.53 us -> 0.01 us  [body(): lax.all_to_all(qgrad_items, 'uly', split_axis=0, concat_axis=1, tiled=True)]
    add x1 -> x3, other arithmetic: 10.1 us -> 5.02 us  [the longest x1 2.5 us: body(): high_part[0] + lax.ppermute(high_part[1], 'core', pair)]
    all_to_all x1, starting transfers between devices: 3.41 us -> 7.15 us  [body(): lax.all_to_all(out_items, 'uly', split_axis=0, concat_axis=1, tiled=True)]
    ppermute x1 -> x2, waiting for transfers between devices: 13.1 us -> 13.9 us  [the longest x1 6.94 us: body(): lax.ppermute(low_total[1], 'core', pair)]
  transfers between devices with their start and end apart: 8 -> 10, of which waited for: 8 -> 9; matrix products, arithmetic and copies ran while one was open for 5% -> 6% of each run, Pallas kernels for 0% -> 7%
where the time goes in v5:
time: 316 us; the launch traced here: 315 us
  waiting for transfers between devices  192 us (61%)
  Pallas kernels  42.3 us (13%)
  starting transfers between devices  27.4 us (9%)
  local copies, waits for them, and re-layouts  18.2 us (6%)
  blocking collectives  13.9 us (4%)
  between operations  13.9 us (4%)
  other arithmetic  8.15 us (3%)
    reduce_scatter x1, waiting for transfers between devices, body(): lax.psum_scatter(low_sum, 'chip', scatter_dimension=0, tiled=True)  80.4 us
    all_gather x1, waiting for transfers between devices, body(): lax.all_gather(kv_mine[:, 0, :], ('chip', 'core'), axis=0, tiled=True)  42.8 us
    pallas_call x1, Pallas kernels, body(): pl.pallas_call(functools.partial(attention_kernel, first_slot=half_slots,...  21.6 us
    pallas_call x1, Pallas kernels, body(): pl.pallas_call(functools.partial(attention_kernel, first_slot=0, slot_cou...  20.7 us
    reduce_scatter x1, waiting for transfers between devices, body(): lax.psum_scatter(high_sum, 'chip', scatter_dimension=0, tiled=True)  19.7 us
    all_to_all x1, blocking collectives, body(): lax.all_to_all(kv_slots, 'uly', split_axis=1, concat_axis=0, tiled=True)  13.9 us
    all_to_all x1, waiting for transfers between devices, body(): lax.all_to_all(out_items, 'uly', split_axis=0, concat_axis=1, tiled=True)  11.7 us
    all_to_all x1, waiting for transfers between devices, body(): lax.all_to_all(grad_slots, 'uly', split_axis=1, concat_axis=0, tiled=True)  10.4 us
  transfers between devices with their start and end apart: 10, of which 9 were waited for; matrix products, arithmetic and copies ran while one was open for 6% of the time, Pallas kernels for 7%

profile of v5, /device:TPU:0, one launch (start us, length us, event | category | flops | bytes accessed | tf_op | source)
XLA Modules:
  0.0 315.4 jit_solution(10397257488333700496)
XLA Ops:
  7.2 0.8 reshape.221
  8.0 0.8 reshape.222
  8.9 13.9 %all_to_all.90 = bf16[64,8,256]{2,0,1:T(8,128)(2,1)} all-to-all(bf16[64,8,256]{2,0,1:T(8,128)(2,1)S(1)} %bitcast.84), channel_id=1, replica_groups=mesh['uly'=8,'chip'=16,'core'=2] {'uly'}, dimensions={1} | all-to-all | bytes 524288 | tf_op jit(solution)/shard_map/all_to_all | solution.py:153
  22.8 1.7 copy.94
  24.4 3.4 %all-to-all-start = ((bf16[64,8,256]{2,0,1:T(8,128)(2,1)}), bf16[64,8,256]{2,0,1:T(8,128)(2,1)S(1)}, u32[]{:S(2)}, u32[]{:S(2)}) async-start(bf16[64,8,256]{2,0,1:T(8,128)(2,1)} %bitcast.72), calls=%async_computation | async-start | bytes 524288 | tf_op jit(solution)/shard_map/all_to_all | solution.py:152
  27.9 0.8 copy.64
  28.7 0.6 gather_fusion
  29.3 0.1 copy.65
  29.4 0.1 and_reduce_fusion
  29.5 0.1 copy.67
  29.6 0.1 iota_add_fusion
  29.7 0.1 add.159
  29.8 1.7 copy.93
  31.5 5.0 %all-to-all-done = bf16[64,8,256]{2,0,1:T(8,128)(2,1)S(1)} async-done(((bf16[64,8,256]{2,0,1:T(8,128)(2,1)}), bf16[64,8,256]{2,0,1:T(8,128)(2,1)S(1)}, u32[]{:S(2)}, u32[]{:S(2)}) %all-to-all-start) | async-done | bytes 262176 | tf_op jit(solution)/shard_map/all_to_all | solution.py:152
  36.5 3.4 %all-to-all-start.1 = ((bf16[64,8,256]{2,0,1:T(8,128)(2,1)}), bf16[64,8,256]{2,0,1:T(8,128)(2,1)S(1)}, u32[]{:S(2)}, u32[]{:S(2)}) async-start(bf16[64,8,256]{2,0,1:T(8,128)(2,1)} %bitcast.71), calls=%async_computation.1 | async-start | bytes 524288 | tf_op jit(solution)/shard_map/all_to_all | solution.py:154
  40.0 0.1 select_n.114
  40.1 0.1 pad_add_fusion.refs_0_
  40.2 10.4 %all-to-all-done.1 = bf16[64,8,256]{2,0,1:T(8,128)(2,1)S(1)} async-done(((bf16[64,8,256]{2,0,1:T(8,128)(2,1)}), bf16[64,8,256]{2,0,1:T(8,128)(2,1)S(1)}, u32[]{:S(2)}, u32[]{:S(2)}) %all-to-all-start.1) | async-done | bytes 262176 | tf_op jit(solution)/shard_map/all_to_all | solution.py:154
  50.5 42.8 %all-gather.2.cloned.1.call-done.refs_3_ = bf16[16384,256]{1,0:T(8,128)(2,1)} async-done(((bf16[512,256]{1,0:T(8,128)(2,1)}), bf16[16384,256]{1,0:T(8,128)(2,1)}) %all-gather.2.cloned.1.call-update) | async-done | bytes 8388624 | tf_op jit(solution)/shard_map/all_gather | solution.py:156
  93.3 21.6 %shard_map.84 = (bf16[256,256]{1,0:T(8,128)(2,1)S(1)}, bf16[256,256]{1,0:T(8,128)(2,1)S(1)}, f32[2,4096,256]{2,1,0:T(8,128)}, f32[2,4096,256]{2,1,0:T(8,128)}) custom-call(s32[656]{0:T(1024)S(1)} %pad_add_fusion.refs_0_, bf16[512,256]{1,0:T(8,128)(2,1)S(1)} %bitcast.74, bf16[512,256]{1,0:T(8,128)(2,1)S(1)} %bitcast.76, ...), custom_call_target="tpu_custom_call" | custom-call | tf_op jit(solution)/shard_map/pallas_call | solution.py:209
  115.0 2.6 slice_bitcast_fusion.1
  117.6 0.3 collective-permute-start
  117.9 6.9 %collective-permute-done = f32[4096,256]{1,0:T(8,128)S(1)} collective-permute-done((f32[4096,256]{1,0:T(8,128)S(1)}, f32[4096,256]{1,0:T(8,128)S(1)}, u32[]{:S(2)}, u32[]{:S(2)}) %collective-permute-start) | collective-permute-done | bytes 4194336 | tf_op jit(solution)/shard_map/ppermute | solution.py:220
  124.8 2.5 bitcast_add_fusion.1
  127.4 20.7 %shard_map.85 = (bf16[256,256]{1,0:T(8,128)(2,1)S(1)}, bf16[256,256]{1,0:T(8,128)(2,1)S(1)}, f32[2,4096,256]{2,1,0:T(8,128)}) custom-call(s32[656]{0:T(1024)S(1)} %pad_add_fusion.refs_0_, bf16[512,256]{1,0:T(8,128)(2,1)S(1)} %bitcast.75, bf16[512,256]{1,0:T(8,128)(2,1)S(1)} %bitcast.77, bf16[16384,256]{1,0:T(8,128)(2,1)} %all-gather.2.cloned.1.call-done.refs_3_, ...), custom_call_target="tpu_custom_call" | custom-call | tf_op jit(solution)/shard_map/pallas_call | solution.py:225
  148.1 2.7 slice_bitcast_fusion
  150.8 0.3 collective-permute-start.1
  151.1 6.9 %collective-permute-done.1 = f32[4096,256]{1,0:T(8,128)S(1)} collective-permute-done((f32[4096,256]{1,0:T(8,128)S(1)}, f32[4096,256]{1,0:T(8,128)S(1)}, u32[]{:S(2)}, u32[]{:S(2)}) %collective-permute-start.1) | collective-permute-done | bytes 4194336 | tf_op jit(solution)/shard_map/ppermute | solution.py:235
  158.0 2.5 bitcast_add_fusion
  160.6 0.5 broadcast.360
  161.1 0.8 reduce
  161.9 0.8 reshape.238
  162.7 7.2 %all-to-all-start.3 = ((bf16[8,2,8192]{2,1,0:T(2,128)(2,1)}), bf16[8,2,8192]{2,1,0:T(2,128)(2,1)S(1)}, u32[]{:S(2)}, u32[]{:S(2)}) async-start(bf16[8,2,8192]{2,1,0:T(2,128)(2,1)} %reshape.238), calls=%async_computation.3 | async-start | bytes 524288 | tf_op jit(solution)/shard_map/all_to_all | solution.py:245
  169.8 0.8 reduce.1
  170.6 0.8 reshape.240
  171.4 11.7 %all-to-all-done.3 = bf16[8,2,8192]{2,1,0:T(2,128)(2,1)S(1)} async-done(((bf16[8,2,8192]{2,1,0:T(2,128)(2,1)}), bf16[8,2,8192]{2,1,0:T(2,128)(2,1)S(1)}, u32[]{:S(2)}, u32[]{:S(2)}) %all-to-all-start.3) | async-done | bytes 262176 | tf_op jit(solution)/shard_map/all_to_all | solution.py:245
  183.1 5.9 %all-to-all-start.4 = ((bf16[8,2,8192]{2,1,0:T(2,128)(2,1)}), bf16[8,2,8192]{2,1,0:T(2,128)(2,1)S(1)}, u32[]{:S(2)}, u32[]{:S(2)}) async-start(bf16[8,2,8192]{2,1,0:T(2,128)(2,1)} %reshape.240), calls=%async_computation.4 | async-start | bytes 524288 | tf_op jit(solution)/shard_map/all_to_all | solution.py:246
  189.0 19.7 %reduce-scatter.5.cloned.1.call-done = f32[1,256,256]{2,1,0:T(8,128)} async-done(((f32[16,256,256]{2,1,0:T(8,128)}), f32[1,256,256]{2,1,0:T(8,128)}) %reduce-scatter.5.cloned.1.call-update) | async-done | bytes 262160 | tf_op jit(solution)/shard_map/reduce_scatter | solution.py:224
  208.7 80.4 %reduce-scatter.3.cloned.1.call-done = f32[1,256,256]{2,1,0:T(8,128)} async-done(((f32[16,256,256]{2,1,0:T(8,128)}), f32[1,256,256]{2,1,0:T(8,128)}) %reduce-scatter.3.cloned.1.call-update) | async-done | bytes 262160 | tf_op jit(solution)/shard_map/reduce_scatter | solution.py:238
  289.1 1.1 maximum_bitcast_fusion
  290.2 1.3 copy.75
  291.6 6.8 %all-to-all-start.5 = ((f32[512,1,256]{2,1,0:T(1,128)}), f32[512,1,256]{2,1,0:T(1,128)S(1)}, u32[]{:S(2)}, u32[]{:S(2)}) async-start(f32[512,1,256]{2,1,0:T(1,128)} %copy.75), calls=%async_computation.7 | async-start | bytes 1048576 | tf_op jit(solution)/shard_map/all_to_all | solution.py:250
  298.3 0.3 reshape.239
  298.7 0.7 copy.85
  299.4 0.3 reshape.241
  299.7 0.7 copy.86
  300.4 7.7 %all-to-all-done.5 = f32[512,1,256]{2,1,0:T(1,128)S(1)} async-done(((f32[512,1,256]{2,1,0:T(1,128)}), f32[512,1,256]{2,1,0:T(1,128)S(1)}, u32[]{:S(2)}, u32[]{:S(2)}) %all-to-all-start.5) | async-done | bytes 524320 | tf_op jit(solution)/shard_map/all_to_all | solution.py:250
  308.2 0.6 copy_bitcast_fusion.2
  (26 shorter events, 0.6 us)
Async XLA Ops:
  7.2 86.2 %all-gather.2.cloned.1.call-start = ((), (), s32[]{:S(2)}) async-start(), calls=%async_computation.8 | async-start | bytes 8650752 | tf_op jit(solution)/shard_map/all_gather | solution.py:156
  24.4 12.1 %all-to-all-start = ((bf16[64,8,256]{2,0,1:T(8,128)(2,1)}), bf16[64,8,256]{2,0,1:T(8,128)(2,1)S(1)}, u32[]{:S(2)}, u32[]{:S(2)}) async-start(bf16[64,8,256]{2,0,1:T(8,128)(2,1)} %bitcast.72), calls=%async_computation | async-start | bytes 524288 | tf_op jit(solution)/shard_map/all_to_all | solution.py:152
  36.5 14.0 %all-to-all-start.1 = ((bf16[64,8,256]{2,0,1:T(8,128)(2,1)}), bf16[64,8,256]{2,0,1:T(8,128)(2,1)S(1)}, u32[]{:S(2)}, u32[]{:S(2)}) async-start(bf16[64,8,256]{2,0,1:T(8,128)(2,1)} %bitcast.71), calls=%async_computation.1 | async-start | bytes 524288 | tf_op jit(solution)/shard_map/all_to_all | solution.py:154
  39.9 168.8 %reduce-scatter.5.cloned.1.call-start = ((), (), s32[]{:S(2)}) async-start(), calls=%async_computation.10 | async-start | bytes 4456448 | tf_op jit(solution)/shard_map/reduce_scatter | solution.py:224
  115.0 9.9 %copy-start.1 = (f32[2,4096,256]{2,1,0:T(8,128)S(1)}, f32[2,4096,256]{2,1,0:T(8,128)}, u32[]{:S(2)}) copy-start(f32[2,4096,256]{2,1,0:T(8,128)} %get-tuple-element.13) | copy-start | bytes 25165828
  117.6 7.2 %collective-permute-start = (f32[4096,256]{1,0:T(8,128)S(1)}, f32[4096,256]{1,0:T(8,128)S(1)}, u32[]{:S(2)}, u32[]{:S(2)}) collective-permute-start(f32[4096,256]{1,0:T(8,128)S(1)} %slice_bitcast_fusion.1), channel_id=1, source_target_pairs={{0,1},{1,0},{2,3},{3,2},{4,5},{5,4},{6,7},{7,6},{8,9},{9,8},{10,11... | collective-permute-start | bytes 12582920 | tf_op jit(solution)/shard_map/ppermute | solution.py:220
  127.4 161.8 %reduce-scatter.3.cloned.1.call-start = ((), (), s32[]{:S(2)}) async-start(), calls=%async_computation.9 | async-start | bytes 4456448 | tf_op jit(solution)/shard_map/reduce_scatter | solution.py:238
  148.1 9.9 %copy-start = (f32[2,4096,256]{2,1,0:T(8,128)S(1)}, f32[2,4096,256]{2,1,0:T(8,128)}, u32[]{:S(2)}) copy-start(f32[2,4096,256]{2,1,0:T(8,128)} %get-tuple-element.20) | copy-start | bytes 25165828
  150.8 7.2 %collective-permute-start.1 = (f32[4096,256]{1,0:T(8,128)S(1)}, f32[4096,256]{1,0:T(8,128)S(1)}, u32[]{:S(2)}, u32[]{:S(2)}) collective-permute-start(f32[4096,256]{1,0:T(8,128)S(1)} %slice_bitcast_fusion), channel_id=1, source_target_pairs={{0,1},{1,0},{2,3},{3,2},{4,5},{5,4},{6,7},{7,6},{8,9},{9,8},{10,11... | collective-permute-start | bytes 12582920 | tf_op jit(solution)/shard_map/ppermute | solution.py:235
  162.7 20.4 %all-to-all-start.3 = ((bf16[8,2,8192]{2,1,0:T(2,128)(2,1)}), bf16[8,2,8192]{2,1,0:T(2,128)(2,1)S(1)}, u32[]{:S(2)}, u32[]{:S(2)}) async-start(bf16[8,2,8192]{2,1,0:T(2,128)(2,1)} %reshape.238), calls=%async_computation.3 | async-start | bytes 524288 | tf_op jit(solution)/shard_map/all_to_all | solution.py:245
  183.1 108.5 %all-to-all-start.4 = ((bf16[8,2,8192]{2,1,0:T(2,128)(2,1)}), bf16[8,2,8192]{2,1,0:T(2,128)(2,1)S(1)}, u32[]{:S(2)}, u32[]{:S(2)}) async-start(bf16[8,2,8192]{2,1,0:T(2,128)(2,1)} %reshape.240), calls=%async_computation.4 | async-start | bytes 524288 | tf_op jit(solution)/shard_map/all_to_all | solution.py:246
  291.6 16.6 %all-to-all-start.5 = ((f32[512,1,256]{2,1,0:T(1,128)}), f32[512,1,256]{2,1,0:T(1,128)S(1)}, u32[]{:S(2)}, u32[]{:S(2)}) async-start(f32[512,1,256]{2,1,0:T(1,128)} %copy.75), calls=%async_computation.7 | async-start | bytes 1048576 | tf_op jit(solution)/shard_map/all_to_all | solution.py:250
Sparse Core Ops, SparseCore 0:
  22.9 70.4 all-gather.1
  127.5 81.1 reduce-scatter.4
  211.3 77.8 reduce-scatter.2

commit v6 on v4

--- a/solution.py
+++ b/solution.py
@@ -14,30 +14,31 @@
 
 
 def attention_kernel(
-    tab_ref, q_ref, g_ref, kv_ref, out_ref, dq_ref, dkv_ref, kvg_ref,
+    tab_ref, q_ref, g_ref, pq_ref, pg_ref, kv_ref, out_ref, dq_ref, dkv_ref, kvg_ref,
     *, heads_dev, slots, seg_len, list_len, units_per_block, score_scale,
 ):
     dkv_ref[...] = jnp.zeros(dkv_ref.shape, jnp.float32)
-    n_items = heads_dev * slots
+    n_items = 2 * heads_dev * slots
     key_len = list_len * BLOCK
     base_at = n_items
     rows_at = n_items + n_items * list_len
     grad_at = rows_at + n_items * list_len * units_per_block
-    plane_rows = dkv_ref.shape[1]
     lane = lax.broadcasted_iota(jnp.int32, (1, key_len), 1)
     lane_block = lane // BLOCK
     lane_offset = lane % BLOCK
     query_offset = lax.broadcasted_iota(jnp.int32, (seg_len, 1), 0)
     nt = (((1,), (1,)), ((), ()))
     tn = (((0,), (0,)), ((), ()))
-    for head in range(heads_dev):
+    sources = ((q_ref, g_ref, True), (pq_ref, pg_ref, False))
+    for source, (sq_ref, sg_ref, own) in enumerate(sources):
+      for head in range(heads_dev):
         cols = slice(head * HEAD_SIZE, (head + 1) * HEAD_SIZE)
 
-        def item_step(slot, carry, head=head, cols=cols):
-            item = head * slots + slot
+        def item_step(slot, carry, head=head, cols=cols, source=source, sq_ref=sq_ref, sg_ref=sg_ref, own=own):
+            item = (source * heads_dev + head) * slots + slot
             rows = pl.ds(pl.multiple_of(slot * seg_len, seg_len), seg_len)
-            query_block = q_ref[rows, cols]
-            grad_block = g_ref[rows, cols]
+            query_block = sq_ref[rows, cols]
+            grad_block = sg_ref[rows, cols]
             key_pos = lane_offset
             base = jnp.zeros((1, key_len), jnp.int32)
             for j in range(list_len):
@@ -67,7 +68,8 @@
             out_block = jnp.dot(
                 weights_low, value_group, preferred_element_type=jnp.float32
             ).astype(jnp.bfloat16)
-            out_ref[rows, cols] = out_block
+            if own:
+                out_ref[rows, cols] = out_block
             row_dot = jnp.sum(
                 grad_block.astype(jnp.float32) * out_block.astype(jnp.float32),
                 axis=1,
@@ -77,19 +79,24 @@
                 grad_block, value_group, nt, preferred_element_type=jnp.float32
             )
             score_grad = (weights * (grad_weights - row_dot) * score_scale).astype(jnp.bfloat16)
-            dq_ref[rows, cols] = jnp.dot(
-                score_grad, key_group, preferred_element_type=jnp.float32
-            ).astype(jnp.bfloat16)
+            if own:
+                dq_ref[rows, cols] = jnp.dot(
+                    score_grad, key_group, preferred_element_type=jnp.float32
+                ).astype(jnp.bfloat16)
             key_part = lax.dot_general(score_grad, query_block, tn, preferred_element_type=jnp.float32)
             value_part = lax.dot_general(weights_low, grad_block, tn, preferred_element_type=jnp.float32)
             for j in range(list_len):
                 for u in range(units_per_block):
                     dst = tab_ref[grad_at + (item * list_len + j) * units_per_block + u]
-                    plane = dst // plane_rows
-                    dst_rows = pl.ds(pl.multiple_of(dst % plane_rows, seg_len), seg_len)
+                    dst_rows = pl.ds(pl.multiple_of(jnp.maximum(dst, 0), seg_len), seg_len)
                     lo = j * BLOCK + u * seg_len
-                    dkv_ref[plane, dst_rows, :HEAD_SIZE] += key_part[lo : lo + seg_len]
-                    dkv_ref[plane, dst_rows, HEAD_SIZE:] += value_part[lo : lo + seg_len]
+                    key_rows = key_part[lo : lo + seg_len]
+                    value_rows = value_part[lo : lo + seg_len]
+
+                    @pl.when(dst >= 0)
+                    def _(dst_rows=dst_rows, key_rows=key_rows, value_rows=value_rows):
+                        dkv_ref[dst_rows, :HEAD_SIZE] += key_rows
+                        dkv_ref[dst_rows, HEAD_SIZE:] += value_rows
             return carry
 
         lax.fori_loop(0, slots, item_step, 0)
@@ -135,38 +142,41 @@
     item_ids = jnp.arange(item_count, dtype=jnp.int32)
     head_ids = item_ids // ulysses_width
     slot_ids = item_ids % ulysses_width
-    first_pos = (slot_ids * cycle_size + cycle_index) * segment_length
-    entries = block_list[head_ids, first_pos // BLOCK]
     earlier = jnp.arange(list_len)[:, None] > jnp.arange(list_len)[None, :]
-    repeated = jnp.any((entries[:, :, None] == entries[:, None, :]) & earlier[None, :, :], axis=2)
-    key_base = jnp.where(repeated, 1 << 30, entries * BLOCK)
     units_per_block = BLOCK // segment_length
-    natural_segs = (
-        entries[:, :, None] * units_per_block
-        + jnp.arange(units_per_block, dtype=jnp.int32)[None, None, :]
-    )
-    canon_rows = (
-        natural_segs % cycle_size * ulysses_width + natural_segs // cycle_size
-    ) * segment_length
-    seg_owner = natural_segs % cycle_size
-    grad_rows = (
-        (
-            (seg_owner % core_count - core_index) % core_count * chip_count
-            + seg_owner // core_count
+    chip_index = lax.axis_index("chip")
+
+    def item_table(source_core):
+        first_pos = (slot_ids * cycle_size + chip_index * core_count + source_core) * segment_length
+        entries = block_list[head_ids, first_pos // BLOCK]
+        repeated = jnp.any(
+            (entries[:, :, None] == entries[:, None, :]) & earlier[None, :, :], axis=2
         )
-        * ulysses_width
-        + natural_segs // cycle_size
-    ) * segment_length
+        key_base = jnp.where(repeated, 1 << 30, entries * BLOCK)
+        natural_segs = (
+            entries[:, :, None] * units_per_block
+            + jnp.arange(units_per_block, dtype=jnp.int32)[None, None, :]
+        )
+        canon_rows = (
+            natural_segs % cycle_size * ulysses_width + natural_segs // cycle_size
+        ) * segment_length
+        seg_owner = natural_segs % cycle_size
+        grad_rows = jnp.where(
+            seg_owner % core_count == core_index,
+            (seg_owner // core_count * ulysses_width + natural_segs // cycle_size) * segment_length,
+            -1,
+        )
+        return first_pos, key_base, canon_rows, grad_rows
+
+    mine = item_table(core_index)
+    peer = item_table(1 - core_index)
     table = jnp.concatenate(
-        [
-            first_pos.reshape(-1),
-            key_base.reshape(-1),
-            canon_rows.reshape(-1),
-            grad_rows.reshape(-1),
-        ]
+        [jnp.concatenate([a.reshape(-1), b.reshape(-1)]) for a, b in zip(mine, peer)]
     ).astype(jnp.int32)
     q_rows = query_all.reshape(ulysses_width * segment_length, head_width)
     g_rows = grad_all.reshape(ulysses_width * segment_length, head_width)
+    pair = [(0, 1), (1, 0)]
+    peer_q, peer_g = lax.ppermute((q_rows, g_rows), "core", pair)
     kernel = functools.partial(
         attention_kernel,
         heads_dev=heads_dev,
@@ -182,15 +192,11 @@
             jax.ShapeDtypeStruct(q_rows.shape, jnp.bfloat16),
             jax.ShapeDtypeStruct(q_rows.shape, jnp.bfloat16),
             jax.ShapeDtypeStruct(
-                (core_count, keys_all.shape[0] // core_count, keys_all.shape[1]), jnp.float32
+                (keys_all.shape[0] // core_count, keys_all.shape[1]), jnp.float32
             ),
         ),
-        in_specs=[
-            pl.BlockSpec(memory_space=pltpu.SMEM),
-            pl.BlockSpec(memory_space=pltpu.VMEM),
-            pl.BlockSpec(memory_space=pltpu.VMEM),
-            pl.BlockSpec(memory_space=pltpu.VMEM),
-        ],
+        in_specs=[pl.BlockSpec(memory_space=pltpu.SMEM)]
+        + [pl.BlockSpec(memory_space=pltpu.VMEM)] * 5,
         out_specs=(
             pl.BlockSpec(memory_space=pltpu.VMEM),
             pl.BlockSpec(memory_space=pltpu.VMEM),
@@ -198,7 +204,7 @@
         ),
         scratch_shapes=[pltpu.VMEM((list_len * BLOCK, 2 * HEAD_SIZE), jnp.bfloat16)],
         compiler_params=pltpu.CompilerParams(vmem_limit_bytes=48 * 1024 * 1024),
-    )(table, q_rows, g_rows, keys_all)
+    )(table, q_rows, g_rows, peer_q, peer_g, keys_all)
     out_items = out_rows.reshape(ulysses_width * segment_length, 1, head_width)
     qgrad_items = qgrad_rows.reshape(ulysses_width * segment_length, 1, head_width)
     attended_back, qgrad_back = (
@@ -207,10 +213,7 @@
     )
     attended = attended_back.reshape(segment_length, ulysses_width * head_width)
     query_grad = qgrad_back.reshape(segment_length, ulysses_width * head_width)
-    received = lax.ppermute(kv_grad_all[1], "core", [(0, 1), (1, 0)])
-    chip_part = (kv_grad_all[0] + received).reshape(
-        chip_count, ulysses_width * segment_length, 2 * HEAD_SIZE
-    )
+    chip_part = kv_grad_all.reshape(chip_count, ulysses_width * segment_length, 2 * HEAD_SIZE)
     owned = lax.psum_scatter(chip_part, "chip", scatter_dimension=0, tiled=True)
     result_tuple = lax.all_to_all(
         owned.reshape(ulysses_width * segment_length, 1, 2 * HEAD_SIZE),

time: 277 us -> 269 us (0.971)
  Pallas kernels: 26.9 us -> 45.1 us
  waiting for transfers between devices: 169 us -> 156 us
  other arithmetic: 12.1 us -> 2.11 us
    pallas_call x1, Pallas kernels: 26.9 us -> 45.1 us  [body(): pl.pallas_call(kernel, out_shape=(jax.ShapeDtypeStruct(q_rows.shape, jnp....]
    ppermute x1 -> x2, waiting for transfers between devices: 13.1 us -> 1.24 us  [body(): peer_q, peer_g = lax.ppermute((q_rows, g_rows), 'core', pair)]
    add x2, other arithmetic: 10.2 us -> 0.17 us  [item_table(): entries[:, :, None] * units_per_block]
    all_to_all x1, waiting for transfers between devices: 7.53 us -> 2.44 us  [body(): lax.all_to_all(qgrad_items, 'uly', split_axis=0, concat_axis=1, tiled=True)]
    all_to_all x1, waiting for transfers between devices: 2.45 us -> 7.38 us  [body(): lax.all_to_all(out_items, 'uly', split_axis=0, concat_axis=1, tiled=True)]
    squeeze x1 -> x0, local copies, waits for them, and re-layouts: 3.92 us -> none  [body(): received = lax.ppermute(kv_grad_all[1], 'core', [(0, 1), (1, 0)])]
    all_to_all x1, starting transfers between devices: 7.12 us -> 3.41 us  [body(): lax.all_to_all(qgrad_items, 'uly', split_axis=0, concat_axis=1, tiled=True)]
    all_to_all x1, starting transfers between devices: 3.41 us -> 6.69 us  [body(): lax.all_to_all(out_items, 'uly', split_axis=0, concat_axis=1, tiled=True)]
  transfers between devices with their start and end apart: 8 -> 9, of which waited for: 8 -> 8; matrix products, arithmetic and copies ran while one was open for 5% -> 6% of each run, Pallas kernels for 0% -> 0%
where the time goes in v6:
time: 269 us; the launch traced here: 268 us
  waiting for transfers between devices  156 us (58%)
  Pallas kernels  45.1 us (17%)
  starting transfers between devices  21.1 us (8%)
  local copies, waits for them, and re-layouts  15.6 us (6%)
  between operations  14.2 us (5%)
  blocking collectives  13.9 us (5%)
    reduce_scatter x1, waiting for transfers between devices, body(): owned = lax.psum_scatter(chip_part, 'chip', scatter_dimension=0, tiled=True)  79.6 us
    pallas_call x1, Pallas kernels, body(): pl.pallas_call(kernel, out_shape=(jax.ShapeDtypeStruct(q_rows.shape, jnp....  45.1 us
    all_gather x1, waiting for transfers between devices, body(): lax.all_gather(kv_mine[:, 0, :], ('chip', 'core'), axis=0, tiled=True)  41.6 us
    all_to_all x1, blocking collectives, body(): lax.all_to_all(kv_slots, 'uly', split_axis=1, concat_axis=0, tiled=True)  13.9 us
    all_to_all x1, waiting for transfers between devices, body(): lax.all_to_all(grad_slots, 'uly', split_axis=1, concat_axis=0, tiled=True)  10.5 us
    all_to_all x1, waiting for transfers between devices, body(): lax.all_to_all(owned.reshape(ulysses_width * segment_length, 1, 2 * HEAD_...  8.89 us
    all_to_all x1, waiting for transfers between devices, body(): lax.all_to_all(out_items, 'uly', split_axis=0, concat_axis=1, tiled=True)  7.38 us
    all_to_all x1, starting transfers between devices, body(): lax.all_to_all(out_items, 'uly', split_axis=0, concat_axis=1, tiled=True)  6.69 us
  transfers between devices with their start and end apart: 9, of which 8 were waited for; matrix products, arithmetic and copies ran while one was open for 6% of the time, Pallas kernels for 0%

profile of v6, /device:TPU:0, one launch (start us, length us, event | category | flops | bytes accessed | tf_op | source)
XLA Modules:
  0.0 267.6 jit_solution(2683241772986531639)
XLA Ops:
  7.2 0.8 reshape.302
  8.0 0.8 reshape.303
  8.8 0.1 pad_maximum_fusion
  8.9 13.9 %all_to_all.90 = bf16[64,8,256]{2,0,1:T(8,128)(2,1)} all-to-all(bf16[64,8,256]{2,0,1:T(8,128)(2,1)S(1)} %bitcast.77), channel_id=1, replica_groups=mesh['uly'=8,'chip'=16,'core'=2] {'uly'}, dimensions={1} | all-to-all | bytes 524288 | tf_op jit(solution)/shard_map/all_to_all | solution.py:137
  22.8 1.7 copy.101
  24.4 3.4 %all-to-all-start = ((bf16[64,8,256]{2,0,1:T(8,128)(2,1)}), bf16[64,8,256]{2,0,1:T(8,128)(2,1)S(1)}, u32[]{:S(2)}, u32[]{:S(2)}) async-start(bf16[64,8,256]{2,0,1:T(8,128)(2,1)} %bitcast.62), calls=%async_computation | async-start | bytes 524288 | tf_op jit(solution)/shard_map/all_to_all | solution.py:136
  27.9 0.8 copy.67
  28.7 0.6 gather_fusion.1
  29.3 0.1 copy.72
  29.4 0.6 gather_fusion
  30.1 0.1 copy.68
  30.1 0.1 and_reduce_fusion
  30.2 0.1 copy.74
  30.3 0.1 copy.70
  30.4 0.1 iota_add_fusion
  30.5 0.1 add.251
  30.7 0.1 iota_add_fusion.1
  30.7 0.1 add.245
  30.9 1.7 copy.100
  32.6 3.9 %all-to-all-done = bf16[64,8,256]{2,0,1:T(8,128)(2,1)S(1)} async-done(((bf16[64,8,256]{2,0,1:T(8,128)(2,1)}), bf16[64,8,256]{2,0,1:T(8,128)(2,1)S(1)}, u32[]{:S(2)}, u32[]{:S(2)}) %all-to-all-start) | async-done | bytes 262176 | tf_op jit(solution)/shard_map/all_to_all | solution.py:136
  36.5 3.4 %all-to-all-start.1 = ((bf16[64,8,256]{2,0,1:T(8,128)(2,1)}), bf16[64,8,256]{2,0,1:T(8,128)(2,1)S(1)}, u32[]{:S(2)}, u32[]{:S(2)}) async-start(bf16[64,8,256]{2,0,1:T(8,128)(2,1)} %bitcast.61), calls=%async_computation.1 | async-start | bytes 524288 | tf_op jit(solution)/shard_map/all_to_all | solution.py:138
  40.0 0.1 collective-permute-start
  40.1 10.5 %all-to-all-done.1 = bf16[64,8,256]{2,0,1:T(8,128)(2,1)S(1)} async-done(((bf16[64,8,256]{2,0,1:T(8,128)(2,1)}), bf16[64,8,256]{2,0,1:T(8,128)(2,1)S(1)}, u32[]{:S(2)}, u32[]{:S(2)}) %all-to-all-start.1) | async-done | bytes 262176 | tf_op jit(solution)/shard_map/all_to_all | solution.py:138
  50.7 0.1 select_n.172
  50.7 0.1 select_n.168
  50.9 0.1 concatenate.14.tab_ref
  50.9 1.2 collective-permute-done.1.pg_ref
  52.2 41.6 %all-gather.2.cloned.1.call-done.kv_ref = bf16[16384,256]{1,0:T(8,128)(2,1)} async-done(((bf16[512,256]{1,0:T(8,128)(2,1)}), bf16[16384,256]{1,0:T(8,128)(2,1)}) %all-gather.2.cloned.1.call-update) | async-done | bytes 8388624 | tf_op jit(solution)/shard_map/all_gather | solution.py:140
  93.7 45.1 %shard_map.84 = (bf16[512,256]{1,0:T(8,128)(2,1)S(1)}, bf16[512,256]{1,0:T(8,128)(2,1)S(1)}, f32[8192,256]{1,0:T(8,128)}) custom-call(s32[1312]{0:T(1024)S(1)} %concatenate.14.tab_ref, bf16[512,256]{1,0:T(8,128)(2,1)S(1)} %bitcast.67, bf16[512,256]{1,0:T(8,128)(2,1)S(1)} %bitcast.69, bf16[512,256]{1,0:T(8,128)(2,1)S(1)} %collective-permute-done.pq_ref, ...), custom_call_target="tpu_custom_call" | custom-call | tf_op jit(solution)/shard_map/pallas_call | solution.py:189
  138.9 0.5 broadcast.619
  139.4 0.8 reduce
  140.2 0.8 reshape.324
  141.0 6.7 %all-to-all-start.3 = ((bf16[8,2,8192]{2,1,0:T(2,128)(2,1)}), bf16[8,2,8192]{2,1,0:T(2,128)(2,1)S(1)}, u32[]{:S(2)}, u32[]{:S(2)}) async-start(bf16[8,2,8192]{2,1,0:T(2,128)(2,1)} %reshape.324), calls=%async_computation.3 | async-start | bytes 524288 | tf_op jit(solution)/shard_map/all_to_all | solution.py:211
  147.7 0.8 reduce.1
  148.5 0.8 reshape.326
  149.2 7.4 %all-to-all-done.3 = bf16[8,2,8192]{2,1,0:T(2,128)(2,1)S(1)} async-done(((bf16[8,2,8192]{2,1,0:T(2,128)(2,1)}), bf16[8,2,8192]{2,1,0:T(2,128)(2,1)S(1)}, u32[]{:S(2)}, u32[]{:S(2)}) %all-to-all-start.3) | async-done | bytes 262176 | tf_op jit(solution)/shard_map/all_to_all | solution.py:211
  156.6 3.4 %all-to-all-start.4 = ((bf16[8,2,8192]{2,1,0:T(2,128)(2,1)}), bf16[8,2,8192]{2,1,0:T(2,128)(2,1)S(1)}, u32[]{:S(2)}, u32[]{:S(2)}) async-start(bf16[8,2,8192]{2,1,0:T(2,128)(2,1)} %reshape.326), calls=%async_computation.4 | async-start | bytes 524288 | tf_op jit(solution)/shard_map/all_to_all | solution.py:212
  160.0 79.6 %reduce-scatter.2.cloned.1.call-done = f32[1,512,256]{2,1,0:T(8,128)} async-done(((f32[16,512,256]{2,1,0:T(8,128)}), f32[1,512,256]{2,1,0:T(8,128)}) %reduce-scatter.2.cloned.1.call-update) | async-done | bytes 524304 | tf_op jit(solution)/shard_map/reduce_scatter | solution.py:217
  239.6 2.4 copy.82
  242.0 2.4 all-to-all-done.4
  244.4 4.0 %all-to-all-start.5 = ((f32[512,1,256]{2,1,0:T(1,128)}), f32[512,1,256]{2,1,0:T(1,128)S(1)}, u32[]{:S(2)}, u32[]{:S(2)}) async-start(f32[512,1,256]{2,1,0:T(1,128)} %copy.82), calls=%async_computation.6 | async-start | bytes 1048576 | tf_op jit(solution)/shard_map/all_to_all | solution.py:218
  248.4 0.3 reshape.325
  248.7 0.7 copy.92
  249.4 0.3 reshape.327
  249.8 0.7 copy.93
  250.5 8.9 %all-to-all-done.5 = f32[512,1,256]{2,1,0:T(1,128)S(1)} async-done(((f32[512,1,256]{2,1,0:T(1,128)}), f32[512,1,256]{2,1,0:T(1,128)S(1)}, u32[]{:S(2)}, u32[]{:S(2)}) %all-to-all-start.5) | async-done | bytes 524320 | tf_op jit(solution)/shard_map/all_to_all | solution.py:218
  259.5 0.6 copy.102
  260.1 0.6 copy.103
  (22 shorter events, 0.4 us)
Async XLA Ops:
  7.2 86.6 %all-gather.2.cloned.1.call-start = ((), (), s32[]{:S(2)}) async-start(), calls=%async_computation.7 | async-start | bytes 8650752 | tf_op jit(solution)/shard_map/all_gather | solution.py:140
  24.4 12.1 %all-to-all-start = ((bf16[64,8,256]{2,0,1:T(8,128)(2,1)}), bf16[64,8,256]{2,0,1:T(8,128)(2,1)S(1)}, u32[]{:S(2)}, u32[]{:S(2)}) async-start(bf16[64,8,256]{2,0,1:T(8,128)(2,1)} %bitcast.62), calls=%async_computation | async-start | bytes 524288 | tf_op jit(solution)/shard_map/all_to_all | solution.py:136
  36.5 14.1 %all-to-all-start.1 = ((bf16[64,8,256]{2,0,1:T(8,128)(2,1)}), bf16[64,8,256]{2,0,1:T(8,128)(2,1)S(1)}, u32[]{:S(2)}, u32[]{:S(2)}) async-start(bf16[64,8,256]{2,0,1:T(8,128)(2,1)} %bitcast.61), calls=%async_computation.1 | async-start | bytes 524288 | tf_op jit(solution)/shard_map/all_to_all | solution.py:138
  39.9 199.7 %reduce-scatter.2.cloned.1.call-start = ((), (), s32[]{:S(2)}) async-start(), calls=%async_computation.8 | async-start | bytes 8912896 | tf_op jit(solution)/shard_map/reduce_scatter | solution.py:217
  40.0 10.9 %collective-permute-start = (bf16[512,256]{1,0:T(8,128)(2,1)S(1)}, bf16[512,256]{1,0:T(8,128)(2,1)S(1)}, u32[]{:S(2)}, u32[]{:S(2)}) collective-permute-start(bf16[512,256]{1,0:T(8,128)(2,1)S(1)} %bitcast.66), channel_id=1, source_target_pairs={{0,1},{1,0},{2,3},{3,2},{4,5},{5,4},{6,7},{7,6},{8,9},{9,8},{10,11... | collective-permute-start | bytes 786440 | tf_op jit(solution)/shard_map/ppermute | solution.py:179
  50.6 1.5 collective-permute-start.1
  141.0 15.7 %all-to-all-start.3 = ((bf16[8,2,8192]{2,1,0:T(2,128)(2,1)}), bf16[8,2,8192]{2,1,0:T(2,128)(2,1)S(1)}, u32[]{:S(2)}, u32[]{:S(2)}) async-start(bf16[8,2,8192]{2,1,0:T(2,128)(2,1)} %reshape.324), calls=%async_computation.3 | async-start | bytes 524288 | tf_op jit(solution)/shard_map/all_to_all | solution.py:211
  156.6 87.8 %all-to-all-start.4 = ((bf16[8,2,8192]{2,1,0:T(2,128)(2,1)}), bf16[8,2,8192]{2,1,0:T(2,128)(2,1)S(1)}, u32[]{:S(2)}, u32[]{:S(2)}) async-start(bf16[8,2,8192]{2,1,0:T(2,128)(2,1)} %reshape.326), calls=%async_computation.4 | async-start | bytes 524288 | tf_op jit(solution)/shard_map/all_to_all | solution.py:212
  244.4 14.9 %all-to-all-start.5 = ((f32[512,1,256]{2,1,0:T(1,128)}), f32[512,1,256]{2,1,0:T(1,128)S(1)}, u32[]{:S(2)}, u32[]{:S(2)}) async-start(f32[512,1,256]{2,1,0:T(1,128)} %copy.82), calls=%async_computation.6 | async-start | bytes 1048576 | tf_op jit(solution)/shard_map/all_to_all | solution.py:218
Sparse Core Ops, SparseCore 0:
  22.9 70.8 all-gather.1
  139.0 100.5 reduce-scatter.1

commit v7 on v6

--- a/solution.py
+++ b/solution.py
@@ -214,7 +214,9 @@
     attended = attended_back.reshape(segment_length, ulysses_width * head_width)
     query_grad = qgrad_back.reshape(segment_length, ulysses_width * head_width)
     chip_part = kv_grad_all.reshape(chip_count, ulysses_width * segment_length, 2 * HEAD_SIZE)
-    owned = lax.psum_scatter(chip_part, "chip", scatter_dimension=0, tiled=True)
+    owned = lax.all_to_all(chip_part, "chip", split_axis=0, concat_axis=0, tiled=True).sum(
+        axis=0, keepdims=True
+    )
     result_tuple = lax.all_to_all(
         owned.reshape(ulysses_width * segment_length, 1, 2 * HEAD_SIZE),
         "uly",

time: 269 us -> 390 us (1.45)
  the two profiles are of different devices: /device:TPU:0 before, /device:TPU:160 now
where the time goes in v7:
time: 390 us; the launch traced here: 389 us
  waiting for transfers between devices  257 us (66%)
  Pallas kernels  45.1 us (12%)
  blocking collectives  30.9 us (8%)
  starting transfers between devices  21.8 us (6%)
  between operations  14.2 us (4%)
  local copies, waits for them, and re-layouts  13.7 us (4%)
  other arithmetic  6.08 us (2%)
    all_to_all x1, waiting for transfers between devices, body(): lax.all_to_all(chip_part, 'chip', split_axis=0, concat_axis=0, tiled=True)  192 us
    pallas_call x1, Pallas kernels, body(): pl.pallas_call(kernel, out_shape=(jax.ShapeDtypeStruct(q_rows.shape, jnp....  45.1 us
    all_gather x1, waiting for transfers between devices, body(): lax.all_gather(kv_mine[:, 0, :], ('chip', 'core'), axis=0, tiled=True)  39.7 us
    all_to_all x1, blocking collectives, body(): lax.all_to_all(kv_slots, 'uly', split_axis=1, concat_axis=0, tiled=True)  15.6 us
    all_to_all x1, blocking collectives, body(): lax.all_to_all(out_items, 'uly', split_axis=0, concat_axis=1, tiled=True)  15.3 us
    all_to_all x1, waiting for transfers between devices, body(): lax.all_to_all(grad_slots, 'uly', split_axis=1, concat_axis=0, tiled=True)  8.51 us
    all_to_all x1, waiting for transfers between devices, body(): lax.all_to_all(owned.reshape(ulysses_width * segment_length, 1, 2 * HEAD_...  7.84 us
  transfers between devices with their start and end apart: 8, of which 7 were waited for; matrix products, arithmetic and copies ran while one was open for 4% of the time, Pallas kernels for 0%

profile of v7, /device:TPU:160, one launch (start us, length us, event | category | flops | bytes accessed | tf_op | source)
XLA Modules:
  0.0 389.0 jit_solution(2804742516337694648)
XLA Ops:
  7.2 0.8 reshape.299
  8.0 0.8 reshape.300
  8.8 0.1 pad_maximum_fusion
  8.9 15.6 %all_to_all.95 = bf16[64,8,256]{2,0,1:T(8,128)(2,1)} all-to-all(bf16[64,8,256]{2,0,1:T(8,128)(2,1)S(1)} %bitcast.76), channel_id=1, replica_groups=mesh['uly'=8,'chip'=16,'core'=2] {'uly'}, dimensions={1} | all-to-all | bytes 524288 | tf_op jit(solution)/shard_map/all_to_all | solution.py:137
  24.5 1.7 copy.101
  26.1 3.4 all-to-all-start
  29.6 0.8 copy.68
  30.4 0.6 gather_fusion.1
  31.0 0.1 copy.73
  31.1 0.6 gather_fusion
  31.8 0.1 copy.69
  31.8 0.1 and_reduce_fusion
  31.9 0.1 copy.75
  32.0 0.1 copy.71
  32.1 0.1 iota_add_fusion
  32.2 0.1 add.249
  32.4 0.1 iota_add_fusion.1
  32.5 0.1 add.243
  32.6 1.7 copy.100
  34.3 3.9 %all-to-all-done = bf16[64,8,256]{2,0,1:T(8,128)(2,1)S(1)} async-done(((bf16[64,8,256]{2,0,1:T(8,128)(2,1)}), bf16[64,8,256]{2,0,1:T(8,128)(2,1)S(1)}, u32[]{:S(2)}, u32[]{:S(2)}) %all-to-all-start) | async-done | bytes 262176 | tf_op jit(solution)/shard_map/all_to_all | solution.py:136
  38.2 3.4 all-to-all-start.1
  41.7 0.1 collective-permute-start
  41.8 8.5 %all-to-all-done.1 = bf16[64,8,256]{2,0,1:T(8,128)(2,1)S(1)} async-done(((bf16[64,8,256]{2,0,1:T(8,128)(2,1)}), bf16[64,8,256]{2,0,1:T(8,128)(2,1)S(1)}, u32[]{:S(2)}, u32[]{:S(2)}) %all-to-all-start.1) | async-done | bytes 262176 | tf_op jit(solution)/shard_map/all_to_all | solution.py:138
  50.3 0.1 select_n.172
  50.4 0.1 select_n.168
  50.5 0.1 concatenate.14.tab_ref
  50.6 1.2 collective-permute-done.1.pg_ref
  51.8 39.7 %all-gather.2.cloned.1.call-done.kv_ref = bf16[16384,256]{1,0:T(8,128)(2,1)} async-done(((bf16[512,256]{1,0:T(8,128)(2,1)}), bf16[16384,256]{1,0:T(8,128)(2,1)}) %all-gather.2.cloned.1.call-update) | async-done | bytes 8388624 | tf_op jit(solution)/shard_map/all_gather | solution.py:140
  91.5 45.1 %shard_map.84 = (bf16[512,256]{1,0:T(8,128)(2,1)S(1)}, bf16[512,256]{1,0:T(8,128)(2,1)S(1)}, f32[8192,256]{1,0:T(8,128)}) custom-call(s32[1312]{0:T(1024)S(1)} %concatenate.14.tab_ref, bf16[512,256]{1,0:T(8,128)(2,1)S(1)} %bitcast.66, bf16[512,256]{1,0:T(8,128)(2,1)S(1)} %bitcast.68, bf16[512,256]{1,0:T(8,128)(2,1)S(1)} %collective-permute-done.pq_ref, ...), custom_call_target="tpu_custom_call" | custom-call | tf_op jit(solution)/shard_map/pallas_call | solution.py:189
  136.6 0.5 broadcast.619
  137.1 0.8 reduce
  138.0 15.3 %all_to_all.96 = bf16[8,2,8192]{2,1,0:T(2,128)(2,1)S(1)} all-to-all(bf16[8,2,8192]{2,1,0:T(2,128)(2,1)S(1)} %reshape.320), channel_id=1, replica_groups=mesh['uly'=8,'chip'=16,'core'=2] {'uly'}, dimensions={0} | all-to-all | bytes 524288 | tf_op jit(solution)/shard_map/all_to_all | solution.py:211
  153.4 7.4 %all-to-all-start.5 = ((f32[16,512,256]{2,1,0:T(8,128)}), f32[16,512,256]{2,1,0:T(8,128)}, u32[]{:S(2)}, u32[]{:S(2)}) async-start(f32[16,512,256]{2,1,0:T(8,128)} %bitcast.71), calls=%async_computation.5 | async-start | bytes 16777216 | tf_op jit(solution)/shard_map/all_to_all | solution.py:217
  160.7 0.8 reduce.1
  161.6 0.8 reshape.322
  162.3 192.4 %all-to-all-done.5 = f32[16,512,256]{2,1,0:T(8,128)} async-done(((f32[16,512,256]{2,1,0:T(8,128)}), f32[16,512,256]{2,1,0:T(8,128)}, u32[]{:S(2)}, u32[]{:S(2)}) %all-to-all-start.5) | async-done | bytes 8388640 | tf_op jit(solution)/shard_map/all_to_all | solution.py:217
  354.7 3.8 all-to-all-start.4
  358.6 4.0 %reduce_sum.18 = f32[512,256]{1,0:T(8,128)S(1)} reduce(f32[16,512,256]{2,1,0:T(8,128)} %all-to-all-done.5, f32[]{:T(128)} %constant.154.clone.1), dimensions={0}, to_apply=%region_2.3 | reduce | flops 1966080 | bytes 8912900 | tf_op jit(solution)/shard_map/reduce_sum | solution.py:217
  362.6 1.2 reshape_broadcast_in_dim.3
  363.7 3.6 all-to-all-done.4
  367.3 3.6 all-to-all-start.6
  370.9 0.3 reshape.321
  371.2 0.7 copy.92
  372.0 0.3 reshape.323
  372.3 0.7 copy.93
  373.0 7.8 %all-to-all-done.6 = f32[512,1,256]{2,1,0:T(1,128)S(1)} async-done(((f32[512,1,256]{2,1,0:T(1,128)}), f32[512,1,256]{2,1,0:T(1,128)S(1)}, u32[]{:S(2)}, u32[]{:S(2)}) %all-to-all-start.6) | async-done | bytes 524320 | tf_op jit(solution)/shard_map/all_to_all | solution.py:220
  380.9 0.6 copy.102
  381.6 0.6 copy.103
  (21 shorter events, 0.4 us)
Async XLA Ops:
  7.2 84.4 %all-gather.2.cloned.1.call-start = ((), (), s32[]{:S(2)}) async-start(), calls=%async_computation.7 | async-start | bytes 8650752 | tf_op jit(solution)/shard_map/all_gather | solution.py:140
  26.1 12.1 %all-to-all-start = ((bf16[64,8,256]{2,0,1:T(8,128)(2,1)}), bf16[64,8,256]{2,0,1:T(8,128)(2,1)S(1)}, u32[]{:S(2)}, u32[]{:S(2)}) async-start(bf16[64,8,256]{2,0,1:T(8,128)(2,1)} %bitcast.61), calls=%async_computation | async-start | bytes 524288 | tf_op jit(solution)/shard_map/all_to_all | solution.py:136
  38.2 12.1 %all-to-all-start.1 = ((bf16[64,8,256]{2,0,1:T(8,128)(2,1)}), bf16[64,8,256]{2,0,1:T(8,128)(2,1)S(1)}, u32[]{:S(2)}, u32[]{:S(2)}) async-start(bf16[64,8,256]{2,0,1:T(8,128)(2,1)} %bitcast.60), calls=%async_computation.1 | async-start | bytes 524288 | tf_op jit(solution)/shard_map/all_to_all | solution.py:138
  41.7 8.9 %collective-permute-start = (bf16[512,256]{1,0:T(8,128)(2,1)S(1)}, bf16[512,256]{1,0:T(8,128)(2,1)S(1)}, u32[]{:S(2)}, u32[]{:S(2)}) collective-permute-start(bf16[512,256]{1,0:T(8,128)(2,1)S(1)} %bitcast.65), channel_id=1, source_target_pairs={{0,1},{1,0},{2,3},{3,2},{4,5},{5,4},{6,7},{7,6},{8,9},{9,8},{10,11... | collective-permute-start | bytes 786440 | tf_op jit(solution)/shard_map/ppermute | solution.py:179
  50.3 1.5 collective-permute-start.1
  153.4 201.4 %all-to-all-start.5 = ((f32[16,512,256]{2,1,0:T(8,128)}), f32[16,512,256]{2,1,0:T(8,128)}, u32[]{:S(2)}, u32[]{:S(2)}) async-start(f32[16,512,256]{2,1,0:T(8,128)} %bitcast.71), calls=%async_computation.5 | async-start | bytes 16777216 | tf_op jit(solution)/shard_map/all_to_all | solution.py:217
  354.7 12.6 %all-to-all-start.4 = ((bf16[8,2,8192]{2,1,0:T(2,128)(2,1)}), bf16[8,2,8192]{2,1,0:T(2,128)(2,1)S(1)}, u32[]{:S(2)}, u32[]{:S(2)}) async-start(bf16[8,2,8192]{2,1,0:T(2,128)(2,1)} %reshape.322), calls=%async_computation.4 | async-start | bytes 524288 | tf_op jit(solution)/shard_map/all_to_all | solution.py:212
  367.3 13.5 %all-to-all-start.6 = ((f32[512,1,256]{2,1,0:T(1,128)}), f32[512,1,256]{2,1,0:T(1,128)S(1)}, u32[]{:S(2)}, u32[]{:S(2)}) async-start(f32[512,1,256]{2,1,0:T(1,128)} %reshape_broadcast_in_dim.3), calls=%async_computation.6 | async-start | bytes 1048576 | tf_op jit(solution)/shard_map/all_to_all | solution.py:220
Sparse Core Ops, SparseCore 0:
  24.6 66.8 all-gather.1

commit v8 on v6

--- a/solution.py
+++ b/solution.py
@@ -14,7 +14,7 @@
 
 
 def attention_kernel(
-    tab_ref, q_ref, g_ref, pq_ref, pg_ref, kv_ref, out_ref, dq_ref, dkv_ref, kvg_ref,
+    tab_ref, q_ref, g_ref, pq_ref, pg_ref, kv_hbm, out_ref, dq_ref, dkv_ref, kvg_ref, sem,
     *, heads_dev, slots, seg_len, list_len, units_per_block, score_scale,
 ):
     dkv_ref[...] = jnp.zeros(dkv_ref.shape, jnp.float32)
@@ -30,12 +30,33 @@
     nt = (((1,), (1,)), ((), ()))
     tn = (((0,), (0,)), ((), ()))
     sources = ((q_ref, g_ref, True), (pq_ref, pg_ref, False))
+
+    def fetch(item, buf):
+        for j in range(list_len):
+            for u in range(units_per_block):
+                src = tab_ref[rows_at + (item * list_len + j) * units_per_block + u]
+                pltpu.make_async_copy(
+                    kv_hbm.at[pl.ds(pl.multiple_of(src, seg_len), seg_len)],
+                    kvg_ref.at[buf, pl.ds(j * BLOCK + u * seg_len, seg_len)],
+                    sem.at[buf],
+                ).start()
+
+    def wait_all(buf):
+        pltpu.make_async_copy(kv_hbm.at[pl.ds(0, key_len)], kvg_ref.at[buf], sem.at[buf]).wait()
+
+    fetch(0, 0)
     for source, (sq_ref, sg_ref, own) in enumerate(sources):
       for head in range(heads_dev):
         cols = slice(head * HEAD_SIZE, (head + 1) * HEAD_SIZE)
 
         def item_step(slot, carry, head=head, cols=cols, source=source, sq_ref=sq_ref, sg_ref=sg_ref, own=own):
             item = (source * heads_dev + head) * slots + slot
+            buf = item % 2
+            wait_all(buf)
+
+            @pl.when(item + 1 < n_items)
+            def _():
+                fetch(item + 1, 1 - buf)
             rows = pl.ds(pl.multiple_of(slot * seg_len, seg_len), seg_len)
             query_block = sq_ref[rows, cols]
             grad_block = sg_ref[rows, cols]
@@ -43,16 +64,11 @@
             base = jnp.zeros((1, key_len), jnp.int32)
             for j in range(list_len):
                 base = jnp.where(lane_block == j, tab_ref[base_at + item * list_len + j], base)
-                for u in range(units_per_block):
-                    src = tab_ref[rows_at + (item * list_len + j) * units_per_block + u]
-                    kvg_ref[pl.ds(j * BLOCK + u * seg_len, seg_len), :] = kv_ref[
-                        pl.ds(pl.multiple_of(src, seg_len), seg_len), :
-                    ]
             key_pos = base + lane_offset
             query_pos = tab_ref[item] + query_offset
             allowed = key_pos <= query_pos
-            key_group = kvg_ref[:, :HEAD_SIZE]
-            value_group = kvg_ref[:, HEAD_SIZE:]
+            key_group = kvg_ref[buf, :, :HEAD_SIZE]
+            value_group = kvg_ref[buf, :, HEAD_SIZE:]
             scores = (
                 lax.dot_general(query_block, key_group, nt, preferred_element_type=jnp.float32)
                 * score_scale
@@ -196,13 +212,17 @@
             ),
         ),
         in_specs=[pl.BlockSpec(memory_space=pltpu.SMEM)]
-        + [pl.BlockSpec(memory_space=pltpu.VMEM)] * 5,
+        + [pl.BlockSpec(memory_space=pltpu.VMEM)] * 4
+        + [pl.BlockSpec(memory_space=pl.ANY)],
         out_specs=(
             pl.BlockSpec(memory_space=pltpu.VMEM),
             pl.BlockSpec(memory_space=pltpu.VMEM),
             pl.BlockSpec(memory_space=pltpu.VMEM),
         ),
-        scratch_shapes=[pltpu.VMEM((list_len * BLOCK, 2 * HEAD_SIZE), jnp.bfloat16)],
+        scratch_shapes=[
+            pltpu.VMEM((2, list_len * BLOCK, 2 * HEAD_SIZE), jnp.bfloat16),
+            pltpu.SemaphoreType.DMA((2,)),
+        ],
         compiler_params=pltpu.CompilerParams(vmem_limit_bytes=48 * 1024 * 1024),
     )(table, q_rows, g_rows, peer_q, peer_g, keys_all)
     out_items = out_rows.reshape(ulysses_width * segment_length, 1, head_width)

time: 269 us -> 270 us (level)
  no operation moved by 1% of the time
where the time goes in v8:
time: 270 us; the launch traced here: 266 us
  waiting for transfers between devices  155 us (57%)
  Pallas kernels  44.1 us (16%)
  starting transfers between devices  20.8 us (8%)
  local copies, waits for them, and re-layouts  15.6 us (6%)
  between operations  14.2 us (5%)
  blocking collectives  13.9 us (5%)
    reduce_scatter x1, waiting for transfers between devices, body(): owned = lax.psum_scatter(chip_part, 'chip', scatter_dimension=0, tiled=True)  79.5 us
    pallas_call x1, Pallas kernels, body(): pl.pallas_call(kernel, out_shape=(jax.ShapeDtypeStruct(q_rows.shape, jnp....  44.1 us
    all_gather x1, waiting for transfers between devices, body(): lax.all_gather(kv_mine[:, 0, :], ('chip', 'core'), axis=0, tiled=True)  41.6 us
    all_to_all x1, blocking collectives, body(): lax.all_to_all(kv_slots, 'uly', split_axis=1, concat_axis=0, tiled=True)  13.9 us
    all_to_all x1, waiting for transfers between devices, body(): lax.all_to_all(grad_slots, 'uly', split_axis=1, concat_axis=0, tiled=True)  10.5 us
    all_to_all x1, waiting for transfers between devices, body(): lax.all_to_all(owned.reshape(ulysses_width * segment_length, 1, 2 * HEAD_...  8.89 us
    all_to_all x1, waiting for transfers between devices, body(): lax.all_to_all(out_items, 'uly', split_axis=0, concat_axis=1, tiled=True)  7.39 us
    all_to_all x1, starting transfers between devices, body(): lax.all_to_all(out_items, 'uly', split_axis=0, concat_axis=1, tiled=True)  6.44 us
  transfers between devices with their start and end apart: 9, of which 8 were waited for; matrix products, arithmetic and copies ran while one was open for 6% of the time, Pallas kernels for 0%

profile of v8, /device:TPU:0, one launch (start us, length us, event | category | flops | bytes accessed | tf_op | source)
XLA Modules:
  0.0 266.2 jit_solution(2938401544525189828)
XLA Ops:
  7.2 0.8 reshape.302
  8.0 0.8 reshape.303
  8.8 0.1 pad_maximum_fusion
  8.9 13.9 %all_to_all.90 = bf16[64,8,256]{2,0,1:T(8,128)(2,1)} all-to-all(bf16[64,8,256]{2,0,1:T(8,128)(2,1)S(1)} %bitcast.77), channel_id=1, replica_groups=mesh['uly'=8,'chip'=16,'core'=2] {'uly'}, dimensions={1} | all-to-all | bytes 524288 | tf_op jit(solution)/shard_map/all_to_all | solution.py:153
  22.8 1.7 copy.101
  24.4 3.4 %all-to-all-start = ((bf16[64,8,256]{2,0,1:T(8,128)(2,1)}), bf16[64,8,256]{2,0,1:T(8,128)(2,1)S(1)}, u32[]{:S(2)}, u32[]{:S(2)}) async-start(bf16[64,8,256]{2,0,1:T(8,128)(2,1)} %bitcast.62), calls=%async_computation | async-start | bytes 524288 | tf_op jit(solution)/shard_map/all_to_all | solution.py:152
  27.9 0.8 copy.67
  28.7 0.6 gather_fusion.1
  29.3 0.1 copy.72
  29.4 0.6 gather_fusion
  30.1 0.1 copy.68
  30.1 0.1 and_reduce_fusion
  30.2 0.1 copy.74
  30.3 0.1 copy.70
  30.4 0.1 iota_add_fusion
  30.5 0.1 add.251
  30.7 0.1 iota_add_fusion.1
  30.7 0.1 add.245
  30.9 1.7 copy.100
  32.6 3.9 %all-to-all-done = bf16[64,8,256]{2,0,1:T(8,128)(2,1)S(1)} async-done(((bf16[64,8,256]{2,0,1:T(8,128)(2,1)}), bf16[64,8,256]{2,0,1:T(8,128)(2,1)S(1)}, u32[]{:S(2)}, u32[]{:S(2)}) %all-to-all-start) | async-done | bytes 262176 | tf_op jit(solution)/shard_map/all_to_all | solution.py:152
  36.5 3.4 %all-to-all-start.1 = ((bf16[64,8,256]{2,0,1:T(8,128)(2,1)}), bf16[64,8,256]{2,0,1:T(8,128)(2,1)S(1)}, u32[]{:S(2)}, u32[]{:S(2)}) async-start(bf16[64,8,256]{2,0,1:T(8,128)(2,1)} %bitcast.61), calls=%async_computation.1 | async-start | bytes 524288 | tf_op jit(solution)/shard_map/all_to_all | solution.py:154
  40.0 0.1 collective-permute-start
  40.1 10.5 %all-to-all-done.1 = bf16[64,8,256]{2,0,1:T(8,128)(2,1)S(1)} async-done(((bf16[64,8,256]{2,0,1:T(8,128)(2,1)}), bf16[64,8,256]{2,0,1:T(8,128)(2,1)S(1)}, u32[]{:S(2)}, u32[]{:S(2)}) %all-to-all-start.1) | async-done | bytes 262176 | tf_op jit(solution)/shard_map/all_to_all | solution.py:154
  50.7 0.1 select_n.172
  50.7 0.1 select_n.168
  50.9 0.1 concatenate.14.tab_ref
  50.9 1.2 collective-permute-done.1.pg_ref
  52.2 41.6 %all-gather.2.cloned.1.call-done.kv_hbm = bf16[16384,256]{1,0:T(8,128)(2,1)} async-done(((bf16[512,256]{1,0:T(8,128)(2,1)}), bf16[16384,256]{1,0:T(8,128)(2,1)}) %all-gather.2.cloned.1.call-update) | async-done | bytes 8388624 | tf_op jit(solution)/shard_map/all_gather | solution.py:156
  93.7 44.1 %shard_map.84 = (bf16[512,256]{1,0:T(8,128)(2,1)S(1)}, bf16[512,256]{1,0:T(8,128)(2,1)S(1)}, f32[8192,256]{1,0:T(8,128)}) custom-call(s32[1312]{0:T(1024)S(1)} %concatenate.14.tab_ref, bf16[512,256]{1,0:T(8,128)(2,1)S(1)} %bitcast.67, bf16[512,256]{1,0:T(8,128)(2,1)S(1)} %bitcast.69, bf16[512,256]{1,0:T(8,128)(2,1)S(1)} %collective-permute-done.pq_ref, ...), custom_call_target="tpu_custom_call" | custom-call | tf_op jit(solution)/shard_map/pallas_call | solution.py:205
  137.9 0.5 broadcast.619
  138.4 0.8 reduce
  139.2 0.8 reshape.324
  140.0 6.4 %all-to-all-start.3 = ((bf16[8,2,8192]{2,1,0:T(2,128)(2,1)}), bf16[8,2,8192]{2,1,0:T(2,128)(2,1)S(1)}, u32[]{:S(2)}, u32[]{:S(2)}) async-start(bf16[8,2,8192]{2,1,0:T(2,128)(2,1)} %reshape.324), calls=%async_computation.3 | async-start | bytes 524288 | tf_op jit(solution)/shard_map/all_to_all | solution.py:231
  146.4 0.8 reduce.1
  147.2 0.8 reshape.326
  148.0 7.4 %all-to-all-done.3 = bf16[8,2,8192]{2,1,0:T(2,128)(2,1)S(1)} async-done(((bf16[8,2,8192]{2,1,0:T(2,128)(2,1)}), bf16[8,2,8192]{2,1,0:T(2,128)(2,1)S(1)}, u32[]{:S(2)}, u32[]{:S(2)}) %all-to-all-start.3) | async-done | bytes 262176 | tf_op jit(solution)/shard_map/all_to_all | solution.py:231
  155.4 3.4 %all-to-all-start.4 = ((bf16[8,2,8192]{2,1,0:T(2,128)(2,1)}), bf16[8,2,8192]{2,1,0:T(2,128)(2,1)S(1)}, u32[]{:S(2)}, u32[]{:S(2)}) async-start(bf16[8,2,8192]{2,1,0:T(2,128)(2,1)} %reshape.326), calls=%async_computation.4 | async-start | bytes 524288 | tf_op jit(solution)/shard_map/all_to_all | solution.py:232
  158.8 79.5 %reduce-scatter.2.cloned.1.call-done = f32[1,512,256]{2,1,0:T(8,128)} async-done(((f32[16,512,256]{2,1,0:T(8,128)}), f32[1,512,256]{2,1,0:T(8,128)}) %reduce-scatter.2.cloned.1.call-update) | async-done | bytes 524304 | tf_op jit(solution)/shard_map/reduce_scatter | solution.py:237
  238.3 2.4 copy.82
  240.6 2.4 all-to-all-done.4
  243.1 4.0 %all-to-all-start.5 = ((f32[512,1,256]{2,1,0:T(1,128)}), f32[512,1,256]{2,1,0:T(1,128)S(1)}, u32[]{:S(2)}, u32[]{:S(2)}) async-start(f32[512,1,256]{2,1,0:T(1,128)} %copy.82), calls=%async_computation.6 | async-start | bytes 1048576 | tf_op jit(solution)/shard_map/all_to_all | solution.py:238
  247.0 0.3 reshape.325
  247.4 0.7 copy.92
  248.1 0.3 reshape.327
  248.4 0.7 copy.93
  249.1 8.9 %all-to-all-done.5 = f32[512,1,256]{2,1,0:T(1,128)S(1)} async-done(((f32[512,1,256]{2,1,0:T(1,128)}), f32[512,1,256]{2,1,0:T(1,128)S(1)}, u32[]{:S(2)}, u32[]{:S(2)}) %all-to-all-start.5) | async-done | bytes 524320 | tf_op jit(solution)/shard_map/all_to_all | solution.py:238
  258.1 0.6 copy.102
  258.7 0.6 copy.103
  (22 shorter events, 0.4 us)
Async XLA Ops:
  7.2 86.6 %all-gather.2.cloned.1.call-start = ((), (), s32[]{:S(2)}) async-start(), calls=%async_computation.7 | async-start | bytes 8650752 | tf_op jit(solution)/shard_map/all_gather | solution.py:156
  24.4 12.1 %all-to-all-start = ((bf16[64,8,256]{2,0,1:T(8,128)(2,1)}), bf16[64,8,256]{2,0,1:T(8,128)(2,1)S(1)}, u32[]{:S(2)}, u32[]{:S(2)}) async-start(bf16[64,8,256]{2,0,1:T(8,128)(2,1)} %bitcast.62), calls=%async_computation | async-start | bytes 524288 | tf_op jit(solution)/shard_map/all_to_all | solution.py:152
  36.5 14.1 %all-to-all-start.1 = ((bf16[64,8,256]{2,0,1:T(8,128)(2,1)}), bf16[64,8,256]{2,0,1:T(8,128)(2,1)S(1)}, u32[]{:S(2)}, u32[]{:S(2)}) async-start(bf16[64,8,256]{2,0,1:T(8,128)(2,1)} %bitcast.61), calls=%async_computation.1 | async-start | bytes 524288 | tf_op jit(solution)/shard_map/all_to_all | solution.py:154
  39.9 198.3 %reduce-scatter.2.cloned.1.call-start = ((), (), s32[]{:S(2)}) async-start(), calls=%async_computation.8 | async-start | bytes 8912896 | tf_op jit(solution)/shard_map/reduce_scatter | solution.py:237
  40.0 10.9 %collective-permute-start = (bf16[512,256]{1,0:T(8,128)(2,1)S(1)}, bf16[512,256]{1,0:T(8,128)(2,1)S(1)}, u32[]{:S(2)}, u32[]{:S(2)}) collective-permute-start(bf16[512,256]{1,0:T(8,128)(2,1)S(1)} %bitcast.66), channel_id=1, source_target_pairs={{0,1},{1,0},{2,3},{3,2},{4,5},{5,4},{6,7},{7,6},{8,9},{9,8},{10,11... | collective-permute-start | bytes 786440 | tf_op jit(solution)/shard_map/ppermute | solution.py:195
  50.6 1.5 collective-permute-start.1
  140.0 15.4 %all-to-all-start.3 = ((bf16[8,2,8192]{2,1,0:T(2,128)(2,1)}), bf16[8,2,8192]{2,1,0:T(2,128)(2,1)S(1)}, u32[]{:S(2)}, u32[]{:S(2)}) async-start(bf16[8,2,8192]{2,1,0:T(2,128)(2,1)} %reshape.324), calls=%async_computation.3 | async-start | bytes 524288 | tf_op jit(solution)/shard_map/all_to_all | solution.py:231
  155.4 87.7 %all-to-all-start.4 = ((bf16[8,2,8192]{2,1,0:T(2,128)(2,1)}), bf16[8,2,8192]{2,1,0:T(2,128)(2,1)S(1)}, u32[]{:S(2)}, u32[]{:S(2)}) async-start(bf16[8,2,8192]{2,1,0:T(2,128)(2,1)} %reshape.326), calls=%async_computation.4 | async-start | bytes 524288 | tf_op jit(solution)/shard_map/all_to_all | solution.py:232
  243.1 14.9 %all-to-all-start.5 = ((f32[512,1,256]{2,1,0:T(1,128)}), f32[512,1,256]{2,1,0:T(1,128)S(1)}, u32[]{:S(2)}, u32[]{:S(2)}) async-start(f32[512,1,256]{2,1,0:T(1,128)} %copy.82), calls=%async_computation.6 | async-start | bytes 1048576 | tf_op jit(solution)/shard_map/all_to_all | solution.py:238
Sparse Core Ops, SparseCore 0:
  22.9 70.8 all-gather.1
  138.0 100.2 reduce-scatter.1

commit v9 on v6

--- a/solution.py
+++ b/solution.py
@@ -215,16 +215,18 @@
     query_grad = qgrad_back.reshape(segment_length, ulysses_width * head_width)
     chip_part = kv_grad_all.reshape(chip_count, ulysses_width * segment_length, 2 * HEAD_SIZE)
     owned = lax.psum_scatter(chip_part, "chip", scatter_dimension=0, tiled=True)
-    result_tuple = lax.all_to_all(
-        owned.reshape(ulysses_width * segment_length, 1, 2 * HEAD_SIZE),
+    by_source = lax.all_to_all(
+        owned.reshape(ulysses_width, segment_length, 2 * HEAD_SIZE),
         "uly",
         split_axis=0,
-        concat_axis=1,
+        concat_axis=0,
         tiled=True,
     )
-    summed_total = result_tuple.reshape(
-        segment_length, KEY_VALUE_HEADS, copy_count, 2 * HEAD_SIZE
-    ).sum(axis=2)
+    summed_total = (
+        by_source.reshape(KEY_VALUE_HEADS, copy_count, segment_length, 2 * HEAD_SIZE)
+        .sum(axis=1)
+        .transpose(1, 0, 2)
+    )
     gradient_keys = (
         summed_total[:, :, :HEAD_SIZE]
         .reshape(segment_length, KEY_VALUE_HEADS * HEAD_SIZE)

time: 269 us -> 269 us (level)
  blocking collectives: 13.9 us -> 102 us
  waiting for transfers between devices: 156 us -> 74.3 us
  starting transfers between devices: 21.1 us -> 17.2 us
  local copies, waits for them, and re-layouts: 15.6 us -> 12.5 us
    all_to_all x0 -> x1, blocking collectives: none -> 87.8 us  [body(): lax.all_to_all(qgrad_items, 'uly', split_axis=0, concat_axis=1, tiled=True)]
    reduce_scatter x1, waiting for transfers between devices: 79.6 us -> 0.01 us  [body(): owned = lax.psum_scatter(chip_part, 'chip', scatter_dimension=0, tiled=True)]
    all_to_all x2 -> x1, starting transfers between devices: 7.39 us -> 3.49 us  [body(): lax.all_to_all(owned.reshape(ulysses_width, segment_length, 2 * HEAD_SIZE...]
    all_to_all x2 -> x1, waiting for transfers between devices: 11.3 us -> 8.91 us  [body(): lax.all_to_all(owned.reshape(ulysses_width, segment_length, 2 * HEAD_SIZE...]
  transfers between devices with their start and end apart: 9 -> 8, of which waited for: 8 -> 6; matrix products, arithmetic and copies ran while one was open for 6% -> 4% of each run, Pallas kernels for 0% -> 0%
where the time goes in v9:
time: 269 us; the launch traced here: 267 us
  blocking collectives  102 us (38%)
  waiting for transfers between devices  74.3 us (28%)
  Pallas kernels  45.1 us (17%)
  starting transfers between devices  17.2 us (6%)
  between operations  14.2 us (5%)
  local copies, waits for them, and re-layouts  12.5 us (5%)
    all_to_all x1, blocking collectives, body(): lax.all_to_all(qgrad_items, 'uly', split_axis=0, concat_axis=1, tiled=True)  87.8 us
    pallas_call x1, Pallas kernels, body(): pl.pallas_call(kernel, out_shape=(jax.ShapeDtypeStruct(q_rows.shape, jnp....  45.1 us
    all_gather x1, waiting for transfers between devices, body(): lax.all_gather(kv_mine[:, 0, :], ('chip', 'core'), axis=0, tiled=True)  41.6 us
    all_to_all x1, blocking collectives, body(): lax.all_to_all(kv_slots, 'uly', split_axis=1, concat_axis=0, tiled=True)  13.9 us
    all_to_all x1, waiting for transfers between devices, body(): lax.all_to_all(grad_slots, 'uly', split_axis=1, concat_axis=0, tiled=True)  10.5 us
    all_to_all x1, waiting for transfers between devices, body(): lax.all_to_all(owned.reshape(ulysses_width, segment_length, 2 * HEAD_SIZE...  8.91 us
    all_to_all x1, waiting for transfers between devices, body(): lax.all_to_all(out_items, 'uly', split_axis=0, concat_axis=1, tiled=True)  8.07 us
    all_to_all x1, starting transfers between devices, body(): lax.all_to_all(out_items, 'uly', split_axis=0, concat_axis=1, tiled=True)  6.69 us
  transfers between devices with their start and end apart: 8, of which 6 were waited for; matrix products, arithmetic and copies ran while one was open for 4% of the time, Pallas kernels for 0%

profile of v9, /device:TPU:0, one launch (start us, length us, event | category | flops | bytes accessed | tf_op | source)
XLA Modules:
  0.0 267.1 jit_solution(5470121067275118377)
XLA Ops:
  7.2 0.0 all-gather.2.cloned.1.call-start
  7.2 0.8 reshape.301
  8.0 0.8 reshape.302
  8.8 0.1 pad_maximum_fusion
  8.9 13.9 %all_to_all.80 = bf16[64,8,256]{2,0,1:T(8,128)(2,1)} all-to-all(bf16[64,8,256]{2,0,1:T(8,128)(2,1)S(1)} %bitcast.74), channel_id=1, replica_groups=mesh['uly'=8,'chip'=16,'core'=2] {'uly'}, dimensions={1} | all-to-all | bytes 524288 | tf_op jit(solution)/shard_map/all_to_all | solution.py:137
  22.7 0.0 all-gather.2.cloned.1.call-update
  22.8 1.7 copy.84
  24.4 3.4 %all-to-all-start = ((bf16[64,8,256]{2,0,1:T(8,128)(2,1)}), bf16[64,8,256]{2,0,1:T(8,128)(2,1)S(1)}, u32[]{:S(2)}, u32[]{:S(2)}) async-start(bf16[64,8,256]{2,0,1:T(8,128)(2,1)} %bitcast.62), calls=%async_computation | async-start | bytes 524288 | tf_op jit(solution)/shard_map/all_to_all | solution.py:136
  27.9 0.8 copy.52
  28.7 0.6 gather_fusion.1
  29.3 0.1 copy.57
  29.4 0.6 gather_fusion
  30.1 0.1 copy.53
  30.1 0.1 and_reduce_fusion
  30.2 0.1 copy.59
  30.3 0.1 copy.55
  30.4 0.1 iota_add_fusion
  30.5 0.1 add.251
  30.7 0.1 iota_add_fusion.1
  30.7 0.1 add.245
  30.9 1.7 copy.83
  32.6 3.9 %all-to-all-done = bf16[64,8,256]{2,0,1:T(8,128)(2,1)S(1)} async-done(((bf16[64,8,256]{2,0,1:T(8,128)(2,1)}), bf16[64,8,256]{2,0,1:T(8,128)(2,1)S(1)}, u32[]{:S(2)}, u32[]{:S(2)}) %all-to-all-start) | async-done | bytes 262176 | tf_op jit(solution)/shard_map/all_to_all | solution.py:136
  36.5 3.4 %all-to-all-start.1 = ((bf16[64,8,256]{2,0,1:T(8,128)(2,1)}), bf16[64,8,256]{2,0,1:T(8,128)(2,1)S(1)}, u32[]{:S(2)}, u32[]{:S(2)}) async-start(bf16[64,8,256]{2,0,1:T(8,128)(2,1)} %bitcast.61), calls=%async_computation.1 | async-start | bytes 524288 | tf_op jit(solution)/shard_map/all_to_all | solution.py:138
  39.9 0.0 reduce-scatter.2.cloned.1.call-start
  40.0 0.1 collective-permute-start
  40.1 10.5 %all-to-all-done.1 = bf16[64,8,256]{2,0,1:T(8,128)(2,1)S(1)} async-done(((bf16[64,8,256]{2,0,1:T(8,128)(2,1)}), bf16[64,8,256]{2,0,1:T(8,128)(2,1)S(1)}, u32[]{:S(2)}, u32[]{:S(2)}) %all-to-all-start.1) | async-done | bytes 262176 | tf_op jit(solution)/shard_map/all_to_all | solution.py:138
  50.7 0.1 select_n.172
  50.7 0.1 select_n.168
  50.9 0.1 concatenate.14.tab_ref
  50.9 1.2 collective-permute-done.1.pg_ref
  52.2 41.6 %all-gather.2.cloned.1.call-done.kv_ref = bf16[16384,256]{1,0:T(8,128)(2,1)} async-done(((bf16[512,256]{1,0:T(8,128)(2,1)}), bf16[16384,256]{1,0:T(8,128)(2,1)}) %all-gather.2.cloned.1.call-update) | async-done | bytes 8388624 | tf_op jit(solution)/shard_map/all_gather | solution.py:140
  93.7 45.1 %shard_map.84 = (bf16[512,256]{1,0:T(8,128)(2,1)S(1)}, bf16[512,256]{1,0:T(8,128)(2,1)S(1)}, f32[8192,256]{1,0:T(8,128)}) custom-call(s32[1312]{0:T(1024)S(1)} %concatenate.14.tab_ref, bf16[512,256]{1,0:T(8,128)(2,1)S(1)} %bitcast.66, bf16[512,256]{1,0:T(8,128)(2,1)S(1)} %bitcast.68, bf16[512,256]{1,0:T(8,128)(2,1)S(1)} %collective-permute-done.pq_ref, ...), custom_call_target="tpu_custom_call" | custom-call | tf_op jit(solution)/shard_map/pallas_call | solution.py:189
  138.9 0.5 broadcast.619
  139.4 0.8 reduce
  140.2 0.8 reshape.323
  141.0 6.7 %all-to-all-start.3 = ((bf16[8,2,8192]{2,1,0:T(2,128)(2,1)}), bf16[8,2,8192]{2,1,0:T(2,128)(2,1)S(1)}, u32[]{:S(2)}, u32[]{:S(2)}) async-start(bf16[8,2,8192]{2,1,0:T(2,128)(2,1)} %reshape.323), calls=%async_computation.3 | async-start | bytes 524288 | tf_op jit(solution)/shard_map/all_to_all | solution.py:211
  147.7 0.8 reduce.1
  148.5 0.1 reshape.325
  148.5 8.1 %all-to-all-done.3 = bf16[8,2,8192]{2,1,0:T(2,128)(2,1)S(1)} async-done(((bf16[8,2,8192]{2,1,0:T(2,128)(2,1)}), bf16[8,2,8192]{2,1,0:T(2,128)(2,1)S(1)}, u32[]{:S(2)}, u32[]{:S(2)}) %all-to-all-start.3) | async-done | bytes 262176 | tf_op jit(solution)/shard_map/all_to_all | solution.py:211
  156.6 87.8 %all_to_all.81 = bf16[8,2,8192]{2,1,0:T(2,128)(2,1)S(1)} all-to-all(bf16[8,2,8192]{2,1,0:T(2,128)(2,1)S(1)} %reshape.325), channel_id=1, replica_groups=mesh['uly'=8,'chip'=16,'core'=2] {'uly'}, dimensions={0} | all-to-all | bytes 524288 | tf_op jit(solution)/shard_map/all_to_all | solution.py:212
  244.4 3.5 %all-to-all-start.5 = ((f32[8,64,256]{2,1,0:T(8,128)}), f32[8,64,256]{2,1,0:T(8,128)S(1)}, u32[]{:S(2)}, u32[]{:S(2)}) async-start(f32[8,64,256]{2,1,0:T(8,128)} %bitcast.76), calls=%async_computation.6 | async-start | bytes 1048576 | tf_op jit(solution)/shard_map/all_to_all | solution.py:218
  247.9 0.3 reshape.324
  248.3 0.7 copy.75
  249.0 0.3 reshape.326
  249.3 0.7 copy.76
  250.0 8.9 %all-to-all-done.5 = f32[8,64,256]{2,1,0:T(8,128)S(1)} async-done(((f32[8,64,256]{2,1,0:T(8,128)}), f32[8,64,256]{2,1,0:T(8,128)S(1)}, u32[]{:S(2)}, u32[]{:S(2)}) %all-to-all-start.5) | async-done | bytes 524320 | tf_op jit(solution)/shard_map/all_to_all | solution.py:218
  259.0 0.6 copy.85
  259.6 0.6 copy.86
  (19 shorter events, 0.3 us)
Async XLA Ops:
  7.2 86.6 %all-gather.2.cloned.1.call-start = ((), (), s32[]{:S(2)}) async-start(), calls=%async_computation.7 | async-start | bytes 8650752 | tf_op jit(solution)/shard_map/all_gather | solution.py:140
  24.4 12.1 %all-to-all-start = ((bf16[64,8,256]{2,0,1:T(8,128)(2,1)}), bf16[64,8,256]{2,0,1:T(8,128)(2,1)S(1)}, u32[]{:S(2)}, u32[]{:S(2)}) async-start(bf16[64,8,256]{2,0,1:T(8,128)(2,1)} %bitcast.62), calls=%async_computation | async-start | bytes 524288 | tf_op jit(solution)/shard_map/all_to_all | solution.py:136
  36.5 14.1 %all-to-all-start.1 = ((bf16[64,8,256]{2,0,1:T(8,128)(2,1)}), bf16[64,8,256]{2,0,1:T(8,128)(2,1)S(1)}, u32[]{:S(2)}, u32[]{:S(2)}) async-start(bf16[64,8,256]{2,0,1:T(8,128)(2,1)} %bitcast.61), calls=%async_computation.1 | async-start | bytes 524288 | tf_op jit(solution)/shard_map/all_to_all | solution.py:138
  39.9 204.5 %reduce-scatter.2.cloned.1.call-start = ((), (), s32[]{:S(2)}) async-start(), calls=%async_computation.8 | async-start | bytes 8912896 | tf_op jit(solution)/shard_map/reduce_scatter | solution.py:217
  40.0 10.9 %collective-permute-start = (bf16[512,256]{1,0:T(8,128)(2,1)S(1)}, bf16[512,256]{1,0:T(8,128)(2,1)S(1)}, u32[]{:S(2)}, u32[]{:S(2)}) collective-permute-start(bf16[512,256]{1,0:T(8,128)(2,1)S(1)} %bitcast.65), channel_id=1, source_target_pairs={{0,1},{1,0},{2,3},{3,2},{4,5},{5,4},{6,7},{7,6},{8,9},{9,8},{10,11... | collective-permute-start | bytes 786440 | tf_op jit(solution)/shard_map/ppermute | solution.py:179
  50.6 1.5 collective-permute-start.1
  141.0 15.7 %all-to-all-start.3 = ((bf16[8,2,8192]{2,1,0:T(2,128)(2,1)}), bf16[8,2,8192]{2,1,0:T(2,128)(2,1)S(1)}, u32[]{:S(2)}, u32[]{:S(2)}) async-start(bf16[8,2,8192]{2,1,0:T(2,128)(2,1)} %reshape.323), calls=%async_computation.3 | async-start | bytes 524288 | tf_op jit(solution)/shard_map/all_to_all | solution.py:211
  244.4 14.5 %all-to-all-start.5 = ((f32[8,64,256]{2,1,0:T(8,128)}), f32[8,64,256]{2,1,0:T(8,128)S(1)}, u32[]{:S(2)}, u32[]{:S(2)}) async-start(f32[8,64,256]{2,1,0:T(8,128)} %bitcast.76), calls=%async_computation.6 | async-start | bytes 1048576 | tf_op jit(solution)/shard_map/all_to_all | solution.py:218
Sparse Core Ops, SparseCore 0:
  22.9 70.8 all-gather.1
  139.0 100.5 reduce-scatter.1

commit v10 on v9

--- a/solution.py
+++ b/solution.py
@@ -131,13 +131,28 @@
         ],
         axis=2,
     )
-    kv_slots = jnp.repeat(kv_local, copy_count, axis=1)
-    query_all, kv_mine, grad_all = (
+    uly_index = lax.axis_index("uly")
+    group_of = lambda u: u // copy_count
+    kv_shifted = [lax.dynamic_index_in_dim(kv_local, group_of(uly_index), axis=1, keepdims=False)]
+    for shift in range(1, ulysses_width):
+        dest_group = group_of((uly_index + shift) % ulysses_width)
+        outgoing = lax.dynamic_index_in_dim(kv_local, dest_group, axis=1, keepdims=False)
+        kv_shifted.append(
+            lax.ppermute(
+                outgoing,
+                "uly",
+                [(u, (u + shift) % ulysses_width) for u in range(ulysses_width)],
+            )
+        )
+    kv_stack = jnp.stack(kv_shifted)
+    kv_mine = kv_stack[(uly_index - jnp.arange(ulysses_width)) % ulysses_width]
+    query_all, grad_all = (
         lax.all_to_all(query_slots, "uly", split_axis=1, concat_axis=0, tiled=True),
-        lax.all_to_all(kv_slots, "uly", split_axis=1, concat_axis=0, tiled=True),
         lax.all_to_all(grad_slots, "uly", split_axis=1, concat_axis=0, tiled=True),
     )
-    keys_all = lax.all_gather(kv_mine[:, 0, :], ("chip", "core"), axis=0, tiled=True)
+    keys_all = lax.all_gather(
+        kv_mine.reshape(ulysses_width * segment_length, 2 * HEAD_SIZE), ("chip", "core"), axis=0, tiled=True
+    )
     item_count = heads_dev * ulysses_width
     item_ids = jnp.arange(item_count, dtype=jnp.int32)
     head_ids = item_ids // ulysses_width

time: 269 us -> 278 us (1.033)
  starting transfers between devices: 17.2 us -> 35.5 us
  blocking collectives: 102 us -> 87.6 us
    ppermute x0 -> x7, starting transfers between devices: none -> 15.1 us  [body(): lax.ppermute(outgoing, 'uly', [(u, (u + shift) % ulysses_width) for u in...]
    all_to_all x1 -> x0, blocking collectives: 13.9 us -> none  [body(): lax.all_to_all(kv_slots, 'uly', split_axis=1, concat_axis=0, tiled=True)]
    all_to_all x1, starting transfers between devices: 3.41 us -> 6.55 us  [body(): lax.all_to_all(query_slots, 'uly', split_axis=1, concat_axis=0, tiled=True)]
  transfers between devices with their start and end apart: 8 -> 15, of which waited for: 6 -> 8; matrix products, arithmetic and copies ran while one was open for 4% -> 4% of each run, Pallas kernels for 0% -> 0%
where the time goes in v10:
time: 278 us; the launch traced here: 276 us
  blocking collectives  87.6 us (32%)
  waiting for transfers between devices  77 us (28%)
  Pallas kernels  45.1 us (16%)
  starting transfers between devices  35.5 us (13%)
  between operations  14.6 us (5%)
  local copies, waits for them, and re-layouts  14.5 us (5%)
    all_to_all x1, blocking collectives, body(): lax.all_to_all(qgrad_items, 'uly', split_axis=0, concat_axis=1, tiled=True)  87.6 us
    pallas_call x1, Pallas kernels, body(): pl.pallas_call(kernel, out_shape=(jax.ShapeDtypeStruct(q_rows.shape, jnp....  45.1 us
    all_gather x1, waiting for transfers between devices, body(): lax.all_gather(kv_mine.reshape(ulysses_width * segment_length, 2 * HEAD_S...  42.9 us
    ppermute x7, starting transfers between devices, body(): lax.ppermute(outgoing, 'uly', [(u, (u + shift) % ulysses_width) for u in...  15.1 us
    all_to_all x1, waiting for transfers between devices, body(): lax.all_to_all(grad_slots, 'uly', split_axis=1, concat_axis=0, tiled=True)  9.66 us
    all_to_all x1, waiting for transfers between devices, body(): lax.all_to_all(owned.reshape(ulysses_width, segment_length, 2 * HEAD_SIZE...  8.91 us
    all_to_all x1, waiting for transfers between devices, body(): lax.all_to_all(out_items, 'uly', split_axis=0, concat_axis=1, tiled=True)  8.07 us
    all_to_all x1, starting transfers between devices, body(): lax.all_to_all(out_items, 'uly', split_axis=0, concat_axis=1, tiled=True)  6.82 us
  transfers between devices with their start and end apart: 15, of which 8 were waited for; matrix products, arithmetic and copies ran while one was open for 4% of the time, Pallas kernels for 0%

profile of v10, /device:TPU:0, one launch (start us, length us, event | category | flops | bytes accessed | tf_op | source)
XLA Modules:
  0.0 276.4 jit_solution(10847553115881020092)
XLA Ops:
  7.5 0.8 reshape.350
  8.3 0.8 reshape.351
  9.1 0.6 constant_dynamic-slice_fusion
  9.8 2.7 collective-permute-start.3
  12.6 3.8 %collective-permute-start.4 = (bf16[64,256]{1,0:T(8,128)(2,1)S(1)}, bf16[64,256]{1,0:T(8,128)(2,1)S(1)}, u32[]{:S(2)}, u32[]{:S(2)}) collective-permute-start(bf16[64,256]{1,0:T(8,128)(2,1)S(1)} %bitcast.118), channel_id=1, source_target_pairs={{0,96},{32,128},{64,160},{96,192},{128,224},{160,0},{192,32},{224,... | collective-permute-start | bytes 98312 | tf_op jit(solution)/shard_map/ppermute | solution.py:141
  16.4 0.5 collective-permute-start.5
  16.9 3.1 %collective-permute-start.6 = (bf16[64,256]{1,0:T(8,128)(2,1)S(1)}, bf16[64,256]{1,0:T(8,128)(2,1)S(1)}, u32[]{:S(2)}, u32[]{:S(2)}) collective-permute-start(bf16[64,256]{1,0:T(8,128)(2,1)S(1)} %bitcast.115), channel_id=1, source_target_pairs={{0,160},{32,192},{64,224},{96,0},{128,32},{160,64},{192,96},{224,1... | collective-permute-start | bytes 98312 | tf_op jit(solution)/shard_map/ppermute | solution.py:141
  20.1 3.1 %collective-permute-start.7 = (bf16[64,256]{1,0:T(8,128)(2,1)S(1)}, bf16[64,256]{1,0:T(8,128)(2,1)S(1)}, u32[]{:S(2)}, u32[]{:S(2)}) collective-permute-start(bf16[64,256]{1,0:T(8,128)(2,1)S(1)} %bitcast.119), channel_id=1, source_target_pairs={{0,192},{32,224},{64,0},{96,32},{128,64},{160,96},{192,128},{224,1... | collective-permute-start | bytes 98312 | tf_op jit(solution)/shard_map/ppermute | solution.py:141
  23.2 1.7 collective-permute-start.8
  25.0 0.7 collective-permute-done.7
  25.6 1.5 collective-permute-done.8
  27.2 1.3 gather_fusion.2
  28.5 1.7 copy.100
  30.1 6.6 %all-to-all-start = ((bf16[64,8,256]{2,0,1:T(8,128)(2,1)}), bf16[64,8,256]{2,0,1:T(8,128)(2,1)S(1)}, u32[]{:S(2)}, u32[]{:S(2)}) async-start(bf16[64,8,256]{2,0,1:T(8,128)(2,1)} %bitcast.89), calls=%async_computation | async-start | bytes 524288 | tf_op jit(solution)/shard_map/all_to_all | solution.py:150
  36.7 0.8 copy.53
  37.5 0.6 gather_fusion.1
  38.3 0.6 gather_fusion
  39.0 0.1 and_reduce_fusion
  39.1 0.1 copy.60
  39.2 0.1 copy.56
  39.3 0.1 iota_add_fusion
  39.4 0.1 add.350
  39.5 0.1 iota_add_fusion.1
  39.6 0.1 add.344
  39.7 1.7 copy.99
  41.4 4.0 %all-to-all-done = bf16[64,8,256]{2,0,1:T(8,128)(2,1)S(1)} async-done(((bf16[64,8,256]{2,0,1:T(8,128)(2,1)}), bf16[64,8,256]{2,0,1:T(8,128)(2,1)S(1)}, u32[]{:S(2)}, u32[]{:S(2)}) %all-to-all-start) | async-done | bytes 262176 | tf_op jit(solution)/shard_map/all_to_all | solution.py:150
  45.4 3.4 %all-to-all-start.1 = ((bf16[64,8,256]{2,0,1:T(8,128)(2,1)}), bf16[64,8,256]{2,0,1:T(8,128)(2,1)S(1)}, u32[]{:S(2)}, u32[]{:S(2)}) async-start(bf16[64,8,256]{2,0,1:T(8,128)(2,1)} %bitcast.88), calls=%async_computation.1 | async-start | bytes 524288 | tf_op jit(solution)/shard_map/all_to_all | solution.py:151
  48.9 0.1 collective-permute-start
  49.0 9.7 %all-to-all-done.1 = bf16[64,8,256]{2,0,1:T(8,128)(2,1)S(1)} async-done(((bf16[64,8,256]{2,0,1:T(8,128)(2,1)}), bf16[64,8,256]{2,0,1:T(8,128)(2,1)S(1)}, u32[]{:S(2)}, u32[]{:S(2)}) %all-to-all-start.1) | async-done | bytes 262176 | tf_op jit(solution)/shard_map/all_to_all | solution.py:151
  58.8 0.1 select_n.271
  59.0 1.2 collective-permute-done.1.pg_ref
  60.2 42.9 %all-gather.2.cloned.1.call-done.kv_ref = bf16[16384,256]{1,0:T(8,128)(2,1)} async-done(((bf16[512,256]{1,0:T(8,128)(2,1)}), bf16[16384,256]{1,0:T(8,128)(2,1)}) %all-gather.2.cloned.1.call-update) | async-done | bytes 8388624 | tf_op jit(solution)/shard_map/all_gather | solution.py:153
  103.1 45.1 %shard_map.84 = (bf16[512,256]{1,0:T(8,128)(2,1)S(1)}, bf16[512,256]{1,0:T(8,128)(2,1)S(1)}, f32[8192,256]{1,0:T(8,128)}) custom-call(s32[1312]{0:T(1024)S(1)} %concatenate.14.tab_ref, bf16[512,256]{1,0:T(8,128)(2,1)S(1)} %bitcast.100, bf16[512,256]{1,0:T(8,128)(2,1)S(1)} %bitcast.102, bf16[512,256]{1,0:T(8,128)(2,1)S(1)} %collective-permute-done.pq_ref, ...), custom_call_target="tpu_custom_call" | custom-call | tf_op jit(solution)/shard_map/pallas_call | solution.py:204
  148.2 0.5 broadcast.703
  148.8 0.8 reduce
  149.6 0.8 reshape.380
  150.3 6.8 %all-to-all-start.2 = ((bf16[8,2,8192]{2,1,0:T(2,128)(2,1)}), bf16[8,2,8192]{2,1,0:T(2,128)(2,1)S(1)}, u32[]{:S(2)}, u32[]{:S(2)}) async-start(bf16[8,2,8192]{2,1,0:T(2,128)(2,1)} %reshape.380), calls=%async_computation.2 | async-start | bytes 524288 | tf_op jit(solution)/shard_map/all_to_all | solution.py:226
  157.2 0.8 reduce.1
  158.0 8.1 %all-to-all-done.2 = bf16[8,2,8192]{2,1,0:T(2,128)(2,1)S(1)} async-done(((bf16[8,2,8192]{2,1,0:T(2,128)(2,1)}), bf16[8,2,8192]{2,1,0:T(2,128)(2,1)S(1)}, u32[]{:S(2)}, u32[]{:S(2)}) %all-to-all-start.2) | async-done | bytes 262176 | tf_op jit(solution)/shard_map/all_to_all | solution.py:226
  166.1 87.6 %all_to_all.65 = bf16[8,2,8192]{2,1,0:T(2,128)(2,1)S(1)} all-to-all(bf16[8,2,8192]{2,1,0:T(2,128)(2,1)S(1)} %reshape.382), channel_id=1, replica_groups=mesh['uly'=8,'chip'=16,'core'=2] {'uly'}, dimensions={0} | all-to-all | bytes 524288 | tf_op jit(solution)/shard_map/all_to_all | solution.py:227
  253.7 3.5 %all-to-all-start.4 = ((f32[8,64,256]{2,1,0:T(8,128)}), f32[8,64,256]{2,1,0:T(8,128)S(1)}, u32[]{:S(2)}, u32[]{:S(2)}) async-start(f32[8,64,256]{2,1,0:T(8,128)} %bitcast.109), calls=%async_computation.5 | async-start | bytes 1048576 | tf_op jit(solution)/shard_map/all_to_all | solution.py:233
  257.2 0.3 reshape.381
  257.6 0.7 copy.83
  258.3 0.3 reshape.383
  258.6 0.7 copy.84
  259.3 8.9 %all-to-all-done.4 = f32[8,64,256]{2,1,0:T(8,128)S(1)} async-done(((f32[8,64,256]{2,1,0:T(8,128)}), f32[8,64,256]{2,1,0:T(8,128)S(1)}, u32[]{:S(2)}, u32[]{:S(2)}) %all-to-all-start.4) | async-done | bytes 524320 | tf_op jit(solution)/shard_map/all_to_all | solution.py:233
  268.3 0.6 copy.101
  268.9 0.6 copy.102
  (50 shorter events, 1.0 us)
Async XLA Ops:
  7.2 95.9 %all-gather.2.cloned.1.call-start = ((), (), s32[]{:S(2)}) async-start(), calls=%async_computation.6 | async-start | bytes 8650752 | tf_op jit(solution)/shard_map/all_gather | solution.py:153
  9.7 10.4 %collective-permute-start.2 = (bf16[64,256]{1,0:T(8,128)(2,1)S(1)}, bf16[64,256]{1,0:T(8,128)(2,1)S(1)}, u32[]{:S(2)}, u32[]{:S(2)}) collective-permute-start(bf16[64,256]{1,0:T(8,128)(2,1)S(1)} %bitcast.121), channel_id=1, source_target_pairs={{0,32},{32,64},{64,96},{96,128},{128,160},{160,192},{192,224},{224... | collective-permute-start | bytes 98312 | tf_op jit(solution)/shard_map/ppermute | solution.py:141
  9.8 13.4 %collective-permute-start.3 = (bf16[64,256]{1,0:T(8,128)(2,1)S(1)}, bf16[64,256]{1,0:T(8,128)(2,1)S(1)}, u32[]{:S(2)}, u32[]{:S(2)}) collective-permute-start(bf16[64,256]{1,0:T(8,128)(2,1)S(1)} %bitcast.120), channel_id=1, source_target_pairs={{0,64},{32,96},{64,128},{96,160},{128,192},{160,224},{192,0},{224,... | collective-permute-start | bytes 98312 | tf_op jit(solution)/shard_map/ppermute | solution.py:141
  12.6 12.3 %collective-permute-start.4 = (bf16[64,256]{1,0:T(8,128)(2,1)S(1)}, bf16[64,256]{1,0:T(8,128)(2,1)S(1)}, u32[]{:S(2)}, u32[]{:S(2)}) collective-permute-start(bf16[64,256]{1,0:T(8,128)(2,1)S(1)} %bitcast.118), channel_id=1, source_target_pairs={{0,96},{32,128},{64,160},{96,192},{128,224},{160,0},{192,32},{224,... | collective-permute-start | bytes 98312 | tf_op jit(solution)/shard_map/ppermute | solution.py:141
  16.4 8.5 %collective-permute-start.5 = (bf16[64,256]{1,0:T(8,128)(2,1)S(1)}, bf16[64,256]{1,0:T(8,128)(2,1)S(1)}, u32[]{:S(2)}, u32[]{:S(2)}) collective-permute-start(bf16[64,256]{1,0:T(8,128)(2,1)S(1)} %bitcast.116), channel_id=1, source_target_pairs={{0,128},{32,160},{64,192},{96,224},{128,0},{160,32},{192,64},{224,... | collective-permute-start | bytes 98312 | tf_op jit(solution)/shard_map/ppermute | solution.py:141
  16.9 8.0 %collective-permute-start.6 = (bf16[64,256]{1,0:T(8,128)(2,1)S(1)}, bf16[64,256]{1,0:T(8,128)(2,1)S(1)}, u32[]{:S(2)}, u32[]{:S(2)}) collective-permute-start(bf16[64,256]{1,0:T(8,128)(2,1)S(1)} %bitcast.115), channel_id=1, source_target_pairs={{0,160},{32,192},{64,224},{96,0},{128,32},{160,64},{192,96},{224,1... | collective-permute-start | bytes 98312 | tf_op jit(solution)/shard_map/ppermute | solution.py:141
  20.1 5.5 %collective-permute-start.7 = (bf16[64,256]{1,0:T(8,128)(2,1)S(1)}, bf16[64,256]{1,0:T(8,128)(2,1)S(1)}, u32[]{:S(2)}, u32[]{:S(2)}) collective-permute-start(bf16[64,256]{1,0:T(8,128)(2,1)S(1)} %bitcast.119), channel_id=1, source_target_pairs={{0,192},{32,224},{64,0},{96,32},{128,64},{160,96},{192,128},{224,1... | collective-permute-start | bytes 98312 | tf_op jit(solution)/shard_map/ppermute | solution.py:141
  23.2 3.9 %collective-permute-start.8 = (bf16[64,256]{1,0:T(8,128)(2,1)S(1)}, bf16[64,256]{1,0:T(8,128)(2,1)S(1)}, u32[]{:S(2)}, u32[]{:S(2)}) collective-permute-start(bf16[64,256]{1,0:T(8,128)(2,1)S(1)} %bitcast.117), channel_id=1, source_target_pairs={{0,224},{32,0},{64,32},{96,64},{128,96},{160,128},{192,160},{224,1... | collective-permute-start | bytes 98312 | tf_op jit(solution)/shard_map/ppermute | solution.py:141
  30.1 15.3 %all-to-all-start = ((bf16[64,8,256]{2,0,1:T(8,128)(2,1)}), bf16[64,8,256]{2,0,1:T(8,128)(2,1)S(1)}, u32[]{:S(2)}, u32[]{:S(2)}) async-start(bf16[64,8,256]{2,0,1:T(8,128)(2,1)} %bitcast.89), calls=%async_computation | async-start | bytes 524288 | tf_op jit(solution)/shard_map/all_to_all | solution.py:150
  45.4 13.3 %all-to-all-start.1 = ((bf16[64,8,256]{2,0,1:T(8,128)(2,1)}), bf16[64,8,256]{2,0,1:T(8,128)(2,1)S(1)}, u32[]{:S(2)}, u32[]{:S(2)}) async-start(bf16[64,8,256]{2,0,1:T(8,128)(2,1)} %bitcast.88), calls=%async_computation.1 | async-start | bytes 524288 | tf_op jit(solution)/shard_map/all_to_all | solution.py:151
  48.8 204.9 %reduce-scatter.2.cloned.1.call-start = ((), (), s32[]{:S(2)}) async-start(), calls=%async_computation.7 | async-start | bytes 8912896 | tf_op jit(solution)/shard_map/reduce_scatter | solution.py:232
  48.9 10.1 %collective-permute-start = (bf16[512,256]{1,0:T(8,128)(2,1)S(1)}, bf16[512,256]{1,0:T(8,128)(2,1)S(1)}, u32[]{:S(2)}, u32[]{:S(2)}) collective-permute-start(bf16[512,256]{1,0:T(8,128)(2,1)S(1)} %bitcast.99), channel_id=1, source_target_pairs={{0,1},{1,0},{2,3},{3,2},{4,5},{5,4},{6,7},{7,6},{8,9},{9,8},{10,11... | collective-permute-start | bytes 786440 | tf_op jit(solution)/shard_map/ppermute | solution.py:194
  58.7 1.5 collective-permute-start.1
  150.3 15.8 %all-to-all-start.2 = ((bf16[8,2,8192]{2,1,0:T(2,128)(2,1)}), bf16[8,2,8192]{2,1,0:T(2,128)(2,1)S(1)}, u32[]{:S(2)}, u32[]{:S(2)}) async-start(bf16[8,2,8192]{2,1,0:T(2,128)(2,1)} %reshape.380), calls=%async_computation.2 | async-start | bytes 524288 | tf_op jit(solution)/shard_map/all_to_all | solution.py:226
  253.7 14.5 %all-to-all-start.4 = ((f32[8,64,256]{2,1,0:T(8,128)}), f32[8,64,256]{2,1,0:T(8,128)S(1)}, u32[]{:S(2)}, u32[]{:S(2)}) async-start(f32[8,64,256]{2,1,0:T(8,128)} %bitcast.109), calls=%async_computation.5 | async-start | bytes 1048576 | tf_op jit(solution)/shard_map/all_to_all | solution.py:233
Sparse Core Ops, SparseCore 0:
  28.6 74.4 all-gather.1
  148.4 100.4 reduce-scatter.1

commit v11 on v9

--- a/solution.py
+++ b/solution.py
@@ -59,11 +59,9 @@
             )
             masked = jnp.where(allowed, scores, -1e30)
             row_max = jnp.max(masked, axis=1, keepdims=True)
-            row_sum = jnp.sum(
-                jnp.where(allowed, jnp.exp(masked - row_max), 0.0), axis=1, keepdims=True
-            )
-            log_sum = row_max + jnp.log(row_sum)
-            weights = jnp.where(allowed, jnp.exp(masked - log_sum), 0.0)
+            shifted = jnp.where(allowed, jnp.exp(masked - row_max), 0.0)
+            row_sum = jnp.sum(shifted, axis=1, keepdims=True)
+            weights = shifted / row_sum
             weights_low = weights.astype(jnp.bfloat16)
             out_block = jnp.dot(
                 weights_low, value_group, preferred_element_type=jnp.float32

time: 269 us -> 268 us (level)
  no operation moved by 1% of the time
where the time goes in v11:
time: 268 us; the launch traced here: 267 us
  blocking collectives  102 us (38%)
  waiting for transfers between devices  74.3 us (28%)
  Pallas kernels  44.7 us (17%)
  starting transfers between devices  17.2 us (6%)
  between operations  14.2 us (5%)
  local copies, waits for them, and re-layouts  12.5 us (5%)
    all_to_all x1, blocking collectives, body(): lax.all_to_all(qgrad_items, 'uly', split_axis=0, concat_axis=1, tiled=True)  87.7 us
    pallas_call x1, Pallas kernels, body(): pl.pallas_call(kernel, out_shape=(jax.ShapeDtypeStruct(q_rows.shape, jnp....  44.7 us
    all_gather x1, waiting for transfers between devices, body(): lax.all_gather(kv_mine[:, 0, :], ('chip', 'core'), axis=0, tiled=True)  41.6 us
    all_to_all x1, blocking collectives, body(): lax.all_to_all(kv_slots, 'uly', split_axis=1, concat_axis=0, tiled=True)  13.9 us
    all_to_all x1, waiting for transfers between devices, body(): lax.all_to_all(grad_slots, 'uly', split_axis=1, concat_axis=0, tiled=True)  10.5 us
    all_to_all x1, waiting for transfers between devices, body(): lax.all_to_all(owned.reshape(ulysses_width, segment_length, 2 * HEAD_SIZE...  8.91 us
    all_to_all x1, waiting for transfers between devices, body(): lax.all_to_all(out_items, 'uly', split_axis=0, concat_axis=1, tiled=True)  8.13 us
    all_to_all x1, starting transfers between devices, body(): lax.all_to_all(out_items, 'uly', split_axis=0, concat_axis=1, tiled=True)  6.69 us
  transfers between devices with their start and end apart: 8, of which 6 were waited for; matrix products, arithmetic and copies ran while one was open for 4% of the time, Pallas kernels for 0%

profile of v11, /device:TPU:0, one launch (start us, length us, event | category | flops | bytes accessed | tf_op | source)
XLA Modules:
  0.0 266.7 jit_solution(5780967040233096697)
XLA Ops:
  7.2 0.0 all-gather.2.cloned.1.call-start
  7.2 0.8 reshape.301
  8.0 0.8 reshape.302
  8.8 0.1 pad_maximum_fusion
  8.9 13.9 %all_to_all.80 = bf16[64,8,256]{2,0,1:T(8,128)(2,1)} all-to-all(bf16[64,8,256]{2,0,1:T(8,128)(2,1)S(1)} %bitcast.74), channel_id=1, replica_groups=mesh['uly'=8,'chip'=16,'core'=2] {'uly'}, dimensions={1} | all-to-all | bytes 524288 | tf_op jit(solution)/shard_map/all_to_all | solution.py:135
  22.7 0.0 all-gather.2.cloned.1.call-update
  22.8 1.7 copy.84
  24.4 3.4 %all-to-all-start = ((bf16[64,8,256]{2,0,1:T(8,128)(2,1)}), bf16[64,8,256]{2,0,1:T(8,128)(2,1)S(1)}, u32[]{:S(2)}, u32[]{:S(2)}) async-start(bf16[64,8,256]{2,0,1:T(8,128)(2,1)} %bitcast.62), calls=%async_computation | async-start | bytes 524288 | tf_op jit(solution)/shard_map/all_to_all | solution.py:134
  27.9 0.8 copy.52
  28.7 0.6 gather_fusion.1
  29.3 0.1 copy.57
  29.4 0.6 gather_fusion
  30.1 0.1 copy.53
  30.1 0.1 and_reduce_fusion
  30.2 0.1 copy.59
  30.3 0.1 copy.55
  30.4 0.1 iota_add_fusion
  30.5 0.1 add.251
  30.7 0.1 iota_add_fusion.1
  30.7 0.1 add.245
  30.9 1.7 copy.83
  32.6 3.9 %all-to-all-done = bf16[64,8,256]{2,0,1:T(8,128)(2,1)S(1)} async-done(((bf16[64,8,256]{2,0,1:T(8,128)(2,1)}), bf16[64,8,256]{2,0,1:T(8,128)(2,1)S(1)}, u32[]{:S(2)}, u32[]{:S(2)}) %all-to-all-start) | async-done | bytes 262176 | tf_op jit(solution)/shard_map/all_to_all | solution.py:134
  36.5 3.4 %all-to-all-start.1 = ((bf16[64,8,256]{2,0,1:T(8,128)(2,1)}), bf16[64,8,256]{2,0,1:T(8,128)(2,1)S(1)}, u32[]{:S(2)}, u32[]{:S(2)}) async-start(bf16[64,8,256]{2,0,1:T(8,128)(2,1)} %bitcast.61), calls=%async_computation.1 | async-start | bytes 524288 | tf_op jit(solution)/shard_map/all_to_all | solution.py:136
  39.9 0.0 reduce-scatter.2.cloned.1.call-start
  40.0 0.1 collective-permute-start
  40.1 10.5 %all-to-all-done.1 = bf16[64,8,256]{2,0,1:T(8,128)(2,1)S(1)} async-done(((bf16[64,8,256]{2,0,1:T(8,128)(2,1)}), bf16[64,8,256]{2,0,1:T(8,128)(2,1)S(1)}, u32[]{:S(2)}, u32[]{:S(2)}) %all-to-all-start.1) | async-done | bytes 262176 | tf_op jit(solution)/shard_map/all_to_all | solution.py:136
  50.7 0.1 select_n.172
  50.7 0.1 select_n.168
  50.9 0.1 concatenate.14.tab_ref
  50.9 1.2 collective-permute-done.1.pg_ref
  52.2 41.6 %all-gather.2.cloned.1.call-done.kv_ref = bf16[16384,256]{1,0:T(8,128)(2,1)} async-done(((bf16[512,256]{1,0:T(8,128)(2,1)}), bf16[16384,256]{1,0:T(8,128)(2,1)}) %all-gather.2.cloned.1.call-update) | async-done | bytes 8388624 | tf_op jit(solution)/shard_map/all_gather | solution.py:138
  93.7 44.7 %shard_map.84 = (bf16[512,256]{1,0:T(8,128)(2,1)S(1)}, bf16[512,256]{1,0:T(8,128)(2,1)S(1)}, f32[8192,256]{1,0:T(8,128)}) custom-call(s32[1312]{0:T(1024)S(1)} %concatenate.14.tab_ref, bf16[512,256]{1,0:T(8,128)(2,1)S(1)} %bitcast.66, bf16[512,256]{1,0:T(8,128)(2,1)S(1)} %bitcast.68, bf16[512,256]{1,0:T(8,128)(2,1)S(1)} %collective-permute-done.pq_ref, ...), custom_call_target="tpu_custom_call" | custom-call | tf_op jit(solution)/shard_map/pallas_call | solution.py:187
  138.5 0.5 broadcast.619
  139.0 0.8 reduce
  139.8 0.8 reshape.323
  140.6 6.7 %all-to-all-start.3 = ((bf16[8,2,8192]{2,1,0:T(2,128)(2,1)}), bf16[8,2,8192]{2,1,0:T(2,128)(2,1)S(1)}, u32[]{:S(2)}, u32[]{:S(2)}) async-start(bf16[8,2,8192]{2,1,0:T(2,128)(2,1)} %reshape.323), calls=%async_computation.3 | async-start | bytes 524288 | tf_op jit(solution)/shard_map/all_to_all | solution.py:209
  147.3 0.8 reduce.1
  148.1 0.1 reshape.325
  148.1 8.1 %all-to-all-done.3 = bf16[8,2,8192]{2,1,0:T(2,128)(2,1)S(1)} async-done(((bf16[8,2,8192]{2,1,0:T(2,128)(2,1)}), bf16[8,2,8192]{2,1,0:T(2,128)(2,1)S(1)}, u32[]{:S(2)}, u32[]{:S(2)}) %all-to-all-start.3) | async-done | bytes 262176 | tf_op jit(solution)/shard_map/all_to_all | solution.py:209
  156.3 87.7 %all_to_all.81 = bf16[8,2,8192]{2,1,0:T(2,128)(2,1)S(1)} all-to-all(bf16[8,2,8192]{2,1,0:T(2,128)(2,1)S(1)} %reshape.325), channel_id=1, replica_groups=mesh['uly'=8,'chip'=16,'core'=2] {'uly'}, dimensions={0} | all-to-all | bytes 524288 | tf_op jit(solution)/shard_map/all_to_all | solution.py:210
  244.0 3.5 %all-to-all-start.5 = ((f32[8,64,256]{2,1,0:T(8,128)}), f32[8,64,256]{2,1,0:T(8,128)S(1)}, u32[]{:S(2)}, u32[]{:S(2)}) async-start(f32[8,64,256]{2,1,0:T(8,128)} %bitcast.76), calls=%async_computation.6 | async-start | bytes 1048576 | tf_op jit(solution)/shard_map/all_to_all | solution.py:216
  247.5 0.3 reshape.324
  247.9 0.7 copy.75
  248.6 0.3 reshape.326
  248.9 0.7 copy.76
  249.6 8.9 %all-to-all-done.5 = f32[8,64,256]{2,1,0:T(8,128)S(1)} async-done(((f32[8,64,256]{2,1,0:T(8,128)}), f32[8,64,256]{2,1,0:T(8,128)S(1)}, u32[]{:S(2)}, u32[]{:S(2)}) %all-to-all-start.5) | async-done | bytes 524320 | tf_op jit(solution)/shard_map/all_to_all | solution.py:216
  258.6 0.6 copy.85
  259.2 0.6 copy.86
  (19 shorter events, 0.3 us)
Async XLA Ops:
  7.2 86.6 %all-gather.2.cloned.1.call-start = ((), (), s32[]{:S(2)}) async-start(), calls=%async_computation.7 | async-start | bytes 8650752 | tf_op jit(solution)/shard_map/all_gather | solution.py:138
  24.4 12.1 %all-to-all-start = ((bf16[64,8,256]{2,0,1:T(8,128)(2,1)}), bf16[64,8,256]{2,0,1:T(8,128)(2,1)S(1)}, u32[]{:S(2)}, u32[]{:S(2)}) async-start(bf16[64,8,256]{2,0,1:T(8,128)(2,1)} %bitcast.62), calls=%async_computation | async-start | bytes 524288 | tf_op jit(solution)/shard_map/all_to_all | solution.py:134
  36.5 14.1 %all-to-all-start.1 = ((bf16[64,8,256]{2,0,1:T(8,128)(2,1)}), bf16[64,8,256]{2,0,1:T(8,128)(2,1)S(1)}, u32[]{:S(2)}, u32[]{:S(2)}) async-start(bf16[64,8,256]{2,0,1:T(8,128)(2,1)} %bitcast.61), calls=%async_computation.1 | async-start | bytes 524288 | tf_op jit(solution)/shard_map/all_to_all | solution.py:136
  39.9 204.1 %reduce-scatter.2.cloned.1.call-start = ((), (), s32[]{:S(2)}) async-start(), calls=%async_computation.8 | async-start | bytes 8912896 | tf_op jit(solution)/shard_map/reduce_scatter | solution.py:215
  40.0 10.9 %collective-permute-start = (bf16[512,256]{1,0:T(8,128)(2,1)S(1)}, bf16[512,256]{1,0:T(8,128)(2,1)S(1)}, u32[]{:S(2)}, u32[]{:S(2)}) collective-permute-start(bf16[512,256]{1,0:T(8,128)(2,1)S(1)} %bitcast.65), channel_id=1, source_target_pairs={{0,1},{1,0},{2,3},{3,2},{4,5},{5,4},{6,7},{7,6},{8,9},{9,8},{10,11... | collective-permute-start | bytes 786440 | tf_op jit(solution)/shard_map/ppermute | solution.py:177
  50.6 1.5 collective-permute-start.1
  140.6 15.7 %all-to-all-start.3 = ((bf16[8,2,8192]{2,1,0:T(2,128)(2,1)}), bf16[8,2,8192]{2,1,0:T(2,128)(2,1)S(1)}, u32[]{:S(2)}, u32[]{:S(2)}) async-start(bf16[8,2,8192]{2,1,0:T(2,128)(2,1)} %reshape.323), calls=%async_computation.3 | async-start | bytes 524288 | tf_op jit(solution)/shard_map/all_to_all | solution.py:209
  244.0 14.5 %all-to-all-start.5 = ((f32[8,64,256]{2,1,0:T(8,128)}), f32[8,64,256]{2,1,0:T(8,128)S(1)}, u32[]{:S(2)}, u32[]{:S(2)}) async-start(f32[8,64,256]{2,1,0:T(8,128)} %bitcast.76), calls=%async_computation.6 | async-start | bytes 1048576 | tf_op jit(solution)/shard_map/all_to_all | solution.py:216
Sparse Core Ops, SparseCore 0:
  22.9 70.8 all-gather.1
  138.6 100.5 reduce-scatter.1

commit v12 on v9

--- a/solution.py
+++ b/solution.py
@@ -132,11 +132,12 @@
         axis=2,
     )
     kv_slots = jnp.repeat(kv_local, copy_count, axis=1)
-    query_all, kv_mine, grad_all = (
-        lax.all_to_all(query_slots, "uly", split_axis=1, concat_axis=0, tiled=True),
-        lax.all_to_all(kv_slots, "uly", split_axis=1, concat_axis=0, tiled=True),
-        lax.all_to_all(grad_slots, "uly", split_axis=1, concat_axis=0, tiled=True),
-    )
+    kv_mine = lax.all_to_all(kv_slots, "uly", split_axis=1, concat_axis=0, tiled=True)
+    both_all = lax.all_to_all(
+        jnp.concatenate([query_slots, grad_slots], axis=2), "uly", split_axis=1, concat_axis=0, tiled=True
+    )
+    query_all = both_all[:, :, :head_width]
+    grad_all = both_all[:, :, head_width:]
     keys_all = lax.all_gather(kv_mine[:, 0, :], ("chip", "core"), axis=0, tiled=True)
     item_count = heads_dev * ulysses_width
     item_ids = jnp.arange(item_count, dtype=jnp.int32)

time: 269 us -> 268 us (level)
  waiting for transfers between devices: 74.3 us -> 78.3 us
  starting transfers between devices: 17.2 us -> 14.5 us
    all_gather x1, waiting for transfers between devices: 41.6 us -> 53.2 us  [body(): lax.all_gather(kv_mine[:, 0, :], ('chip', 'core'), axis=0, tiled=True)]
    all_to_all x2 -> x1, waiting for transfers between devices: 14.5 us -> 6.82 us  [body(): lax.all_to_all(jnp.concatenate([query_slots, grad_slots], axis=2), 'uly',...]
    all_to_all x2 -> x1, starting transfers between devices: 6.83 us -> 3.49 us  [body(): lax.all_to_all(jnp.concatenate([query_slots, grad_slots], axis=2), 'uly',...]
  transfers between devices with their start and end apart: 8 -> 7, of which waited for: 6 -> 6; matrix products, arithmetic and copies ran while one was open for 4% -> 4% of each run, Pallas kernels for 0% -> 0%
where the time goes in v12:
time: 268 us; the launch traced here: 267 us
  blocking collectives  101 us (38%)
  waiting for transfers between devices  78.3 us (29%)
  Pallas kernels  45.1 us (17%)
  starting transfers between devices  14.5 us (5%)
  between operations  14.2 us (5%)
  local copies, waits for them, and re-layouts  10.3 us (4%)
  other arithmetic  2.99 us (1%)
    all_to_all x1, blocking collectives, body(): lax.all_to_all(qgrad_items, 'uly', split_axis=0, concat_axis=1, tiled=True)  87.6 us
    all_gather x1, waiting for transfers between devices, body(): lax.all_gather(kv_mine[:, 0, :], ('chip', 'core'), axis=0, tiled=True)  53.2 us
    pallas_call x1, Pallas kernels, body(): pl.pallas_call(kernel, out_shape=(jax.ShapeDtypeStruct(q_rows.shape, jnp....  45.1 us
    all_to_all x1, blocking collectives, body(): lax.all_to_all(kv_slots, 'uly', split_axis=1, concat_axis=0, tiled=True)  13.9 us
    all_to_all x1, waiting for transfers between devices, body(): lax.all_to_all(owned.reshape(ulysses_width, segment_length, 2 * HEAD_SIZE...  8.91 us
    all_to_all x1, waiting for transfers between devices, body(): lax.all_to_all(out_items, 'uly', split_axis=0, concat_axis=1, tiled=True)  8.07 us
    all_to_all x1, starting transfers between devices, body(): lax.all_to_all(out_items, 'uly', split_axis=0, concat_axis=1, tiled=True)  6.88 us
    all_to_all x1, waiting for transfers between devices, body(): lax.all_to_all(jnp.concatenate([query_slots, grad_slots], axis=2), 'uly',...  6.82 us
  transfers between devices with their start and end apart: 7, of which 6 were waited for; matrix products, arithmetic and copies ran while one was open for 4% of the time, Pallas kernels for 0%

profile of v12, /device:TPU:0, one launch (start us, length us, event | category | flops | bytes accessed | tf_op | source)
XLA Modules:
  0.0 266.8 jit_solution(18151281490287195631)
XLA Ops:
  7.2 0.0 all-gather.2.cloned.1.call-start
  7.2 0.8 reshape.299
  8.0 0.8 reshape.300
  8.8 0.1 pad_maximum_fusion.1
  8.9 13.9 %all_to_all.68 = bf16[64,8,256]{2,0,1:T(8,128)(2,1)} all-to-all(bf16[64,8,256]{2,0,1:T(8,128)(2,1)S(1)} %bitcast.68), channel_id=1, replica_groups=mesh['uly'=8,'chip'=16,'core'=2] {'uly'}, dimensions={1} | all-to-all | bytes 524288 | tf_op jit(solution)/shard_map/all_to_all | solution.py:135
  22.7 0.0 all-gather.2.cloned.1.call-update
  22.8 1.1 copy_bitcast_fusion
  23.8 0.9 pad_maximum_fusion
  24.7 3.5 %all-to-all-start = ((bf16[64,8,512]{2,0,1:T(8,128)(2,1)}), bf16[64,8,512]{2,0,1:T(8,128)(2,1)S(1)}, u32[]{:S(2)}, u32[]{:S(2)}) async-start(bf16[64,8,512]{2,0,1:T(8,128)(2,1)} %pad_maximum_fusion), calls=%async_computation | async-start | bytes 1048576 | tf_op jit(solution)/shard_map/all_to_all | solution.py:136
  28.2 0.0 reduce-scatter.2.cloned.1.call-start
  28.3 0.8 copy.52
  29.1 0.6 gather_fusion.1
  29.8 0.1 copy.57
  29.9 0.6 gather_fusion
  30.5 0.1 copy.53
  30.6 0.1 and_reduce_fusion
  30.7 0.1 copy.59
  30.7 0.1 copy.55
  30.9 0.1 iota_add_fusion
  30.9 0.1 iota_add_fusion.1
  31.0 0.1 add.251
  31.2 0.1 add.245
  31.4 6.8 %all-to-all-done = bf16[64,8,512]{2,0,1:T(8,128)(2,1)S(1)} async-done(((bf16[64,8,512]{2,0,1:T(8,128)(2,1)}), bf16[64,8,512]{2,0,1:T(8,128)(2,1)S(1)}, u32[]{:S(2)}, u32[]{:S(2)}) %all-to-all-start) | async-done | bytes 524320 | tf_op jit(solution)/shard_map/all_to_all | solution.py:136
  38.2 0.1 collective-permute-start
  38.3 0.5 collective-permute-start.1
  38.8 0.1 select_n.172
  38.9 0.1 select_n.168
  39.0 0.1 concatenate.17.tab_ref
  39.1 0.8 collective-permute-done.pq_ref
  39.9 0.4 collective-permute-done.1.pg_ref
  40.3 53.2 %all-gather.2.cloned.1.call-done.kv_ref = bf16[16384,256]{1,0:T(8,128)(2,1)} async-done(((bf16[512,256]{1,0:T(8,128)(2,1)}), bf16[16384,256]{1,0:T(8,128)(2,1)}) %all-gather.2.cloned.1.call-update) | async-done | bytes 8388624 | tf_op jit(solution)/shard_map/all_gather | solution.py:141
  93.5 45.1 %shard_map.84 = (bf16[512,256]{1,0:T(8,128)(2,1)S(1)}, bf16[512,256]{1,0:T(8,128)(2,1)S(1)}, f32[8192,256]{1,0:T(8,128)}) custom-call(s32[1312]{0:T(1024)S(1)} %concatenate.17.tab_ref, bf16[512,256]{1,0:T(8,128)(2,1)S(1)} %get-tuple-element.17.q_ref, bf16[512,256]{1,0:T(8,128)(2,1)S(1)} %get-tuple-element.16.g_ref, ...), custom_call_target="tpu_custom_call" | custom-call | tf_op jit(solution)/shard_map/pallas_call | solution.py:190
  138.6 0.5 broadcast.619
  139.2 0.8 reduce
  140.0 0.8 reshape.321
  140.7 6.9 %all-to-all-start.2 = ((bf16[8,2,8192]{2,1,0:T(2,128)(2,1)}), bf16[8,2,8192]{2,1,0:T(2,128)(2,1)S(1)}, u32[]{:S(2)}, u32[]{:S(2)}) async-start(bf16[8,2,8192]{2,1,0:T(2,128)(2,1)} %reshape.321), calls=%async_computation.2 | async-start | bytes 524288 | tf_op jit(solution)/shard_map/all_to_all | solution.py:212
  147.6 0.8 reduce.1
  148.4 0.1 reshape.323
  148.5 8.1 %all-to-all-done.2 = bf16[8,2,8192]{2,1,0:T(2,128)(2,1)S(1)} async-done(((bf16[8,2,8192]{2,1,0:T(2,128)(2,1)}), bf16[8,2,8192]{2,1,0:T(2,128)(2,1)S(1)}, u32[]{:S(2)}, u32[]{:S(2)}) %all-to-all-start.2) | async-done | bytes 262176 | tf_op jit(solution)/shard_map/all_to_all | solution.py:212
  156.6 87.6 %all_to_all.69 = bf16[8,2,8192]{2,1,0:T(2,128)(2,1)S(1)} all-to-all(bf16[8,2,8192]{2,1,0:T(2,128)(2,1)S(1)} %reshape.323), channel_id=1, replica_groups=mesh['uly'=8,'chip'=16,'core'=2] {'uly'}, dimensions={0} | all-to-all | bytes 524288 | tf_op jit(solution)/shard_map/all_to_all | solution.py:213
  244.2 3.5 %all-to-all-start.4 = ((f32[8,64,256]{2,1,0:T(8,128)}), f32[8,64,256]{2,1,0:T(8,128)S(1)}, u32[]{:S(2)}, u32[]{:S(2)}) async-start(f32[8,64,256]{2,1,0:T(8,128)} %bitcast.70), calls=%async_computation.5 | async-start | bytes 1048576 | tf_op jit(solution)/shard_map/all_to_all | solution.py:219
  247.7 0.3 reshape.322
  248.0 0.7 copy.75
  248.7 0.3 reshape.324
  249.1 0.7 copy.76
  249.8 8.9 %all-to-all-done.4 = f32[8,64,256]{2,1,0:T(8,128)S(1)} async-done(((f32[8,64,256]{2,1,0:T(8,128)}), f32[8,64,256]{2,1,0:T(8,128)S(1)}, u32[]{:S(2)}, u32[]{:S(2)}) %all-to-all-start.4) | async-done | bytes 524320 | tf_op jit(solution)/shard_map/all_to_all | solution.py:219
  258.7 0.6 copy.83
  259.4 0.6 copy.84
  (18 shorter events, 0.3 us)
Async XLA Ops:
  7.2 86.4 %all-gather.2.cloned.1.call-start = ((), (), s32[]{:S(2)}) async-start(), calls=%async_computation.6 | async-start | bytes 8650752 | tf_op jit(solution)/shard_map/all_gather | solution.py:141
  24.7 13.5 %all-to-all-start = ((bf16[64,8,512]{2,0,1:T(8,128)(2,1)}), bf16[64,8,512]{2,0,1:T(8,128)(2,1)S(1)}, u32[]{:S(2)}, u32[]{:S(2)}) async-start(bf16[64,8,512]{2,0,1:T(8,128)(2,1)} %pad_maximum_fusion), calls=%async_computation | async-start | bytes 1048576 | tf_op jit(solution)/shard_map/all_to_all | solution.py:136
  28.2 216.0 %reduce-scatter.2.cloned.1.call-start = ((), (), s32[]{:S(2)}) async-start(), calls=%async_computation.7 | async-start | bytes 8912896 | tf_op jit(solution)/shard_map/reduce_scatter | solution.py:218
  38.2 1.7 collective-permute-start
  38.3 2.0 collective-permute-start.1
  140.7 15.8 %all-to-all-start.2 = ((bf16[8,2,8192]{2,1,0:T(2,128)(2,1)}), bf16[8,2,8192]{2,1,0:T(2,128)(2,1)S(1)}, u32[]{:S(2)}, u32[]{:S(2)}) async-start(bf16[8,2,8192]{2,1,0:T(2,128)(2,1)} %reshape.321), calls=%async_computation.2 | async-start | bytes 524288 | tf_op jit(solution)/shard_map/all_to_all | solution.py:212
  244.2 14.5 %all-to-all-start.4 = ((f32[8,64,256]{2,1,0:T(8,128)}), f32[8,64,256]{2,1,0:T(8,128)S(1)}, u32[]{:S(2)}, u32[]{:S(2)}) async-start(f32[8,64,256]{2,1,0:T(8,128)} %bitcast.70), calls=%async_computation.5 | async-start | bytes 1048576 | tf_op jit(solution)/shard_map/all_to_all | solution.py:219
Sparse Core Ops, SparseCore 0:
  22.9 70.5 all-gather.1
  138.8 100.5 reduce-scatter.1

commit v13 on v12

--- a/solution.py
+++ b/solution.py
@@ -208,10 +208,11 @@
     )(table, q_rows, g_rows, peer_q, peer_g, keys_all)
     out_items = out_rows.reshape(ulysses_width * segment_length, 1, head_width)
     qgrad_items = qgrad_rows.reshape(ulysses_width * segment_length, 1, head_width)
-    attended_back, qgrad_back = (
-        lax.all_to_all(out_items, "uly", split_axis=0, concat_axis=1, tiled=True),
-        lax.all_to_all(qgrad_items, "uly", split_axis=0, concat_axis=1, tiled=True),
-    )
+    both_back = lax.all_to_all(
+        jnp.concatenate([out_items, qgrad_items], axis=2), "uly", split_axis=0, concat_axis=1, tiled=True
+    )
+    attended_back = both_back[:, :, :head_width]
+    qgrad_back = both_back[:, :, head_width:]
     attended = attended_back.reshape(segment_length, ulysses_width * head_width)
     query_grad = qgrad_back.reshape(segment_length, ulysses_width * head_width)
     chip_part = kv_grad_all.reshape(chip_count, ulysses_width * segment_length, 2 * HEAD_SIZE)

time: 268 us -> 266 us (level)
  blocking collectives: 101 us -> 117 us
  waiting for transfers between devices: 78.3 us -> 69.1 us
  starting transfers between devices: 14.5 us -> 7.65 us
    all_to_all x1, blocking collectives: 87.6 us -> 103 us  [body(): lax.all_to_all(jnp.concatenate([out_items, qgrad_items], axis=2), 'uly',...]
    all_to_all x1 -> x0, waiting for transfers between devices: 8.07 us -> none  [body(): lax.all_to_all(out_items, 'uly', split_axis=0, concat_axis=1, tiled=True)]
    all_to_all x1 -> x0, starting transfers between devices: 6.88 us -> none  [body(): lax.all_to_all(out_items, 'uly', split_axis=0, concat_axis=1, tiled=True)]
  transfers between devices with their start and end apart: 7 -> 6, of which waited for: 6 -> 5; matrix products, arithmetic and copies ran while one was open for 4% -> 4% of each run, Pallas kernels for 0% -> 0%
where the time goes in v13:
time: 266 us; the launch traced here: 265 us
  blocking collectives  117 us (44%)
  waiting for transfers between devices  69.1 us (26%)
  Pallas kernels  45.1 us (17%)
  between operations  14.2 us (5%)
  local copies, waits for them, and re-layouts  9.92 us (4%)
  starting transfers between devices  7.65 us (3%)
    all_to_all x1, blocking collectives, body(): lax.all_to_all(jnp.concatenate([out_items, qgrad_items], axis=2), 'uly',...  103 us
    all_gather x1, waiting for transfers between devices, body(): lax.all_gather(kv_mine[:, 0, :], ('chip', 'core'), axis=0, tiled=True)  53.2 us
    pallas_call x1, Pallas kernels, body(): pl.pallas_call(kernel, out_shape=(jax.ShapeDtypeStruct(q_rows.shape, jnp....  45.1 us
    all_to_all x1, blocking collectives, body(): lax.all_to_all(kv_slots, 'uly', split_axis=1, concat_axis=0, tiled=True)  13.9 us
    all_to_all x1, waiting for transfers between devices, body(): lax.all_to_all(owned.reshape(ulysses_width, segment_length, 2 * HEAD_SIZE...  7.83 us
    all_to_all x1, waiting for transfers between devices, body(): lax.all_to_all(jnp.concatenate([query_slots, grad_slots], axis=2), 'uly',...  6.82 us
  transfers between devices with their start and end apart: 6, of which 5 were waited for; matrix products, arithmetic and copies ran while one was open for 4% of the time, Pallas kernels for 0%

profile of v13, /device:TPU:0, one launch (start us, length us, event | category | flops | bytes accessed | tf_op | source)
XLA Modules:
  0.0 265.0 jit_solution(12523769127430430164)
XLA Ops:
  7.2 0.0 all-gather.2.cloned.1.call-start
  7.2 0.8 reshape.297
  8.0 0.8 reshape.298
  8.8 0.1 pad_maximum_fusion.2
  8.9 13.9 %all_to_all.56 = bf16[64,8,256]{2,0,1:T(8,128)(2,1)} all-to-all(bf16[64,8,256]{2,0,1:T(8,128)(2,1)S(1)} %bitcast.60), channel_id=1, replica_groups=mesh['uly'=8,'chip'=16,'core'=2] {'uly'}, dimensions={1} | all-to-all | bytes 524288 | tf_op jit(solution)/shard_map/all_to_all | solution.py:135
  22.7 0.0 all-gather.2.cloned.1.call-update
  22.8 1.1 copy_bitcast_fusion
  23.8 0.9 pad_maximum_fusion
  24.7 3.5 %all-to-all-start = ((bf16[64,8,512]{2,0,1:T(8,128)(2,1)}), bf16[64,8,512]{2,0,1:T(8,128)(2,1)S(1)}, u32[]{:S(2)}, u32[]{:S(2)}) async-start(bf16[64,8,512]{2,0,1:T(8,128)(2,1)} %pad_maximum_fusion), calls=%async_computation | async-start | bytes 1048576 | tf_op jit(solution)/shard_map/all_to_all | solution.py:136
  28.2 0.0 reduce-scatter.2.cloned.1.call-start
  28.3 0.8 copy.49
  29.1 0.6 gather_fusion.1
  29.8 0.1 copy.54
  29.9 0.6 gather_fusion
  30.5 0.1 copy.50
  30.6 0.1 and_reduce_fusion
  30.7 0.1 copy.56
  30.7 0.1 copy.52
  30.9 0.1 iota_add_fusion
  30.9 0.1 iota_add_fusion.1
  31.0 0.1 add.251
  31.2 0.1 add.245
  31.4 6.8 %all-to-all-done = bf16[64,8,512]{2,0,1:T(8,128)(2,1)S(1)} async-done(((bf16[64,8,512]{2,0,1:T(8,128)(2,1)}), bf16[64,8,512]{2,0,1:T(8,128)(2,1)S(1)}, u32[]{:S(2)}, u32[]{:S(2)}) %all-to-all-start) | async-done | bytes 524320 | tf_op jit(solution)/shard_map/all_to_all | solution.py:136
  38.2 0.1 collective-permute-start
  38.3 0.5 collective-permute-start.1
  38.8 0.1 select_n.172
  38.9 0.1 select_n.168
  39.0 0.1 concatenate.20.tab_ref
  39.1 0.8 collective-permute-done.pq_ref
  39.9 0.4 collective-permute-done.1.pg_ref
  40.3 53.2 %all-gather.2.cloned.1.call-done.kv_ref = bf16[16384,256]{1,0:T(8,128)(2,1)} async-done(((bf16[512,256]{1,0:T(8,128)(2,1)}), bf16[16384,256]{1,0:T(8,128)(2,1)}) %all-gather.2.cloned.1.call-update) | async-done | bytes 8388624 | tf_op jit(solution)/shard_map/all_gather | solution.py:141
  93.5 45.1 %shard_map.84 = (bf16[512,256]{1,0:T(8,128)(2,1)S(1)}, bf16[512,256]{1,0:T(8,128)(2,1)S(1)}, f32[8192,256]{1,0:T(8,128)}) custom-call(s32[1312]{0:T(1024)S(1)} %concatenate.20.tab_ref, bf16[512,256]{1,0:T(8,128)(2,1)S(1)} %get-tuple-element.19.q_ref, bf16[512,256]{1,0:T(8,128)(2,1)S(1)} %get-tuple-element.18.g_ref, ...), custom_call_target="tpu_custom_call" | custom-call | tf_op jit(solution)/shard_map/pallas_call | solution.py:190
  138.6 0.0 reduce-scatter.2.cloned.1.call-update
  138.7 0.5 broadcast.619
  139.2 1.0 reduce
  140.2 0.4 reshape.319
  140.6 102.7 %all_to_all.57 = bf16[8,2,16384]{2,1,0:T(2,128)(2,1)S(1)} all-to-all(bf16[8,2,16384]{2,1,0:T(2,128)(2,1)S(1)} %reshape.319), channel_id=1, replica_groups=mesh['uly'=8,'chip'=16,'core'=2] {'uly'}, dimensions={0} | all-to-all | bytes 1048576 | tf_op jit(solution)/shard_map/all_to_all | solution.py:211
  243.3 0.0 reduce-scatter.2.cloned.1.call-done
  243.3 3.5 %all-to-all-start.3 = ((f32[8,64,256]{2,1,0:T(8,128)}), f32[8,64,256]{2,1,0:T(8,128)S(1)}, u32[]{:S(2)}, u32[]{:S(2)}) async-start(f32[8,64,256]{2,1,0:T(8,128)} %bitcast.62), calls=%async_computation.4 | async-start | bytes 1048576 | tf_op jit(solution)/shard_map/all_to_all | solution.py:220
  246.8 0.5 reshape.320
  247.4 0.1 copy.65
  247.5 0.1 slice_bitcast_fusion
  247.6 0.7 copy.68
  248.3 0.7 copy.69
  249.0 7.8 %all-to-all-done.3 = f32[8,64,256]{2,1,0:T(8,128)S(1)} async-done(((f32[8,64,256]{2,1,0:T(8,128)}), f32[8,64,256]{2,1,0:T(8,128)S(1)}, u32[]{:S(2)}, u32[]{:S(2)}) %all-to-all-start.3) | async-done | bytes 524320 | tf_op jit(solution)/shard_map/all_to_all | solution.py:220
  256.9 0.6 copy.76
  257.5 0.6 copy.77
  (15 shorter events, 0.3 us)
Async XLA Ops:
  7.2 86.4 %all-gather.2.cloned.1.call-start = ((), (), s32[]{:S(2)}) async-start(), calls=%async_computation.5 | async-start | bytes 8650752 | tf_op jit(solution)/shard_map/all_gather | solution.py:141
  24.7 13.5 %all-to-all-start = ((bf16[64,8,512]{2,0,1:T(8,128)(2,1)}), bf16[64,8,512]{2,0,1:T(8,128)(2,1)S(1)}, u32[]{:S(2)}, u32[]{:S(2)}) async-start(bf16[64,8,512]{2,0,1:T(8,128)(2,1)} %pad_maximum_fusion), calls=%async_computation | async-start | bytes 1048576 | tf_op jit(solution)/shard_map/all_to_all | solution.py:136
  28.2 215.1 %reduce-scatter.2.cloned.1.call-start = ((), (), s32[]{:S(2)}) async-start(), calls=%async_computation.6 | async-start | bytes 8912896 | tf_op jit(solution)/shard_map/reduce_scatter | solution.py:219
  38.2 1.7 collective-permute-start
  38.3 2.0 collective-permute-start.1
  243.3 13.5 %all-to-all-start.3 = ((f32[8,64,256]{2,1,0:T(8,128)}), f32[8,64,256]{2,1,0:T(8,128)S(1)}, u32[]{:S(2)}, u32[]{:S(2)}) async-start(f32[8,64,256]{2,1,0:T(8,128)} %bitcast.62), calls=%async_computation.4 | async-start | bytes 1048576 | tf_op jit(solution)/shard_map/all_to_all | solution.py:220
Sparse Core Ops, SparseCore 0:
  22.9 70.5 all-gather.1
  138.8 100.5 reduce-scatter.1
